TPU v7x, 512 devices: a whole 4x8x8 slice. The times are simulated.
512 devices in a mesh: depth: 32 (over y, x), lat: 16 (over z, core).
Axes of the slice: x: 4, y: 8, z: 8, core: 2. Of those that a mesh axis runs over, the one named last changes fastest.
Arguments:
- thermal_state: float32 [1024, 8, 2048], P('depth', None, 'lat'), may hold values from -5 to 5
- sideways_face_flux_factor: float32 [1024, 8, 2048], P('depth', None, 'lat'), may hold values from 1 to 10
- downward_face_flux_factor: float32 [1024, 8, 2048], P('depth', None, 'lat'), may hold values from 1 to 10
Outputs:
- final_temperature: float32 [1024, 8, 2048], P('depth', None, 'lat')
All inputs are finite; a program needn't handle non-finite values.
Results may differ from a plain program's by a relative error of at most 0.0013.
Values sent between devices are 32-bit elements; how exact they have to be, the bound alone decides.
No kernel may reach another device: no remote copies, remote signals or barrier semaphores. Data moves between devices by JAX's collectives and lax.ppermute only.
A program may use at most 64 MiB of HBM per device.

v0:
```python
import jax
import jax.numpy as jnp
from jax import lax
from jax.sharding import PartitionSpec as P

sideways_coupling_quotient = 20.0
ratio_z = 2000.0


def extended(x, sides, width):
    for axis, dim in sides:
        count, length = (lax.axis_size(axis), x.shape[dim])
        up = [(i, (i + 1) % count) for i in range(count - 1)]
        down = [(j, i) for i, j in up]
        last = lax.slice_in_dim(x, length - width, length, axis=dim)
        first = lax.slice_in_dim(x, 0, width, axis=dim)
        before = lax.ppermute(last, axis, up)
        after = lax.ppermute(first, axis, down)
        x = jnp.concatenate([before, x, after], axis=dim)
    return x


def from_behind(x, axis, by):
    count = lax.axis_size(axis)
    pairs = [(i, i + by) for i in range(count) if 0 <= i + by < count]
    return lax.ppermute(x, axis, pairs)


def take_rows(values, start, stop, axis_index):
    return lax.slice_in_dim(values, start, stop, axis=axis_index)


def moved(values, stride, axis_index, filler, forward):
    count = values.shape[axis_index]
    pad_shape = list(values.shape)
    pad_shape[axis_index] = stride
    padding = jnp.full(pad_shape, filler, values.dtype)
    if forward:
        return jnp.concatenate(
            [take_rows(values, stride, count, axis_index), padding], axis=axis_index
        )
    return jnp.concatenate(
        [padding, take_rows(values, 0, count - stride, axis_index)], axis=axis_index
    )


def level_update(lower_band, diagonal, upper_band, rights, below, above):
    alpha_term = -lower_band / below[1]
    gamma_term = -upper_band / above[1]
    new_diagonal = diagonal + alpha_term * below[2] + gamma_term * above[0]
    new_rights = tuple(
        (
            column + alpha_term * low_col + gamma_term * high_col
            for column, low_col, high_col in zip(rights, below[3], above[3])
        )
    )
    return (alpha_term * below[0], new_diagonal, gamma_term * above[2], new_rights)


def cyclic(lower_band, diagonal, upper_band, rights, axis_index):
    count = lower_band.shape[axis_index]
    stride = 1
    while stride < count:
        below = (
            moved(lower_band, stride, axis_index, 0.0, False),
            moved(diagonal, stride, axis_index, 1.0, False),
            moved(upper_band, stride, axis_index, 0.0, False),
            tuple((moved(column, stride, axis_index, 0.0, False) for column in rights)),
        )
        above = (
            moved(lower_band, stride, axis_index, 0.0, True),
            moved(diagonal, stride, axis_index, 1.0, True),
            moved(upper_band, stride, axis_index, 0.0, True),
            tuple((moved(column, stride, axis_index, 0.0, True) for column in rights)),
        )
        lower_band, diagonal, upper_band, rights = level_update(
            lower_band, diagonal, upper_band, rights, below, above
        )
        stride = stride * 2
    return tuple((column / diagonal for column in rights))


def partition_solve(lower_band, upper_inner, rights, axis_index, fetch_next, reduced, fetch_prev):
    count = lower_band.shape[axis_index]
    inner_lower = take_rows(lower_band, 0, count - 1, axis_index)
    diagonal = 1.0 - inner_lower - upper_inner
    positions = lax.broadcasted_iota(jnp.int32, inner_lower.shape, axis_index)
    first_lower = take_rows(inner_lower, 0, 1, axis_index)
    last_upper = take_rows(upper_inner, count - 2, count - 1, axis_index)
    solve_lower = jnp.where(positions == 0, 0.0, inner_lower)
    solve_upper = jnp.where(positions == count - 2, 0.0, upper_inner)
    from_prev = jnp.where(positions == 0, -first_lower, 0.0)
    from_next = jnp.where(positions == count - 2, -last_upper, 0.0)
    inner_rights = take_rows(rights, 0, count - 1, axis_index)
    local_part, prev_part, next_part = cyclic(
        solve_lower, diagonal, solve_upper, (inner_rights, from_prev, from_next), axis_index
    )
    heads = (
        take_rows(local_part, 0, 1, axis_index),
        take_rows(prev_part, 0, 1, axis_index),
        take_rows(next_part, 0, 1, axis_index),
    )
    head_local, head_prev, head_next, last_coupling = fetch_next(heads)
    tail_local = take_rows(local_part, count - 2, count - 1, axis_index)
    tail_prev = take_rows(prev_part, count - 2, count - 1, axis_index)
    tail_next = take_rows(next_part, count - 2, count - 1, axis_index)
    lower_last = take_rows(lower_band, count - 1, count, axis_index)
    right_last = take_rows(rights, count - 1, count, axis_index)
    coeff_lower = lower_last * tail_prev
    coeff_diag = (
        1.0 - lower_last - last_coupling + lower_last * tail_next + last_coupling * head_prev
    )
    coeff_upper = last_coupling * head_next
    coeff_right = right_last - lower_last * tail_local - last_coupling * head_local
    interface_value = reduced(coeff_lower, coeff_diag, coeff_upper, coeff_right)
    previous = fetch_prev(interface_value)
    inner_values = local_part + prev_part * previous + next_part * interface_value
    return jnp.concatenate([inner_values, interface_value], axis=axis_index)


def on_device(thermal_state, sideways_face_flux_factor, downward_face_flux_factor):
    sideways_node_count = thermal_state.shape[2]
    grouped_sweep_rows = jnp.stack([thermal_state, sideways_face_flux_factor])
    padded = extended(grouped_sweep_rows, (("lat", 3),), 1)
    initial_operand_swapped = padded[0, :, :, :sideways_node_count]
    source_vector_swapped = padded[0, :, :, 2:]
    source_vector_downward = padded[1, :, :, 2:]
    known_operator_term = thermal_state + sideways_coupling_quotient * (
        source_vector_downward * (source_vector_swapped - thermal_state)
        - sideways_face_flux_factor * (thermal_state - initial_operand_swapped)
    )

    def depth_next(heads):
        arrived = from_behind(
            (heads[0], heads[1], heads[2], downward_face_flux_factor[0:1]), "depth", -1
        )
        return (arrived[0], arrived[1], arrived[2], -ratio_z * arrived[3])

    def depth_reduced(coeff_lower, coeff_diag, coeff_upper, coeff_right):
        gathered = (
            lax.all_gather(coeff_lower, "depth", axis=0, tiled=True),
            lax.all_gather(coeff_diag, "depth", axis=0, tiled=True),
            lax.all_gather(coeff_upper, "depth", axis=0, tiled=True),
            lax.all_gather(coeff_right, "depth", axis=0, tiled=True),
        )
        solved = cyclic(gathered[0], gathered[1], gathered[2], (gathered[3],), 0)[0]
        return lax.dynamic_slice_in_dim(solved, lax.axis_index("depth"), 1, 0)

    def depth_prev(interface_value):
        return from_behind(interface_value, "depth", 1)

    half_step = partition_solve(
        -ratio_z * downward_face_flux_factor,
        -ratio_z * downward_face_flux_factor[1:],
        known_operator_term,
        0,
        depth_next,
        depth_reduced,
        depth_prev,
    )
    reflected = 2.0 * half_step - known_operator_term
    lines = lax.all_to_all(reflected, "lat", split_axis=0, concat_axis=2, tiled=True)
    conduct_lines = lax.all_to_all(
        sideways_face_flux_factor, "lat", split_axis=0, concat_axis=2, tiled=True
    )
    lower_band = -sideways_coupling_quotient * conduct_lines
    upper_band = -sideways_coupling_quotient * jnp.concatenate(
        [conduct_lines[:, :, 1:], jnp.zeros_like(conduct_lines[:, :, :1])], axis=2
    )
    diagonal = 1.0 - lower_band - upper_band
    solve_lower = jnp.concatenate(
        [jnp.zeros_like(lower_band[:, :, :1]), lower_band[:, :, 1:]], axis=2
    )
    solved = cyclic(solve_lower, diagonal, upper_band, (lines,), 2)[0]
    return lax.all_to_all(solved, "lat", split_axis=2, concat_axis=0, tiled=True)


def solution(mesh):
    in_specs = (P("depth", None, "lat"), P("depth", None, "lat"), P("depth", None, "lat"))
    out_specs = P("depth", None, "lat")
    return jax.shard_map(
        on_device, mesh=mesh, in_specs=in_specs, out_specs=out_specs, check_vma=False
    )
```

profile of v0, /device:TPU:1, one launch (start us, length us, event | category | flops | bytes accessed | tf_op | source)
XLA Modules:
  0.0 245.1 jit_solution(14447107847641421287)
XLA Ops:
  0.0 1.3 slice_maximum_fusion
  1.3 8.8 %collective-permute-start = (f32[2,32,8,1]{3,2,1,0:T(8,128)S(1)}, f32[2,32,8,1]{3,2,1,0:T(8,128)S(1)}, u32[]{:S(2)}, u32[]{:S(2)}) collective-permute-start(f32[2,32,8,1]{3,2,1,0:T(8,128)S(1)} %get-tuple-element.67), channel_id=1, source_target_pairs={{1,0},{2,1},{3,2},{4,3},{5,4},{6,5},{7,6},{8,7},{9,8},{10,9},{11,1... | collective-permute-start | bytes 6152 | tf_op jit(solution)/shard_map/ppermute | solution.py:18
  10.1 1.9 collective-permute-start.1
  12.0 0.7 slice.672
  12.7 1.3 collective-permute-start.2
  14.0 0.9 broadcast_multiply_fusion.1
  14.9 0.9 slice_multiply_fusion
  15.9 1.2 fusion.5
  18.8 1.3 collective-permute-start.3
  20.3 1.3 collective-permute-start.4
  21.6 2.2 collective-permute-done.3
  23.8 2.1 collective-permute-done.4
  25.9 1.3 collective-permute-start.5
  27.2 34.0 %all_gather.13 = f32[32,8,128]{2,1,0:T(8,128)S(1)} all-gather(f32[1,8,128]{2,1,0:T(8,128)S(1)} %get-tuple-element.205), channel_id=1, replica_groups=mesh['depth'=32,'lat'=16] {'depth'}, dimensions={0}, use_global_device_ids=true | all-gather | bytes 135168 | tf_op jit(solution)/shard_map/all_gather | solution.py:141
  61.2 28.5 %all_gather.14 = f32[32,8,128]{2,1,0:T(8,128)S(1)} all-gather(f32[1,8,128]{2,1,0:T(8,128)S(1)} %get-tuple-element.84), channel_id=1, replica_groups=mesh['depth'=32,'lat'=16] {'depth'}, dimensions={0}, use_global_device_ids=true | all-gather | bytes 135168 | tf_op jit(solution)/shard_map/all_gather | solution.py:142
  89.7 28.7 %all_gather.12 = f32[32,8,128]{2,1,0:T(8,128)S(1)} all-gather(f32[1,8,128]{2,1,0:T(8,128)S(1)} %get-tuple-element.85), channel_id=1, replica_groups=mesh['depth'=32,'lat'=16] {'depth'}, dimensions={0}, use_global_device_ids=true | all-gather | bytes 135168 | tf_op jit(solution)/shard_map/all_gather | solution.py:144
  118.4 29.4 %all_gather.15 = f32[32,8,128]{2,1,0:T(8,128)S(1)} all-gather(f32[1,8,128]{2,1,0:T(8,128)S(1)} %multiply_multiply_fusion), channel_id=1, replica_groups=mesh['depth'=32,'lat'=16] {'depth'}, dimensions={0}, use_global_device_ids=true | all-gather | bytes 135168 | tf_op jit(solution)/shard_map/all_gather | solution.py:143
  148.9 1.7 collective-permute-start.6
  150.6 44.6 %all-to-all-start.1 = ((f32[32,8,128]{2,1,0:T(8,128)}), f32[32,8,128]{2,1,0:T(8,128)S(1)}, u32[]{:S(2)}, u32[]{:S(2)}) async-start(f32[32,8,128]{2,1,0:T(8,128)} %param.4), calls=%async_computation.1 | async-start | bytes 262144 | tf_op jit(solution)/shard_map/all_to_all | solution.py:163
  195.3 0.7 fusion.9
  195.9 8.5 %all-to-all-done.1 = f32[32,8,128]{2,1,0:T(8,128)S(1)} async-done(((f32[32,8,128]{2,1,0:T(8,128)}), f32[32,8,128]{2,1,0:T(8,128)S(1)}, u32[]{:S(2)}, u32[]{:S(2)}) %all-to-all-start.1) | async-done | bytes 131104 | tf_op jit(solution)/shard_map/all_to_all | solution.py:163
  204.4 3.6 %all-to-all-start = ((f32[32,8,128]{2,1,0:T(8,128)}), f32[32,8,128]{2,1,0:T(8,128)S(1)}, u32[]{:S(2)}, u32[]{:S(2)}) async-start(f32[32,8,128]{2,1,0:T(8,128)} %fusion.9), calls=%async_computation | async-start | bytes 262144 | tf_op jit(solution)/shard_map/all_to_all | solution.py:162
  208.6 7.8 %all-to-all-done = f32[32,8,128]{2,1,0:T(8,128)S(1)} async-done(((f32[32,8,128]{2,1,0:T(8,128)}), f32[32,8,128]{2,1,0:T(8,128)S(1)}, u32[]{:S(2)}, u32[]{:S(2)}) %all-to-all-start) | async-done | bytes 131104 | tf_op jit(solution)/shard_map/all_to_all | solution.py:162
  217.0 0.2 multiply_add_fusion.17
  217.8 0.2 multiply_add_fusion.15
  222.4 1.0 copy.11
  223.4 3.3 %reshape = f32[16,1,2048]{2,1,0:T(1,128)S(1)} reshape(f32[2048,2,8]{2,1,0:T(2,128)S(1)} %bitcast.51) | data formatting | bytes 262144
  226.8 11.8 %all_to_all.54 = f32[16,1,2048]{2,1,0:T(1,128)S(1)} all-to-all(f32[16,1,2048]{2,1,0:T(1,128)S(1)} %reshape), channel_id=1, replica_groups=mesh['depth'=32,'lat'=16] {'lat'}, dimensions={0} | all-to-all | bytes 262144 | tf_op jit(solution)/shard_map/all_to_all | solution.py:175
  238.6 0.5 broadcast.435
  239.1 0.9 reduce
  240.1 3.2 %reshape.1 = f32[2048,2,8]{2,1,0:T(2,128)S(1)} reshape(f32[16,2048]{1,0:T(8,128)S(1)} %reduce) | data formatting | bytes 262144
  243.2 1.9 copy.15
  (152 shorter events, 8.2 us)
Async XLA Ops:
  0.0 15.9 %copy-start = (f32[32,8,128]{2,1,0:T(8,128)S(1)}, f32[32,8,128]{2,1,0:T(8,128)}, u32[]{:S(2)}) copy-start(f32[32,8,128]{2,1,0:T(8,128)} %param.3) | copy-start | bytes 393220
  0.0 17.2 %copy-start.1 = (f32[32,8,128]{2,1,0:T(8,128)S(1)}, f32[32,8,128]{2,1,0:T(8,128)}, u32[]{:S(2)}) copy-start(f32[32,8,128]{2,1,0:T(8,128)} %param.5) | copy-start | bytes 393220
  1.3 14.6 %collective-permute-start = (f32[2,32,8,1]{3,2,1,0:T(8,128)S(1)}, f32[2,32,8,1]{3,2,1,0:T(8,128)S(1)}, u32[]{:S(2)}, u32[]{:S(2)}) collective-permute-start(f32[2,32,8,1]{3,2,1,0:T(8,128)S(1)} %get-tuple-element.67), channel_id=1, source_target_pairs={{1,0},{2,1},{3,2},{4,3},{5,4},{6,5},{7,6},{8,7},{9,8},{10,9},{11,1... | collective-permute-start | bytes 6152 | tf_op jit(solution)/shard_map/ppermute | solution.py:18
  10.1 5.8 %collective-permute-start.1 = (f32[2,32,8,1]{3,2,1,0:T(8,128)S(1)}, f32[2,32,8,1]{3,2,1,0:T(8,128)S(1)}, u32[]{:S(2)}, u32[]{:S(2)}) collective-permute-start(f32[2,32,8,1]{3,2,1,0:T(8,128)S(1)} %get-tuple-element.68), channel_id=1, source_target_pairs={{0,1},{1,2},{2,3},{3,4},{4,5},{5,6},{6,7},{7,8},{8,9},{9,10},{10,1... | collective-permute-start | bytes 6152 | tf_op jit(solution)/shard_map/ppermute | solution.py:17
  12.7 8.9 %collective-permute-start.2 = (f32[1,8,128]{2,1,0:T(8,128)S(1)}, f32[1,8,128]{2,1,0:T(8,128)S(1)}, u32[]{:S(2)}, u32[]{:S(2)}) collective-permute-start(f32[1,8,128]{2,1,0:T(8,128)S(1)} %slice.672), channel_id=1, source_target_pairs={{16,0},{32,16},{48,32},{64,48},{80,64},{96,80},{112,96},{128,112},... | collective-permute-start | bytes 12296 | tf_op jit(solution)/shard_map/ppermute | solution.py:26
  18.8 5.0 %collective-permute-start.3 = (f32[1,8,128]{2,1,0:T(8,128)S(1)}, f32[1,8,128]{2,1,0:T(8,128)S(1)}, u32[]{:S(2)}, u32[]{:S(2)}) collective-permute-start(f32[1,8,128]{2,1,0:T(8,128)S(1)} %slice.870), channel_id=1, source_target_pairs={{16,0},{32,16},{48,32},{64,48},{80,64},{96,80},{112,96},{128,112},... | collective-permute-start | bytes 12296 | tf_op jit(solution)/shard_map/ppermute | solution.py:26
  20.3 5.6 %collective-permute-start.4 = (f32[1,8,128]{2,1,0:T(8,128)S(1)}, f32[1,8,128]{2,1,0:T(8,128)S(1)}, u32[]{:S(2)}, u32[]{:S(2)}) collective-permute-start(f32[1,8,128]{2,1,0:T(8,128)S(1)} %slice.884), channel_id=1, source_target_pairs={{16,0},{32,16},{48,32},{64,48},{80,64},{96,80},{112,96},{128,112},... | collective-permute-start | bytes 12296 | tf_op jit(solution)/shard_map/ppermute | solution.py:26
  25.9 92.6 %collective-permute-start.5 = (f32[1,8,128]{2,1,0:T(8,128)S(1)}, f32[1,8,128]{2,1,0:T(8,128)S(1)}, u32[]{:S(2)}, u32[]{:S(2)}) collective-permute-start(f32[1,8,128]{2,1,0:T(8,128)S(1)} %get-tuple-element.212), channel_id=1, source_target_pairs={{16,0},{32,16},{48,32},{64,48},{80,64},{96,80},{112,96},{128,112},... | collective-permute-start | bytes 12296 | tf_op jit(solution)/shard_map/ppermute | solution.py:26
  148.9 46.3 %collective-permute-start.6 = (f32[1,8,128]{2,1,0:T(8,128)S(1)}, f32[1,8,128]{2,1,0:T(8,128)S(1)}, u32[]{:S(2)}, u32[]{:S(2)}) collective-permute-start(f32[1,8,128]{2,1,0:T(8,128)S(1)} %fusion.18), channel_id=1, source_target_pairs={{0,16},{16,32},{32,48},{48,64},{64,80},{80,96},{96,112},{112,128},... | collective-permute-start | bytes 12296 | tf_op jit(solution)/shard_map/ppermute | solution.py:26
  150.6 53.8 %all-to-all-start.1 = ((f32[32,8,128]{2,1,0:T(8,128)}), f32[32,8,128]{2,1,0:T(8,128)S(1)}, u32[]{:S(2)}, u32[]{:S(2)}) async-start(f32[32,8,128]{2,1,0:T(8,128)} %param.4), calls=%async_computation.1 | async-start | bytes 262144 | tf_op jit(solution)/shard_map/all_to_all | solution.py:163
  204.4 12.0 %all-to-all-start = ((f32[32,8,128]{2,1,0:T(8,128)}), f32[32,8,128]{2,1,0:T(8,128)S(1)}, u32[]{:S(2)}, u32[]{:S(2)}) async-start(f32[32,8,128]{2,1,0:T(8,128)} %fusion.9), calls=%async_computation | async-start | bytes 262144 | tf_op jit(solution)/shard_map/all_to_all | solution.py:162
where the time goes:
time: 246 us; the launch traced here: 245 us
  blocking collectives  132 us (54%)
  starting transfers between devices  65.8 us (27%)
  waiting for transfers between devices  20.6 us (8%)
  local copies, waits for them, and re-layouts  14.5 us (6%)
  other arithmetic  10.7 us (4%)
    all_to_all x1, starting transfers between devices, on_device(): lax.all_to_all(sideways_face_flux_factor, 'lat', split_axis=0, concat_axi...  44.6 us
    all_gather x1, blocking collectives, depth_reduced(): lax.all_gather(coeff_lower, 'depth', axis=0, tiled=True)  34 us
    all_gather x1, blocking collectives, depth_reduced(): lax.all_gather(coeff_upper, 'depth', axis=0, tiled=True)  29.4 us
    all_gather x1, blocking collectives, depth_reduced(): lax.all_gather(coeff_right, 'depth', axis=0, tiled=True)  28.7 us
    all_gather x1, blocking collectives, depth_reduced(): lax.all_gather(coeff_diag, 'depth', axis=0, tiled=True)  28.5 us
    all_to_all x1, blocking collectives, on_device(): lax.all_to_all(solved, 'lat', split_axis=2, concat_axis=0, tiled=True)  11.8 us
    ppermute x1, starting transfers between devices, extended(): after = lax.ppermute(first, axis, down)  8.79 us
    all_to_all x1, waiting for transfers between devices, on_device(): lax.all_to_all(sideways_face_flux_factor, 'lat', split_axis=0, concat_axi...  8.46 us
  transfers between devices with their start and end apart: 9, of which 4 were waited for; matrix products, arithmetic and copies ran while one was open for 3% of the time, Pallas kernels for 0%

commit v1 on v0

v1 whole, which is shorter than its diff:
```python
import jax
import jax.numpy as jnp
from jax import lax
from jax.sharding import PartitionSpec as P

sideways_coupling_quotient = 20.0
ratio_z = 2000.0


def take_rows(values, start, stop, axis_index):
    return lax.slice_in_dim(values, start, stop, axis=axis_index)


def moved(values, stride, axis_index, filler, forward):
    count = values.shape[axis_index]
    pad_shape = list(values.shape)
    pad_shape[axis_index] = stride
    padding = jnp.full(pad_shape, filler, values.dtype)
    if forward:
        return jnp.concatenate(
            [take_rows(values, stride, count, axis_index), padding], axis=axis_index
        )
    return jnp.concatenate(
        [padding, take_rows(values, 0, count - stride, axis_index)], axis=axis_index
    )


def level_update(lower_band, diagonal, upper_band, rights, below, above):
    alpha_term = -lower_band / below[1]
    gamma_term = -upper_band / above[1]
    new_diagonal = diagonal + alpha_term * below[2] + gamma_term * above[0]
    new_rights = tuple(
        (
            column + alpha_term * low_col + gamma_term * high_col
            for column, low_col, high_col in zip(rights, below[3], above[3])
        )
    )
    return (alpha_term * below[0], new_diagonal, gamma_term * above[2], new_rights)


def cyclic(lower_band, diagonal, upper_band, rights, axis_index):
    count = lower_band.shape[axis_index]
    stride = 1
    while stride < count:
        below = (
            moved(lower_band, stride, axis_index, 0.0, False),
            moved(diagonal, stride, axis_index, 1.0, False),
            moved(upper_band, stride, axis_index, 0.0, False),
            tuple((moved(column, stride, axis_index, 0.0, False) for column in rights)),
        )
        above = (
            moved(lower_band, stride, axis_index, 0.0, True),
            moved(diagonal, stride, axis_index, 1.0, True),
            moved(upper_band, stride, axis_index, 0.0, True),
            tuple((moved(column, stride, axis_index, 0.0, True) for column in rights)),
        )
        lower_band, diagonal, upper_band, rights = level_update(
            lower_band, diagonal, upper_band, rights, below, above
        )
        stride = stride * 2
    return tuple((column / diagonal for column in rights))


def gathered(values, axis):
    count = lax.axis_size(axis)
    copies = jnp.broadcast_to(values[None], (count,) + values.shape)
    return lax.all_to_all(copies, axis, 0, 0, tiled=False)


def partition_solve(conduct, first_next, rights, ratio, axis_index, axis):
    count = conduct.shape[axis_index]
    lower_band = -ratio * conduct
    inner_lower = take_rows(lower_band, 0, count - 1, axis_index)
    upper_inner = -ratio * take_rows(conduct, 1, count, axis_index)
    diagonal = 1.0 - inner_lower - upper_inner
    positions = lax.broadcasted_iota(jnp.int32, inner_lower.shape, axis_index)
    first_lower = take_rows(inner_lower, 0, 1, axis_index)
    last_upper = take_rows(upper_inner, count - 2, count - 1, axis_index)
    solve_lower = jnp.where(positions == 0, 0.0, inner_lower)
    solve_upper = jnp.where(positions == count - 2, 0.0, upper_inner)
    from_prev = jnp.where(positions == 0, -first_lower, 0.0)
    from_next = jnp.where(positions == count - 2, -last_upper, 0.0)
    inner_rights = take_rows(rights, 0, count - 1, axis_index)
    local_part, prev_part, next_part = cyclic(
        solve_lower, diagonal, solve_upper, (inner_rights, from_prev, from_next), axis_index
    )
    tail_local = take_rows(local_part, count - 2, count - 1, axis_index)
    tail_prev = take_rows(prev_part, count - 2, count - 1, axis_index)
    tail_next = take_rows(next_part, count - 2, count - 1, axis_index)
    lower_last = take_rows(lower_band, count - 1, count, axis_index)
    right_last = take_rows(rights, count - 1, count, axis_index)
    pieces = jnp.stack(
        [
            lower_last * tail_prev,
            1.0 - lower_last + lower_last * tail_next,
            right_last - lower_last * tail_local,
            take_rows(local_part, 0, 1, axis_index),
            take_rows(prev_part, 0, 1, axis_index),
            take_rows(next_part, 0, 1, axis_index),
            take_rows(conduct, 0, 1, axis_index),
        ]
    )
    line_shape = pieces.shape[1:]
    flat = pieces.reshape(7, -1)
    every = gathered(flat, axis)
    blocks = every.shape[0]
    own_lower, own_diag, own_right = every[:, 0], every[:, 1], every[:, 2]
    zero_row = jnp.zeros_like(every[:1, 0])
    next_heads = [
        jnp.concatenate([every[1:, i], zero_row], axis=0) for i in (3, 4, 5, 6)
    ]
    head_local, head_prev, head_next, next_conduct = next_heads
    coupling = -ratio * next_conduct
    red_diag = own_diag - coupling + coupling * head_prev
    red_upper = coupling * head_next
    red_right = own_right - coupling * head_local
    solved = cyclic(own_lower, red_diag, red_upper, (red_right,), 0)[0]
    padded = jnp.concatenate([zero_row, solved], axis=0)
    index = lax.axis_index(axis)
    previous = lax.dynamic_slice_in_dim(padded, index, 1, 0).reshape(line_shape)
    interface_value = lax.dynamic_slice_in_dim(padded, index + 1, 1, 0).reshape(line_shape)
    inner_values = local_part + prev_part * previous + next_part * interface_value
    del blocks, first_next
    return jnp.concatenate([inner_values, interface_value], axis=axis_index)


def on_device(thermal_state, sideways_face_flux_factor, downward_face_flux_factor):
    width = thermal_state.shape[2]
    count = lax.axis_size("lat")
    right_pairs = [(i, i + 1) for i in range(count - 1)]
    left_pairs = [(i + 1, i) for i in range(count - 1)]
    first_cols = jnp.stack(
        [thermal_state[:, :, :1], sideways_face_flux_factor[:, :, :1]]
    )
    from_right = lax.ppermute(first_cols, "lat", left_pairs)
    from_left = lax.ppermute(thermal_state[:, :, width - 1 :], "lat", right_pairs)
    temp_right = jnp.concatenate([thermal_state[:, :, 1:], from_right[0]], axis=2)
    conduct_right = jnp.concatenate(
        [sideways_face_flux_factor[:, :, 1:], from_right[1]], axis=2
    )
    temp_left = jnp.concatenate([from_left, thermal_state[:, :, : width - 1]], axis=2)
    known_operator_term = thermal_state + sideways_coupling_quotient * (
        conduct_right * (temp_right - thermal_state)
        - sideways_face_flux_factor * (thermal_state - temp_left)
    )
    half_step = partition_solve(
        downward_face_flux_factor, None, known_operator_term, ratio_z, 0, "depth"
    )
    reflected = 2.0 * half_step - known_operator_term
    return partition_solve(
        sideways_face_flux_factor, None, reflected, sideways_coupling_quotient, 2, "lat"
    )


def solution(mesh):
    in_specs = (P("depth", None, "lat"), P("depth", None, "lat"), P("depth", None, "lat"))
    out_specs = P("depth", None, "lat")
    return jax.shard_map(
        on_device, mesh=mesh, in_specs=in_specs, out_specs=out_specs, check_vma=False
    )
```

time: 246 us -> 129 us (0.52)
  blocking collectives: 132 us -> 0 us
  starting transfers between devices: 65.8 us -> 27.4 us
  local copies, waits for them, and re-layouts: 14.5 us -> 38.4 us
  other arithmetic: 10.7 us -> 26.1 us
  waiting for transfers between devices: 20.6 us -> 34.7 us
    all_gather x4 -> x0, blocking collectives: 121 us -> none  [the longest x1 34 us: depth_reduced(): lax.all_gather(coeff_lower, 'depth', axis=0, tiled=True)]
    all_to_all x2, starting transfers between devices: 48.2 us -> 16.6 us  [gathered(): return lax.all_to_all(copies, axis, 0, 0, tiled=False)]
    all_to_all x2, waiting for transfers between devices: 16.3 us -> 34.7 us  [gathered(): return lax.all_to_all(copies, axis, 0, 0, tiled=False)]
    slice x93 -> x113, local copies, waits for them, and re-layouts: 3.58 us -> 18.5 us  [take_rows(): return lax.slice_in_dim(values, start, stop, axis=axis_index)]
    all_to_all x1 -> x0, blocking collectives: 11.8 us -> none  [on_device(): lax.all_to_all(solved, 'lat', split_axis=2, concat_axis=0, tiled=True)]
    ppermute x7 -> x2, starting transfers between devices: 17.6 us -> 10.8 us  [the longest x1 8.77 us: on_device(): from_right = lax.ppermute(first_cols, 'lat', left_pairs)]
    add x17 -> x19, other arithmetic: 2.71 us -> 9.28 us  [level_update(): column + alpha_term * low_col + gamma_term * high_col]
    broadcast_in_dim x0 -> x4, local copies, waits for them, and re-layouts: none -> 4.47 us  [the longest x1 1.89 us: partition_solve(): from_next = jnp.where(positions == count - 2, -last_upper, 0.0)]
  transfers between devices with their start and end apart: 9 -> 4, of which waited for: 4 -> 2; matrix products, arithmetic and copies ran while one was open for 3% -> 11% of each run, Pallas kernels for 0% -> 0%
where the time goes in v1:
time: 129 us; the launch traced here: 128 us
  local copies, waits for them, and re-layouts  38.4 us (30%)
  waiting for transfers between devices  34.7 us (27%)
  starting transfers between devices  27.4 us (21%)
  other arithmetic  26.1 us (20%)
    all_to_all x2, waiting for transfers between devices, gathered(): return lax.all_to_all(copies, axis, 0, 0, tiled=False)  34.7 us
    slice x113, local copies, waits for them, and re-layouts, take_rows(): return lax.slice_in_dim(values, start, stop, axis=axis_index)  18.5 us
    all_to_all x2, starting transfers between devices, gathered(): return lax.all_to_all(copies, axis, 0, 0, tiled=False)  16.6 us
    add x19, other arithmetic, level_update(): column + alpha_term * low_col + gamma_term * high_col  9.28 us
    ppermute x1, starting transfers between devices, on_device(): from_right = lax.ppermute(first_cols, 'lat', left_pairs)  8.77 us
    unnamed x45, local copies, waits for them, and re-layouts  5.07 us
  transfers between devices with their start and end apart: 4, of which 2 were waited for; matrix products, arithmetic and copies ran while one was open for 11% of the time, Pallas kernels for 0%

profile of v1, /device:TPU:1, one launch (start us, length us, event | category | flops | bytes accessed | tf_op | source)
XLA Modules:
  0.0 127.9 jit_solution(4941519757792977759)
XLA Ops:
  0.0 1.2 copy.185
  2.1 8.8 %collective-permute-start = (f32[2,32,8,1]{1,2,3,0:T(8,128)}, f32[2,32,8,1]{1,2,3,0:T(8,128)S(1)}, u32[]{:S(2)}, u32[]{:S(2)}) collective-permute-start(f32[2,32,8,1]{1,2,3,0:T(8,128)} %pad_maximum_fusion.2), channel_id=1, source_target_pairs={{1,0},{2,1},{3,2},{4,3},{5,4},{6,5},{7,6},{8,7},{9,8},{10,9},{11,1... | collective-permute-start | bytes 6152 | tf_op jit(solution)/shard_map/ppermute | solution.py:135
  11.7 2.0 %collective-permute-start.1 = (f32[32,8,1]{2,1,0:T(8,128)}, f32[32,8,1]{2,1,0:T(8,128)}, u32[]{:S(2)}, u32[]{:S(2)}) collective-permute-start(f32[32,8,1]{2,1,0:T(8,128)} %slice.798), channel_id=1, source_target_pairs={{0,1},{1,2},{2,3},{3,4},{4,5},{5,6},{6,7},{7,8},{8,9},{9,10},{10,1... | collective-permute-start | bytes 3080 | tf_op jit(solution)/shard_map/ppermute | solution.py:136
  14.3 0.8 slice_negate_fusion.1
  15.1 1.3 broadcast_multiply_fusion.2
  16.4 1.1 fusion.55
  17.5 1.0 slice_negate_fusion
  19.1 1.9 %copy.238 = f32[1,8,128]{1,2,0:T(8,128)S(1)} copy(f32[1,8,128]{0,1,2:T(8,128)} %slice_negate_fusion) | data formatting | bytes 8192 | tf_op jit(solution)/shard_map/jit(_where)/broadcast_in_dim | solution.py:82
  21.0 0.8 copy.237
  21.8 1.1 pad_maximum_fusion
  22.9 1.0 copy.191
  23.9 1.5 %fusion.5 = f32[32,8,128]{0,1,2:T(8,128)S(1)} fusion(f32[32,8,128]{0,1,2:T(8,128)} %copy-done.2, f32[32,8,1]{0,1,2:T(8,128)S(1)} %get-tuple-element.393, f32[32,8,127]{0,1,2:T(8,128)} %get-tuple-element.158, f32[32,8,1]{0,1,2:T(8,128)S(1)} %get-tuple-element.392, f32[32,8,127]{0,1,2:T(8,128)S(1)} %slice-done, f32[32,8,128]{0,1,2:T(8,128)S(1)} %copy.185, ...), kind=kLoop, calls=%fused_computation.13 | loop fusion | flops 294912 | bytes 786432 | tf_op jit(solution)/shard_map/add | solution.py:142
  25.7 0.8 copy-done.7
  28.8 1.0 multiply_add_fusion.4
  31.3 0.8 multiply_add_fusion.3
  37.3 1.0 add_divide_fusion.2
  38.3 2.3 %fusion.28 = (f32[1,8,128]{0,1,2:T(8,128)}, f32[1,8,128]{0,1,2:T(8,128)}, f32[1,8,128]{0,1,2:T(8,128)}, f32[1,8,128]{0,1,2:T(8,128)}, f32[1,8,128]{0,1,2:T(8,128)}, /*index=5*/f32[1,8,128]{0,1,2:T(8,128)}) fusion(f32[31,8,128]{0,1,2:T(8,128)S(1)} %add_divide_fusion, f32[32,8,128]{0,1,2:T(8,128)S(1)} %broadcast_multiply_fusion.1, ...), kind=kLoop, calls=%fused_computation.228 | loop fusion | flops 6144 | bytes 57344 | tf_op jit(solution)/shard_map/slice | solution.py:11
  40.6 1.3 %copy.202 = f32[1,8,128]{2,1,0:T(8,128)S(1)} copy(f32[1,8,128]{0,1,2:T(8,128)} %get-tuple-element.163) | data formatting | bytes 8192 | tf_op jit(solution)/shard_map/sub | solution.py:96
  41.9 1.2 copy.203
  43.4 1.3 %copy.205 = f32[1,8,128]{2,1,0:T(8,128)S(1)} copy(f32[1,8,128]{0,1,2:T(8,128)} %get-tuple-element.161) | data formatting | bytes 8192 | tf_op jit(solution)/shard_map/slice | solution.py:11
  44.7 1.2 copy.198
  46.9 1.1 broadcast_in_dim.70
  48.0 6.5 %all-to-all-start = ((f32[32,7,1024]{2,1,0:T(8,128)}), f32[32,7,1024]{2,1,0:T(8,128)}, u32[]{:S(2)}, u32[]{:S(2)}) async-start(f32[32,7,1024]{2,1,0:T(8,128)} %broadcast_in_dim.70), calls=%async_computation | async-start | bytes 2097152 | tf_op jit(solution)/shard_map/all_to_all | solution.py:67
  56.1 1.1 fusion.95
  57.1 25.5 %all-to-all-done = f32[32,7,1024]{2,1,0:T(8,128)} async-done(((f32[32,7,1024]{2,1,0:T(8,128)}), f32[32,7,1024]{2,1,0:T(8,128)}, u32[]{:S(2)}, u32[]{:S(2)}) %all-to-all-start) | async-done | bytes 917536 | tf_op jit(solution)/shard_map/all_to_all | solution.py:67
  82.6 4.2 %fusion.24 = (f32[31,1,1024]{2,1,0:T(1,128)S(1)}, f32[31,1,1024]{2,1,0:T(1,128)S(1)}, f32[31,1,1024]{2,1,0:T(1,128)S(1)}, f32[31,1,1024]{2,1,0:T(1,128)S(1)}, f3...) fusion(f32[32,7,1024]{2,1,0:T(8,128)} %all-to-all-done), kind=kLoop, calls=%fused_computation.224 | loop fusion | bytes 1523712 | tf_op jit(solution)/shard_map/slice | solution.py:11
  86.9 2.4 %fusion.25 = (f32[32,1,1024]{2,1,0:T(1,128)S(1)}, f32[32,1,1024]{2,1,0:T(1,128)S(1)}, f32[32,1,1024]{2,1,0:T(1,128)S(1)}) fusion(f32[32,7,1024]{2,1,0:T(8,128)} %all-to-all-done), kind=kLoop, calls=%fused_computation.225 | loop fusion | bytes 786432 | tf_op jit(solution)/shard_map/slice | solution.py:107
  92.1 0.9 copy-done.4
  94.3 1.0 copy-done.1
  95.7 1.0 multiply_add_fusion.23
  105.1 10.1 %all-to-all-start.1 = ((f32[16,7,256]{2,1,0:T(8,128)}), f32[16,7,256]{2,1,0:T(8,128)S(1)}, u32[]{:S(2)}, u32[]{:S(2)}) async-start(f32[16,7,256]{2,1,0:T(8,128)} %broadcast_in_dim.77), calls=%async_computation.1 | async-start | bytes 262144 | tf_op jit(solution)/shard_map/all_to_all | solution.py:67
  115.2 9.2 %all-to-all-done.1 = f32[16,7,256]{2,1,0:T(8,128)S(1)} async-done(((f32[16,7,256]{2,1,0:T(8,128)}), f32[16,7,256]{2,1,0:T(8,128)S(1)}, u32[]{:S(2)}, u32[]{:S(2)}) %all-to-all-start.1) | async-done | bytes 114720 | tf_op jit(solution)/shard_map/all_to_all | solution.py:67
  (237 shorter events, 30.1 us)
Async XLA Ops:
  0.0 1.2 copy-start.12
  1.5 17.6 %copy-start.2 = (f32[32,8,128]{0,1,2:T(8,128)}, f32[32,8,128]{0,1,2:T(8,128)S(1)}, u32[]{:S(2)}) copy-start(f32[32,8,128]{0,1,2:T(8,128)S(1)} %copy.193) | copy-start | bytes 393220
  2.1 21.8 %collective-permute-start = (f32[2,32,8,1]{1,2,3,0:T(8,128)}, f32[2,32,8,1]{1,2,3,0:T(8,128)S(1)}, u32[]{:S(2)}, u32[]{:S(2)}) collective-permute-start(f32[2,32,8,1]{1,2,3,0:T(8,128)} %pad_maximum_fusion.2), channel_id=1, source_target_pairs={{1,0},{2,1},{3,2},{4,3},{5,4},{6,5},{7,6},{8,7},{9,8},{10,9},{11,1... | collective-permute-start | bytes 6152 | tf_op jit(solution)/shard_map/ppermute | solution.py:135
  11.7 2.1 %copy-start.13 = (f32[32,8,128]{2,1,0:T(8,128)S(1)}, f32[32,8,128]{2,1,0:T(8,128)}, u32[]{:S(2)}) copy-start(f32[32,8,128]{2,1,0:T(8,128)} %param.5) | copy-start | bytes 393220
  11.7 10.2 %collective-permute-start.1 = (f32[32,8,1]{2,1,0:T(8,128)}, f32[32,8,1]{2,1,0:T(8,128)}, u32[]{:S(2)}, u32[]{:S(2)}) collective-permute-start(f32[32,8,1]{2,1,0:T(8,128)} %slice.798), channel_id=1, source_target_pairs={{0,1},{1,2},{2,3},{3,4},{4,5},{5,6},{6,7},{7,8},{8,9},{9,10},{10,1... | collective-permute-start | bytes 3080 | tf_op jit(solution)/shard_map/ppermute | solution.py:136
  13.8 1.3 %copy-start.3 = (f32[32,8,128]{0,1,2:T(8,128)}, f32[32,8,128]{0,1,2:T(8,128)S(1)}, u32[]{:S(2)}) copy-start(f32[32,8,128]{0,1,2:T(8,128)S(1)} %broadcast_multiply_fusion) | copy-start | bytes 393220
  19.1 1.9 %copy-start.9 = (f32[1,8,128]{0,1,2:T(8,128)S(1)}, f32[1,8,128]{0,1,2:T(8,128)}, u32[]{:S(2)}) copy-start(f32[1,8,128]{0,1,2:T(8,128)} %slice_negate_fusion.1) | copy-start | bytes 12292
  21.8 2.1 %slice-start = ((f32[32,8,128]{0,1,2:T(8,128)}), f32[32,8,127]{0,1,2:T(8,128)S(1)}, s32[]{:S(2)}) async-start(f32[32,8,128]{0,1,2:T(8,128)} %copy-done.2), calls=%async_computation.2 | async-start | bytes 1040384 | tf_op jit(solution)/shard_map/slice | solution.py:137
  25.4 1.0 copy-start.7
  25.5 1.2 copy-start.8
  25.7 1.0 copy-start.14
  40.6 2.5 %copy-start.6 = (f32[1,8,128]{0,1,2:T(8,128)S(1)}, f32[1,8,128]{0,1,2:T(8,128)}, u32[]{:S(2)}) copy-start(f32[1,8,128]{0,1,2:T(8,128)} %get-tuple-element.166) | copy-start | bytes 12292
  43.4 2.5 %copy-start.5 = (f32[1,8,128]{0,1,2:T(8,128)S(1)}, f32[1,8,128]{0,1,2:T(8,128)}, u32[]{:S(2)}) copy-start(f32[1,8,128]{0,1,2:T(8,128)} %get-tuple-element.162) | copy-start | bytes 12292
  46.1 0.7 slice-start.1
  48.0 8.1 %copy-start = (f32[32,8,127]{0,1,2:T(8,128)S(1)}, f32[32,8,127]{0,1,2:T(8,128)}, u32[]{:S(2)}) copy-start(f32[32,8,127]{0,1,2:T(8,128)} %get-tuple-element.157) | copy-start | bytes 390148
  48.0 34.6 %all-to-all-start = ((f32[32,7,1024]{2,1,0:T(8,128)}), f32[32,7,1024]{2,1,0:T(8,128)}, u32[]{:S(2)}, u32[]{:S(2)}) async-start(f32[32,7,1024]{2,1,0:T(8,128)} %broadcast_in_dim.70), calls=%async_computation | async-start | bytes 2097152 | tf_op jit(solution)/shard_map/all_to_all | solution.py:67
  92.0 1.0 copy-start.4
  92.0 1.2 copy-start.10
  92.1 1.3 %copy-start.11 = (f32[32,8,126]{0,1,2:T(8,128)S(1)}, f32[32,8,126]{0,1,2:T(8,128)}, u32[]{:S(2)}) copy-start(f32[32,8,126]{0,1,2:T(8,128)} %get-tuple-element.309) | copy-start | bytes 387076
  94.2 1.0 copy-start.1
  105.1 19.3 %all-to-all-start.1 = ((f32[16,7,256]{2,1,0:T(8,128)}), f32[16,7,256]{2,1,0:T(8,128)S(1)}, u32[]{:S(2)}, u32[]{:S(2)}) async-start(f32[16,7,256]{2,1,0:T(8,128)} %broadcast_in_dim.77), calls=%async_computation.1 | async-start | bytes 262144 | tf_op jit(solution)/shard_map/all_to_all | solution.py:67

commit v2 on v1

--- a/solution.py
+++ b/solution.py
@@ -2,6 +2,8 @@
 import jax.numpy as jnp
 from jax import lax
 from jax.sharding import PartitionSpec as P
+from jax.experimental import pallas as pl
+from jax.experimental.pallas import tpu as pltpu
 
 sideways_coupling_quotient = 20.0
 ratio_z = 2000.0
@@ -65,6 +67,97 @@
     count = lax.axis_size(axis)
     copies = jnp.broadcast_to(values[None], (count,) + values.shape)
     return lax.all_to_all(copies, axis, 0, 0, tiled=False)
+
+
+def depth_kernel(t_ref, s_ref, d_ref, tr_ref, sr_ref, tl_ref, base_ref, p_ref, n_ref, pieces_ref):
+    rows, _, width = t_ref.shape
+    temp = t_ref[...]
+    conduct = s_ref[...]
+    lane = lax.broadcasted_iota(jnp.int32, temp.shape, 2)
+    last = lane == width - 1
+    first = lane == 0
+    temp_right = jnp.where(last, tr_ref[...], pltpu.roll(temp, width - 1, 2))
+    conduct_right = jnp.where(last, sr_ref[...], pltpu.roll(conduct, width - 1, 2))
+    temp_left = jnp.where(first, tl_ref[...], pltpu.roll(temp, 1, 2))
+    base_ref[...] = temp + sideways_coupling_quotient * (
+        conduct_right * (temp_right - temp) - conduct * (temp - temp_left)
+    )
+    inner = rows - 1
+    lower = [-ratio_z * d_ref[i] for i in range(rows)]
+    upper = [lower[i + 1] for i in range(inner)]
+    c_term, r_local, r_prev = [], [], []
+    r_next = None
+    for i in range(inner):
+        diagonal = 1.0 - lower[i] - upper[i]
+        rhs = base_ref[i]
+        if i == 0:
+            den = diagonal
+            local = rhs / den
+            prev = -lower[i] / den
+        else:
+            den = diagonal - lower[i] * c_term[i - 1]
+            local = (rhs - lower[i] * r_local[i - 1]) / den
+            prev = (-lower[i] * r_prev[i - 1]) / den
+        if i < inner - 1:
+            c_term.append(upper[i] / den)
+        else:
+            c_term.append(None)
+            r_next = -upper[i] / den
+        r_local.append(local)
+        r_prev.append(prev)
+    local = r_local[inner - 1]
+    prev = r_prev[inner - 1]
+    nxt = r_next
+    lower_last = lower[rows - 1]
+    right_last = base_ref[rows - 1]
+    pieces_ref[0] = lower_last * prev
+    pieces_ref[1] = 1.0 - lower_last + lower_last * nxt
+    pieces_ref[2] = right_last - lower_last * local
+    base_ref[rows - 1] = -right_last
+    p_ref[rows - 1] = jnp.zeros_like(local)
+    n_ref[rows - 1] = jnp.full_like(local, 2.0)
+    for i in range(inner - 1, -1, -1):
+        if i < inner - 1:
+            local = r_local[i] - c_term[i] * local
+            prev = r_prev[i] - c_term[i] * prev
+            nxt = -c_term[i] * nxt
+        base_ref[i] = 2.0 * local - base_ref[i]
+        p_ref[i] = 2.0 * prev
+        n_ref[i] = 2.0 * nxt
+    pieces_ref[3] = local
+    pieces_ref[4] = prev
+    pieces_ref[5] = nxt
+    pieces_ref[6] = d_ref[0]
+
+
+def depth_local(temp, conduct, downward, temp_next, conduct_next, temp_prev):
+    rows, lines, width = temp.shape
+    full = jax.ShapeDtypeStruct(temp.shape, temp.dtype)
+    return pl.pallas_call(
+        depth_kernel,
+        out_shape=(full, full, full, jax.ShapeDtypeStruct((7, lines, width), temp.dtype)),
+    )(temp, conduct, downward, temp_next, conduct_next, temp_prev)
+
+
+def reduced_solve(pieces, ratio, axis):
+    line_shape = pieces.shape[1:]
+    every = gathered(pieces.reshape(7, -1), axis)
+    own_lower, own_diag, own_right = every[:, 0], every[:, 1], every[:, 2]
+    zero_row = jnp.zeros_like(every[:1, 0])
+    next_heads = [
+        jnp.concatenate([every[1:, i], zero_row], axis=0) for i in (3, 4, 5, 6)
+    ]
+    head_local, head_prev, head_next, next_conduct = next_heads
+    coupling = -ratio * next_conduct
+    red_diag = own_diag - coupling + coupling * head_prev
+    red_upper = coupling * head_next
+    red_right = own_right - coupling * head_local
+    solved = cyclic(own_lower, red_diag, red_upper, (red_right,), 0)[0]
+    padded = jnp.concatenate([zero_row, solved], axis=0)
+    index = lax.axis_index(axis)
+    previous = lax.dynamic_slice_in_dim(padded, index, 1, 0).reshape(line_shape)
+    interface_value = lax.dynamic_slice_in_dim(padded, index + 1, 1, 0).reshape(line_shape)
+    return previous, interface_value
 
 
 def partition_solve(conduct, first_next, rights, ratio, axis_index, axis):
@@ -134,19 +227,16 @@
     )
     from_right = lax.ppermute(first_cols, "lat", left_pairs)
     from_left = lax.ppermute(thermal_state[:, :, width - 1 :], "lat", right_pairs)
-    temp_right = jnp.concatenate([thermal_state[:, :, 1:], from_right[0]], axis=2)
-    conduct_right = jnp.concatenate(
-        [sideways_face_flux_factor[:, :, 1:], from_right[1]], axis=2
-    )
-    temp_left = jnp.concatenate([from_left, thermal_state[:, :, : width - 1]], axis=2)
-    known_operator_term = thermal_state + sideways_coupling_quotient * (
-        conduct_right * (temp_right - thermal_state)
-        - sideways_face_flux_factor * (thermal_state - temp_left)
-    )
-    half_step = partition_solve(
-        downward_face_flux_factor, None, known_operator_term, ratio_z, 0, "depth"
-    )
-    reflected = 2.0 * half_step - known_operator_term
+    base, prev_weight, own_weight, pieces = depth_local(
+        thermal_state,
+        sideways_face_flux_factor,
+        downward_face_flux_factor,
+        from_right[0],
+        from_right[1],
+        from_left,
+    )
+    previous, interface_value = reduced_solve(pieces, ratio_z, "depth")
+    reflected = base + prev_weight * previous + own_weight * interface_value
     return partition_solve(
         sideways_face_flux_factor, None, reflected, sideways_coupling_quotient, 2, "lat"
     )

time: 129 us -> 88.9 us (0.69)
  local copies, waits for them, and re-layouts: 38.4 us -> 16.6 us
  other arithmetic: 26.1 us -> 5.55 us
  Pallas kernels: 0 us -> 2.33 us
    slice x113 -> x77, local copies, waits for them, and re-layouts: 18.5 us -> 4.79 us  [take_rows(): return lax.slice_in_dim(values, start, stop, axis=axis_index)]
    add x19 -> x14, other arithmetic: 9.28 us -> 2.29 us  [level_update(): column + alpha_term * low_col + gamma_term * high_col]
    slice x2 -> x1, local copies, waits for them, and re-layouts: 2.47 us -> 0.04 us  [partition_solve(): own_lower, own_diag, own_right = (every[:, 0], every[:, 1], every[:, 2])]
    pallas_call x0 -> x1, Pallas kernels: none -> 2.33 us  [depth_local(): pl.pallas_call(depth_kernel, out_shape=(full, full, full, jax.ShapeDtypeS...]
    slice x1, other arithmetic: 2.34 us -> 0.47 us  [take_rows(): return lax.slice_in_dim(values, start, stop, axis=axis_index)]
    div x6 -> x4, other arithmetic: 2.37 us -> 0.5 us  [cyclic(): return tuple((column / diagonal for column in rights))]
    broadcast_in_dim x1, local copies, waits for them, and re-layouts: 1.89 us -> 0.24 us  [partition_solve(): from_next = jnp.where(positions == count - 2, -last_upper, 0.0)]
    add x1 -> x2, other arithmetic: 1.52 us -> 0.1 us  [the longest x1 0.08 us: reduced_solve(): red_diag = own_diag - coupling + coupling * head_prev]
  transfers between devices with their start and end apart: 4 -> 4, of which waited for: 2 -> 2; matrix products, arithmetic and copies ran while one was open for 11% -> 4% of each run, Pallas kernels for 0% -> 0%
where the time goes in v2:
time: 88.9 us; the launch traced here: 88.4 us
  waiting for transfers between devices  34.7 us (39%)
  starting transfers between devices  28.1 us (32%)
  local copies, waits for them, and re-layouts  16.6 us (19%)
  other arithmetic  5.55 us (6%)
  Pallas kernels  2.33 us (3%)
  between operations  1.1 us (1%)
    all_to_all x2, waiting for transfers between devices, gathered(): return lax.all_to_all(copies, axis, 0, 0, tiled=False)  34.7 us
    all_to_all x2, starting transfers between devices, gathered(): return lax.all_to_all(copies, axis, 0, 0, tiled=False)  17.4 us
    ppermute x1, starting transfers between devices, on_device(): from_right = lax.ppermute(first_cols, 'lat', left_pairs)  8.79 us
    slice x77, local copies, waits for them, and re-layouts, take_rows(): return lax.slice_in_dim(values, start, stop, axis=axis_index)  4.79 us
    unnamed x21, local copies, waits for them, and re-layouts  4.16 us
    pallas_call x1, Pallas kernels, depth_local(): pl.pallas_call(depth_kernel, out_shape=(full, full, full, jax.ShapeDtypeS...  2.33 us
    add x14, other arithmetic, level_update(): column + alpha_term * low_col + gamma_term * high_col  2.29 us
    ppermute x1, starting transfers between devices, on_device(): lax.ppermute(thermal_state[:, :, width - 1:], 'lat', right_pairs)  1.92 us
  transfers between devices with their start and end apart: 4, of which 2 were waited for; matrix products, arithmetic and copies ran while one was open for 4% of the time, Pallas kernels for 0%

profile of v2, /device:TPU:1, one launch (start us, length us, event | category | flops | bytes accessed | tf_op | source)
XLA Modules:
  0.0 88.4 jit_solution(9379616594516105689)
XLA Ops:
  0.0 1.1 %fusion.47 = (f32[32,8,1]{2,1,0:T(8,128)S(1)}, f32[32,8,1]{2,1,0:T(8,128)S(1)}) fusion(f32[32,8,128]{2,1,0:T(8,128)} %t_ref.1), kind=kLoop, calls=%fused_computation.194 | loop fusion | bytes 4096 | tf_op jit(solution)/shard_map/slice | solution.py:229
  1.2 0.8 copy-done
  2.2 8.8 %collective-permute-start = (f32[2,32,8,1]{1,2,3,0:T(8,128)S(1)}, f32[2,32,8,1]{1,2,3,0:T(8,128)S(1)}, u32[]{:S(2)}, u32[]{:S(2)}) collective-permute-start(f32[2,32,8,1]{1,2,3,0:T(8,128)S(1)} %pad_maximum_fusion.1), channel_id=1, source_target_pairs={{1,0},{2,1},{3,2},{4,3},{5,4},{6,5},{7,6},{8,7},{9,8},{10,9},{11,1... | collective-permute-start | bytes 6152 | tf_op jit(solution)/shard_map/ppermute | solution.py:228
  11.0 1.9 %collective-permute-start.1 = (f32[32,8,1]{2,1,0:T(8,128)S(1)}, f32[32,8,1]{2,1,0:T(8,128)S(1)}, u32[]{:S(2)}, u32[]{:S(2)}) collective-permute-start(f32[32,8,1]{2,1,0:T(8,128)S(1)} %get-tuple-element.189), channel_id=1, source_target_pairs={{0,1},{1,2},{2,3},{3,4},{4,5},{5,6},{6,7},{7,8},{8,9},{9,10},{10,1... | collective-permute-start | bytes 3080 | tf_op jit(solution)/shard_map/ppermute | solution.py:229
  13.1 0.2 copy.78
  13.7 0.2 copy.79
  14.1 0.8 copy.54.tr_ref
  14.8 0.8 copy.55.sr_ref
  15.6 0.6 copy-done.5
  16.3 2.3 %shard_map.37 = (f32[32,8,128]{2,1,0:T(8,128)}, f32[32,8,128]{2,1,0:T(8,128)}, f32[32,8,128]{2,1,0:T(8,128)}, f32[7,8,128]{2,1,0:T(8,128)}) custom-call(f32[32,8,128]{2,1,0:T(8,128)} %t_ref.1, f32[32,8,128]{2,1,0:T(8,128)} %s_ref.1, f32[32,8,128]{2,1,0:T(8,128)} %d_ref.1, f32[32,8,1]{2,1,0:T(8,128)} %copy.54.tr_ref, f32[32,8,1]{2,1,0:T(8,128)} %copy.55.sr_ref, ...), custom_call_target="tpu_custom_call" | custom-call | tf_op jit(solution)/shard_map/pallas_call | solution.py:136
  18.6 0.8 copy.155
  19.4 1.1 %broadcast_in_dim.40 = f32[32,7,1024]{2,1,0:T(8,128)} broadcast(f32[7,1024]{1,0:T(8,128)S(1)} %bitcast.99), dimensions={1,2} | broadcast | bytes 946176 | tf_op jit(solution)/shard_map/broadcast_in_dim | solution.py:68
  20.5 6.3 %all-to-all-start = ((f32[32,7,1024]{2,1,0:T(8,128)}), f32[32,7,1024]{2,1,0:T(8,128)S(1)}, u32[]{:S(2)}, u32[]{:S(2)}) async-start(f32[32,7,1024]{2,1,0:T(8,128)} %broadcast_in_dim.40), calls=%async_computation | async-start | bytes 2097152 | tf_op jit(solution)/shard_map/all_to_all | solution.py:69
  26.9 0.8 copy-done.1
  27.7 0.2 multiply_add_fusion.12
  28.5 25.6 %all-to-all-done = f32[32,7,1024]{2,1,0:T(8,128)S(1)} async-done(((f32[32,7,1024]{2,1,0:T(8,128)}), f32[32,7,1024]{2,1,0:T(8,128)S(1)}, u32[]{:S(2)}, u32[]{:S(2)}) %all-to-all-start) | async-done | bytes 917536 | tf_op jit(solution)/shard_map/all_to_all | solution.py:69
  54.0 0.5 fusion.18
  54.7 0.3 fusion.19
  56.6 0.7 copy-done.3
  57.6 0.3 fusion.5
  58.6 0.2 multiply_add_fusion.23
  59.6 0.2 multiply_add_fusion.21
  60.6 0.2 multiply_add_fusion.19
  61.6 0.2 multiply_add_fusion.17
  63.4 0.5 slice_reduce_fusion
  64.4 0.7 broadcast_in_dim.47
  65.1 11.1 %all-to-all-start.1 = ((f32[16,7,256]{2,1,0:T(8,128)}), f32[16,7,256]{2,1,0:T(8,128)S(1)}, u32[]{:S(2)}, u32[]{:S(2)}) async-start(f32[16,7,256]{2,1,0:T(8,128)} %broadcast_in_dim.47), calls=%async_computation.1 | async-start | bytes 262144 | tf_op jit(solution)/shard_map/all_to_all | solution.py:69
  76.2 9.2 %all-to-all-done.1 = f32[16,7,256]{2,1,0:T(8,128)S(1)} async-done(((f32[16,7,256]{2,1,0:T(8,128)}), f32[16,7,256]{2,1,0:T(8,128)S(1)}, u32[]{:S(2)}, u32[]{:S(2)}) %all-to-all-start.1) | async-done | bytes 114720 | tf_op jit(solution)/shard_map/all_to_all | solution.py:69
  86.0 0.5 broadcast.385
  86.5 0.7 fusion.17
  87.3 0.2 reshape.30
  87.7 0.8 pad_maximum_fusion
  (146 shorter events, 8.6 us)
Async XLA Ops:
  1.1 0.9 %copy-start = (f32[32,8,128]{2,1,0:T(8,128)S(1)}, f32[32,8,128]{2,1,0:T(8,128)}, u32[]{:S(2)}) copy-start(f32[32,8,128]{2,1,0:T(8,128)} %s_ref.1) | copy-start | bytes 393220
  2.2 11.8 %collective-permute-start = (f32[2,32,8,1]{1,2,3,0:T(8,128)S(1)}, f32[2,32,8,1]{1,2,3,0:T(8,128)S(1)}, u32[]{:S(2)}, u32[]{:S(2)}) collective-permute-start(f32[2,32,8,1]{1,2,3,0:T(8,128)S(1)} %pad_maximum_fusion.1), channel_id=1, source_target_pairs={{1,0},{2,1},{3,2},{4,3},{5,4},{6,5},{7,6},{8,7},{9,8},{10,9},{11,1... | collective-permute-start | bytes 6152 | tf_op jit(solution)/shard_map/ppermute | solution.py:228
  11.0 4.6 %collective-permute-start.1 = (f32[32,8,1]{2,1,0:T(8,128)S(1)}, f32[32,8,1]{2,1,0:T(8,128)S(1)}, u32[]{:S(2)}, u32[]{:S(2)}) collective-permute-start(f32[32,8,1]{2,1,0:T(8,128)S(1)} %get-tuple-element.189), channel_id=1, source_target_pairs={{0,1},{1,2},{2,3},{3,4},{4,5},{5,6},{6,7},{7,8},{8,9},{9,10},{10,1... | collective-permute-start | bytes 3080 | tf_op jit(solution)/shard_map/ppermute | solution.py:229
  15.6 0.6 copy-start.5
  20.5 33.6 %all-to-all-start = ((f32[32,7,1024]{2,1,0:T(8,128)}), f32[32,7,1024]{2,1,0:T(8,128)S(1)}, u32[]{:S(2)}, u32[]{:S(2)}) async-start(f32[32,7,1024]{2,1,0:T(8,128)} %broadcast_in_dim.40), calls=%async_computation | async-start | bytes 2097152 | tf_op jit(solution)/shard_map/all_to_all | solution.py:69
  26.8 0.9 %copy-start.1 = (f32[32,8,128]{2,1,0:T(8,128)S(1)}, f32[32,8,128]{2,1,0:T(8,128)}, u32[]{:S(2)}) copy-start(f32[32,8,128]{2,1,0:T(8,128)} %s_ref.1) | copy-start | bytes 393220
  56.4 0.9 %copy-start.3 = (f32[32,8,128]{2,1,0:T(8,128)S(1)}, f32[32,8,128]{2,1,0:T(8,128)}, u32[]{:S(2)}) copy-start(f32[32,8,128]{2,1,0:T(8,128)} %get-tuple-element.10) | copy-start | bytes 393220
  56.4 1.0 %copy-start.4 = (f32[32,8,128]{2,1,0:T(8,128)S(1)}, f32[32,8,128]{2,1,0:T(8,128)}, u32[]{:S(2)}) copy-start(f32[32,8,128]{2,1,0:T(8,128)} %get-tuple-element.12) | copy-start | bytes 393220
  56.5 0.9 %copy-start.2 = (f32[32,8,128]{2,1,0:T(8,128)S(1)}, f32[32,8,128]{2,1,0:T(8,128)}, u32[]{:S(2)}) copy-start(f32[32,8,128]{2,1,0:T(8,128)} %get-tuple-element.9) | copy-start | bytes 393220
  65.1 20.3 %all-to-all-start.1 = ((f32[16,7,256]{2,1,0:T(8,128)}), f32[16,7,256]{2,1,0:T(8,128)S(1)}, u32[]{:S(2)}, u32[]{:S(2)}) async-start(f32[16,7,256]{2,1,0:T(8,128)} %broadcast_in_dim.47), calls=%async_computation.1 | async-start | bytes 262144 | tf_op jit(solution)/shard_map/all_to_all | solution.py:69

commit v3 on v2

--- a/solution.py
+++ b/solution.py
@@ -61,12 +61,6 @@
         )
         stride = stride * 2
     return tuple((column / diagonal for column in rights))
-
-
-def gathered(values, axis):
-    count = lax.axis_size(axis)
-    copies = jnp.broadcast_to(values[None], (count,) + values.shape)
-    return lax.all_to_all(copies, axis, 0, 0, tiled=False)
 
 
 def depth_kernel(t_ref, s_ref, d_ref, tr_ref, sr_ref, tl_ref, base_ref, p_ref, n_ref, pieces_ref):
@@ -110,9 +104,9 @@
     nxt = r_next
     lower_last = lower[rows - 1]
     right_last = base_ref[rows - 1]
-    pieces_ref[0] = lower_last * prev
-    pieces_ref[1] = 1.0 - lower_last + lower_last * nxt
-    pieces_ref[2] = right_last - lower_last * local
+    own_lower = lower_last * prev
+    own_diag = 1.0 - lower_last + lower_last * nxt
+    own_right = right_last - lower_last * local
     base_ref[rows - 1] = -right_last
     p_ref[rows - 1] = jnp.zeros_like(local)
     n_ref[rows - 1] = jnp.full_like(local, 2.0)
@@ -124,35 +118,37 @@
         base_ref[i] = 2.0 * local - base_ref[i]
         p_ref[i] = 2.0 * prev
         n_ref[i] = 2.0 * nxt
-    pieces_ref[3] = local
-    pieces_ref[4] = prev
-    pieces_ref[5] = nxt
-    pieces_ref[6] = d_ref[0]
-
-
-def depth_local(temp, conduct, downward, temp_next, conduct_next, temp_prev):
+    head_coupling = lower[0]
+    own = (
+        own_lower,
+        own_diag,
+        own_right,
+        head_coupling * (prev - 1.0),
+        head_coupling * nxt,
+        head_coupling * local,
+    )
+    for block in range(pieces_ref.shape[0]):
+        for i in range(6):
+            pieces_ref[block, i] = own[i]
+
+
+def depth_local(temp, conduct, downward, temp_next, conduct_next, temp_prev, blocks):
     rows, lines, width = temp.shape
     full = jax.ShapeDtypeStruct(temp.shape, temp.dtype)
-    return pl.pallas_call(
-        depth_kernel,
-        out_shape=(full, full, full, jax.ShapeDtypeStruct((7, lines, width), temp.dtype)),
-    )(temp, conduct, downward, temp_next, conduct_next, temp_prev)
-
-
-def reduced_solve(pieces, ratio, axis):
-    line_shape = pieces.shape[1:]
-    every = gathered(pieces.reshape(7, -1), axis)
-    own_lower, own_diag, own_right = every[:, 0], every[:, 1], every[:, 2]
+    copies = jax.ShapeDtypeStruct((blocks, 6, lines, width), temp.dtype)
+    return pl.pallas_call(depth_kernel, out_shape=(full, full, full, copies))(temp, conduct, downward, temp_next, conduct_next, temp_prev)
+
+
+def reduced_solve(copies, ratio, axis):
+    line_shape = copies.shape[2:]
+    flat = copies.reshape(copies.shape[:2] + (-1,))
+    every = lax.all_to_all(flat, axis, 0, 0, tiled=False)
     zero_row = jnp.zeros_like(every[:1, 0])
-    next_heads = [
-        jnp.concatenate([every[1:, i], zero_row], axis=0) for i in (3, 4, 5, 6)
-    ]
-    head_local, head_prev, head_next, next_conduct = next_heads
-    coupling = -ratio * next_conduct
-    red_diag = own_diag - coupling + coupling * head_prev
-    red_upper = coupling * head_next
-    red_right = own_right - coupling * head_local
-    solved = cyclic(own_lower, red_diag, red_upper, (red_right,), 0)[0]
+    from_next = [jnp.concatenate([every[1:, i], zero_row], axis=0) for i in (3, 4, 5)]
+    red_diag = every[:, 1] + from_next[0]
+    red_upper = from_next[1]
+    red_right = every[:, 2] - from_next[2]
+    solved = cyclic(every[:, 0], red_diag, red_upper, (red_right,), 0)[0]
     padded = jnp.concatenate([zero_row, solved], axis=0)
     index = lax.axis_index(axis)
     previous = lax.dynamic_slice_in_dim(padded, index, 1, 0).reshape(line_shape)
@@ -182,38 +178,21 @@
     tail_next = take_rows(next_part, count - 2, count - 1, axis_index)
     lower_last = take_rows(lower_band, count - 1, count, axis_index)
     right_last = take_rows(rights, count - 1, count, axis_index)
+    head_coupling = take_rows(lower_band, 0, 1, axis_index)
     pieces = jnp.stack(
         [
             lower_last * tail_prev,
             1.0 - lower_last + lower_last * tail_next,
             right_last - lower_last * tail_local,
-            take_rows(local_part, 0, 1, axis_index),
-            take_rows(prev_part, 0, 1, axis_index),
-            take_rows(next_part, 0, 1, axis_index),
-            take_rows(conduct, 0, 1, axis_index),
+            head_coupling * (take_rows(prev_part, 0, 1, axis_index) - 1.0),
+            head_coupling * take_rows(next_part, 0, 1, axis_index),
+            head_coupling * take_rows(local_part, 0, 1, axis_index),
         ]
     )
-    line_shape = pieces.shape[1:]
-    flat = pieces.reshape(7, -1)
-    every = gathered(flat, axis)
-    blocks = every.shape[0]
-    own_lower, own_diag, own_right = every[:, 0], every[:, 1], every[:, 2]
-    zero_row = jnp.zeros_like(every[:1, 0])
-    next_heads = [
-        jnp.concatenate([every[1:, i], zero_row], axis=0) for i in (3, 4, 5, 6)
-    ]
-    head_local, head_prev, head_next, next_conduct = next_heads
-    coupling = -ratio * next_conduct
-    red_diag = own_diag - coupling + coupling * head_prev
-    red_upper = coupling * head_next
-    red_right = own_right - coupling * head_local
-    solved = cyclic(own_lower, red_diag, red_upper, (red_right,), 0)[0]
-    padded = jnp.concatenate([zero_row, solved], axis=0)
-    index = lax.axis_index(axis)
-    previous = lax.dynamic_slice_in_dim(padded, index, 1, 0).reshape(line_shape)
-    interface_value = lax.dynamic_slice_in_dim(padded, index + 1, 1, 0).reshape(line_shape)
+    blocks = lax.axis_size(axis)
+    copies = jnp.broadcast_to(pieces[None], (blocks,) + pieces.shape)
+    previous, interface_value = reduced_solve(copies, ratio, axis)
     inner_values = local_part + prev_part * previous + next_part * interface_value
-    del blocks, first_next
     return jnp.concatenate([inner_values, interface_value], axis=axis_index)
 
 
@@ -234,6 +213,7 @@
         from_right[0],
         from_right[1],
         from_left,
+        lax.axis_size("depth"),
     )
     previous, interface_value = reduced_solve(pieces, ratio_z, "depth")
     reflected = base + prev_weight * previous + own_weight * interface_value

time: 88.9 us -> 89.2 us (level)
  waiting for transfers between devices: 34.7 us -> 35.6 us
    reshape x1 -> x2, local copies, waits for them, and re-layouts: 0.22 us -> 2.45 us  [the longest x1 2.23 us: reduced_solve(): flat = copies.reshape(copies.shape[:2] + (-1,))]
    unnamed x21 -> x22, local copies, waits for them, and re-layouts: 4.16 us -> 2.68 us
    broadcast_in_dim x2 -> x1, local copies, waits for them, and re-layouts: 1.76 us -> 0.67 us  [partition_solve(): copies = jnp.broadcast_to(pieces[None], (blocks,) + pieces.shape)]
    all_to_all x2, waiting for transfers between devices: 34.7 us -> 35.6 us  [reduced_solve(): every = lax.all_to_all(flat, axis, 0, 0, tiled=False)]
    add x14 -> x12, other arithmetic: 2.29 us -> 2.16 us  [level_update(): column + alpha_term * low_col + gamma_term * high_col]
where the time goes in v3:
time: 89.2 us; the launch traced here: 88.8 us
  waiting for transfers between devices  35.6 us (40%)
  starting transfers between devices  28.2 us (32%)
  local copies, waits for them, and re-layouts  15.9 us (18%)
  other arithmetic  5.41 us (6%)
  Pallas kernels  2.59 us (3%)
  between operations  1.06 us (1%)
    all_to_all x2, waiting for transfers between devices, reduced_solve(): every = lax.all_to_all(flat, axis, 0, 0, tiled=False)  35.6 us
    all_to_all x2, starting transfers between devices, reduced_solve(): every = lax.all_to_all(flat, axis, 0, 0, tiled=False)  17.5 us
    ppermute x1, starting transfers between devices, on_device(): from_right = lax.ppermute(first_cols, 'lat', left_pairs)  8.78 us
    slice x77, local copies, waits for them, and re-layouts, take_rows(): return lax.slice_in_dim(values, start, stop, axis=axis_index)  4.68 us
    unnamed x22, local copies, waits for them, and re-layouts  2.68 us
    pallas_call x1, Pallas kernels, depth_local(): pl.pallas_call(depth_kernel, out_shape=(full, full, full, copies))  2.59 us
    reshape x1, local copies, waits for them, and re-layouts, reduced_solve(): flat = copies.reshape(copies.shape[:2] + (-1,))  2.23 us
    add x12, other arithmetic, level_update(): column + alpha_term * low_col + gamma_term * high_col  2.16 us
  transfers between devices with their start and end apart: 4, of which 2 were waited for; matrix products, arithmetic and copies ran while one was open for 4% of the time, Pallas kernels for 0%

profile of v3, /device:TPU:1, one launch (start us, length us, event | category | flops | bytes accessed | tf_op | source)
XLA Modules:
  0.0 88.8 jit_solution(160921429260485075)
XLA Ops:
  0.0 1.1 %fusion.58 = (f32[32,8,1]{2,1,0:T(8,128)S(1)}, f32[32,8,1]{2,1,0:T(8,128)S(1)}) fusion(f32[32,8,128]{2,1,0:T(8,128)} %t_ref.1), kind=kLoop, calls=%fused_computation.199 | loop fusion | bytes 4096 | tf_op jit(solution)/shard_map/slice | solution.py:208
  1.2 0.8 copy-done
  2.1 8.8 %collective-permute-start = (f32[2,32,8,1]{1,2,3,0:T(8,128)S(1)}, f32[2,32,8,1]{1,2,3,0:T(8,128)S(1)}, u32[]{:S(2)}, u32[]{:S(2)}) collective-permute-start(f32[2,32,8,1]{1,2,3,0:T(8,128)S(1)} %pad_maximum_fusion.1), channel_id=1, source_target_pairs={{1,0},{2,1},{3,2},{4,3},{5,4},{6,5},{7,6},{8,7},{9,8},{10,9},{11,1... | collective-permute-start | bytes 6152 | tf_op jit(solution)/shard_map/ppermute | solution.py:207
  10.9 1.9 %collective-permute-start.1 = (f32[32,8,1]{2,1,0:T(8,128)S(1)}, f32[32,8,1]{2,1,0:T(8,128)S(1)}, u32[]{:S(2)}, u32[]{:S(2)}) collective-permute-start(f32[32,8,1]{2,1,0:T(8,128)S(1)} %get-tuple-element.178), channel_id=1, source_target_pairs={{0,1},{1,2},{2,3},{3,4},{4,5},{5,6},{6,7},{7,8},{8,9},{9,10},{10,1... | collective-permute-start | bytes 3080 | tf_op jit(solution)/shard_map/ppermute | solution.py:208
  13.1 0.2 copy.86
  13.7 0.2 copy.85
  13.9 0.8 copy.61.tr_ref
  14.7 0.8 copy.62.sr_ref
  15.5 0.6 copy-done.5
  16.2 2.6 %shard_map.37 = (f32[32,8,128]{2,1,0:T(8,128)}, f32[32,8,128]{2,1,0:T(8,128)}, f32[32,8,128]{2,1,0:T(8,128)}, f32[32,6,8,128]{3,2,1,0:T(8,128)}) custom-call(f32[32,8,128]{2,1,0:T(8,128)} %t_ref.1, f32[32,8,128]{2,1,0:T(8,128)} %s_ref.1, f32[32,8,128]{2,1,0:T(8,128)} %d_ref.1, f32[32,8,1]{2,1,0:T(8,128)} %copy.61.tr_ref, f32[32,8,1]{2,1,0:T(8,128)} %copy.62.sr_ref, ...), custom_call_target="tpu_custom_call" | custom-call | tf_op jit(solution)/shard_map/pallas_call | solution.py:139
  18.7 2.2 %reshape.37 = f32[32,6,1024]{2,1,0:T(8,128)} reshape(f32[32,6,8,128]{3,2,1,0:T(8,128)} %get-tuple-element.11) | data formatting | bytes 1572864 | tf_op jit(solution)/shard_map/reshape | solution.py:144
  21.0 6.4 %all-to-all-start = ((f32[32,6,1024]{2,1,0:T(8,128)}), f32[32,6,1024]{2,1,0:T(8,128)S(1)}, u32[]{:S(2)}, u32[]{:S(2)}) async-start(f32[32,6,1024]{2,1,0:T(8,128)} %reshape.37), calls=%async_computation | async-start | bytes 2097152 | tf_op jit(solution)/shard_map/all_to_all | solution.py:145
  27.4 0.2 multiply_add_fusion.6
  28.2 26.5 %all-to-all-done = f32[32,6,1024]{2,1,0:T(8,128)S(1)} async-done(((f32[32,6,1024]{2,1,0:T(8,128)}), f32[32,6,1024]{2,1,0:T(8,128)S(1)}, u32[]{:S(2)}, u32[]{:S(2)}) %all-to-all-start) | async-done | bytes 786464 | tf_op jit(solution)/shard_map/all_to_all | solution.py:145
  54.7 0.4 fusion.20
  55.2 0.3 fusion.21
  57.0 0.8 copy-done.3
  58.0 0.3 multiply_add_fusion.5
  59.0 0.2 multiply_add_fusion.4
  60.0 0.2 multiply_add_fusion.3
  61.0 0.2 multiply_add_fusion.2
  61.9 0.2 multiply_add_fusion.1
  62.6 0.2 multiply_add_fusion.7
  63.5 0.2 add_divide_fusion
  63.7 0.5 fusion
  64.8 0.7 broadcast_in_dim.36
  65.5 11.1 %all-to-all-start.1 = ((f32[16,6,256]{2,1,0:T(8,128)}), f32[16,6,256]{2,1,0:T(8,128)S(1)}, u32[]{:S(2)}, u32[]{:S(2)}) async-start(f32[16,6,256]{2,1,0:T(8,128)} %broadcast_in_dim.36), calls=%async_computation.1 | async-start | bytes 262144 | tf_op jit(solution)/shard_map/all_to_all | solution.py:145
  76.6 9.2 %all-to-all-done.1 = f32[16,6,256]{2,1,0:T(8,128)S(1)} async-done(((f32[16,6,256]{2,1,0:T(8,128)}), f32[16,6,256]{2,1,0:T(8,128)S(1)}, u32[]{:S(2)}, u32[]{:S(2)}) %all-to-all-start.1) | async-done | bytes 98336 | tf_op jit(solution)/shard_map/all_to_all | solution.py:145
  86.3 0.5 broadcast.387
  86.8 0.7 fusion.19
  87.7 0.2 reshape.38
  88.0 0.8 pad_maximum_fusion
  (142 shorter events, 7.8 us)
Async XLA Ops:
  1.1 0.9 %copy-start = (f32[32,8,128]{2,1,0:T(8,128)S(1)}, f32[32,8,128]{2,1,0:T(8,128)}, u32[]{:S(2)}) copy-start(f32[32,8,128]{2,1,0:T(8,128)} %s_ref.1) | copy-start | bytes 393220
  2.1 11.8 %collective-permute-start = (f32[2,32,8,1]{1,2,3,0:T(8,128)S(1)}, f32[2,32,8,1]{1,2,3,0:T(8,128)S(1)}, u32[]{:S(2)}, u32[]{:S(2)}) collective-permute-start(f32[2,32,8,1]{1,2,3,0:T(8,128)S(1)} %pad_maximum_fusion.1), channel_id=1, source_target_pairs={{1,0},{2,1},{3,2},{4,3},{5,4},{6,5},{7,6},{8,7},{9,8},{10,9},{11,1... | collective-permute-start | bytes 6152 | tf_op jit(solution)/shard_map/ppermute | solution.py:207
  10.9 4.6 %collective-permute-start.1 = (f32[32,8,1]{2,1,0:T(8,128)S(1)}, f32[32,8,1]{2,1,0:T(8,128)S(1)}, u32[]{:S(2)}, u32[]{:S(2)}) collective-permute-start(f32[32,8,1]{2,1,0:T(8,128)S(1)} %get-tuple-element.178), channel_id=1, source_target_pairs={{0,1},{1,2},{2,3},{3,4},{4,5},{5,6},{6,7},{7,8},{8,9},{9,10},{10,1... | collective-permute-start | bytes 3080 | tf_op jit(solution)/shard_map/ppermute | solution.py:208
  15.5 0.6 copy-start.5
  21.0 6.4 %copy-start.1 = (f32[32,8,128]{2,1,0:T(8,128)S(1)}, f32[32,8,128]{2,1,0:T(8,128)}, u32[]{:S(2)}) copy-start(f32[32,8,128]{2,1,0:T(8,128)} %s_ref.1) | copy-start | bytes 393220
  21.0 33.7 %all-to-all-start = ((f32[32,6,1024]{2,1,0:T(8,128)}), f32[32,6,1024]{2,1,0:T(8,128)S(1)}, u32[]{:S(2)}, u32[]{:S(2)}) async-start(f32[32,6,1024]{2,1,0:T(8,128)} %reshape.37), calls=%async_computation | async-start | bytes 2097152 | tf_op jit(solution)/shard_map/all_to_all | solution.py:145
  56.8 0.9 %copy-start.3 = (f32[32,8,128]{2,1,0:T(8,128)S(1)}, f32[32,8,128]{2,1,0:T(8,128)}, u32[]{:S(2)}) copy-start(f32[32,8,128]{2,1,0:T(8,128)} %get-tuple-element.10) | copy-start | bytes 393220
  56.8 1.0 %copy-start.4 = (f32[32,8,128]{2,1,0:T(8,128)S(1)}, f32[32,8,128]{2,1,0:T(8,128)}, u32[]{:S(2)}) copy-start(f32[32,8,128]{2,1,0:T(8,128)} %get-tuple-element.12) | copy-start | bytes 393220
  56.9 1.0 %copy-start.2 = (f32[32,8,128]{2,1,0:T(8,128)S(1)}, f32[32,8,128]{2,1,0:T(8,128)}, u32[]{:S(2)}) copy-start(f32[32,8,128]{2,1,0:T(8,128)} %get-tuple-element.9) | copy-start | bytes 393220
  65.5 20.3 %all-to-all-start.1 = ((f32[16,6,256]{2,1,0:T(8,128)}), f32[16,6,256]{2,1,0:T(8,128)S(1)}, u32[]{:S(2)}, u32[]{:S(2)}) async-start(f32[16,6,256]{2,1,0:T(8,128)} %broadcast_in_dim.36), calls=%async_computation.1 | async-start | bytes 262144 | tf_op jit(solution)/shard_map/all_to_all | solution.py:145

commit v4 on v3

--- a/solution.py
+++ b/solution.py
@@ -63,15 +63,15 @@
     return tuple((column / diagonal for column in rights))
 
 
-def depth_kernel(t_ref, s_ref, d_ref, tr_ref, sr_ref, tl_ref, base_ref, p_ref, n_ref, pieces_ref):
+def depth_kernel(t_ref, s_ref, d_ref, right_ref, tl_ref, base_ref, p_ref, n_ref, pieces_ref):
     rows, _, width = t_ref.shape
     temp = t_ref[...]
     conduct = s_ref[...]
     lane = lax.broadcasted_iota(jnp.int32, temp.shape, 2)
     last = lane == width - 1
     first = lane == 0
-    temp_right = jnp.where(last, tr_ref[...], pltpu.roll(temp, width - 1, 2))
-    conduct_right = jnp.where(last, sr_ref[...], pltpu.roll(conduct, width - 1, 2))
+    temp_right = jnp.where(last, right_ref[0], pltpu.roll(temp, width - 1, 2))
+    conduct_right = jnp.where(last, right_ref[1], pltpu.roll(conduct, width - 1, 2))
     temp_left = jnp.where(first, tl_ref[...], pltpu.roll(temp, 1, 2))
     base_ref[...] = temp + sideways_coupling_quotient * (
         conduct_right * (temp_right - temp) - conduct * (temp - temp_left)
@@ -132,17 +132,18 @@
             pieces_ref[block, i] = own[i]
 
 
-def depth_local(temp, conduct, downward, temp_next, conduct_next, temp_prev, blocks):
+def depth_local(temp, conduct, downward, from_right, temp_prev, blocks):
     rows, lines, width = temp.shape
     full = jax.ShapeDtypeStruct(temp.shape, temp.dtype)
     copies = jax.ShapeDtypeStruct((blocks, 6, lines, width), temp.dtype)
-    return pl.pallas_call(depth_kernel, out_shape=(full, full, full, copies))(temp, conduct, downward, temp_next, conduct_next, temp_prev)
+    return pl.pallas_call(depth_kernel, out_shape=(full, full, full, copies))(
+        temp, conduct, downward, from_right, temp_prev
+    )
 
 
 def reduced_solve(copies, ratio, axis):
     line_shape = copies.shape[2:]
-    flat = copies.reshape(copies.shape[:2] + (-1,))
-    every = lax.all_to_all(flat, axis, 0, 0, tiled=False)
+    every = lax.all_to_all(copies, axis, 0, 0, tiled=False)
     zero_row = jnp.zeros_like(every[:1, 0])
     from_next = [jnp.concatenate([every[1:, i], zero_row], axis=0) for i in (3, 4, 5)]
     red_diag = every[:, 1] + from_next[0]
@@ -151,8 +152,8 @@
     solved = cyclic(every[:, 0], red_diag, red_upper, (red_right,), 0)[0]
     padded = jnp.concatenate([zero_row, solved], axis=0)
     index = lax.axis_index(axis)
-    previous = lax.dynamic_slice_in_dim(padded, index, 1, 0).reshape(line_shape)
-    interface_value = lax.dynamic_slice_in_dim(padded, index + 1, 1, 0).reshape(line_shape)
+    previous = lax.dynamic_slice_in_dim(padded, index, 1, 0)[0]
+    interface_value = lax.dynamic_slice_in_dim(padded, index + 1, 1, 0)[0]
     return previous, interface_value
 
 
@@ -210,8 +211,7 @@
         thermal_state,
         sideways_face_flux_factor,
         downward_face_flux_factor,
-        from_right[0],
-        from_right[1],
+        from_right,
         from_left,
         lax.axis_size("depth"),
     )

time: 89.2 us -> 82.2 us (0.922)
  waiting for transfers between devices: 35.6 us -> 31.1 us
  local copies, waits for them, and re-layouts: 15.9 us -> 12 us
  starting transfers between devices: 28.2 us -> 29.2 us
    all_to_all x2, waiting for transfers between devices: 35.6 us -> 29.1 us  [reduced_solve(): every = lax.all_to_all(copies, axis, 0, 0, tiled=False)]
    reshape x2 -> x0, local copies, waits for them, and re-layouts: 2.45 us -> none  [the longest x1 2.23 us: reduced_solve(): flat = copies.reshape(copies.shape[:2] + (-1,))]
    ppermute x1, waiting for transfers between devices: 0.01 us -> 1.93 us  [on_device(): lax.ppermute(thermal_state[:, :, width - 1:], 'lat', right_pairs)]
    unnamed x22 -> x24, local copies, waits for them, and re-layouts: 2.68 us -> 4.33 us
    squeeze x3 -> x1, local copies, waits for them, and re-layouts: 1.58 us -> 0.14 us  [reduced_solve(): interface_value = lax.dynamic_slice_in_dim(padded, index + 1, 1, 0)[0]]
    dynamic_slice x3 -> x0, local copies, waits for them, and re-layouts: 1.22 us -> none  [the longest x2 1.19 us: reduced_solve(): lax.dynamic_slice_in_dim(padded, index + 1, 1, 0).reshape(line_shape)]
    all_to_all x2, starting transfers between devices: 17.5 us -> 18.5 us  [reduced_solve(): every = lax.all_to_all(copies, axis, 0, 0, tiled=False)]
    slice x77 -> x76, local copies, waits for them, and re-layouts: 4.68 us -> 4.35 us  [take_rows(): return lax.slice_in_dim(values, start, stop, axis=axis_index)]
  transfers between devices with their start and end apart: 4 -> 4, of which waited for: 2 -> 3; matrix products, arithmetic and copies ran while one was open for 4% -> 1% of each run, Pallas kernels for 0% -> 0%
where the time goes in v4:
time: 82.2 us; the launch traced here: 81.9 us
  waiting for transfers between devices  31.1 us (38%)
  starting transfers between devices  29.2 us (36%)
  local copies, waits for them, and re-layouts  12 us (15%)
  other arithmetic  6.05 us (7%)
  Pallas kernels  2.54 us (3%)
  between operations  0.96 us (1%)
    all_to_all x2, waiting for transfers between devices, reduced_solve(): every = lax.all_to_all(copies, axis, 0, 0, tiled=False)  29.1 us
    all_to_all x2, starting transfers between devices, reduced_solve(): every = lax.all_to_all(copies, axis, 0, 0, tiled=False)  18.5 us
    ppermute x1, starting transfers between devices, on_device(): from_right = lax.ppermute(first_cols, 'lat', left_pairs)  8.79 us
    slice x76, local copies, waits for them, and re-layouts, take_rows(): return lax.slice_in_dim(values, start, stop, axis=axis_index)  4.35 us
    unnamed x24, local copies, waits for them, and re-layouts  4.33 us
    pallas_call x1, Pallas kernels, depth_local(): pl.pallas_call(depth_kernel, out_shape=(full, full, full, copies))  2.54 us
    add x12, other arithmetic, level_update(): column + alpha_term * low_col + gamma_term * high_col  2.24 us
    ppermute x1, waiting for transfers between devices, on_device(): lax.ppermute(thermal_state[:, :, width - 1:], 'lat', right_pairs)  1.93 us
  transfers between devices with their start and end apart: 4, of which 3 were waited for; matrix products, arithmetic and copies ran while one was open for 1% of the time, Pallas kernels for 0%

profile of v4, /device:TPU:1, one launch (start us, length us, event | category | flops | bytes accessed | tf_op | source)
XLA Modules:
  0.0 81.9 jit_solution(1015164910435616444)
XLA Ops:
  0.0 1.1 %fusion.75 = (f32[32,8,1]{2,1,0:T(8,128)S(1)}, f32[32,8,1]{2,1,0:T(8,128)S(1)}) fusion(f32[32,8,128]{2,1,0:T(8,128)} %t_ref.1), kind=kLoop, calls=%fused_computation.220 | loop fusion | bytes 4096 | tf_op jit(solution)/shard_map/slice | solution.py:209
  1.2 0.8 copy-done
  2.1 0.2 copy.305
  2.3 8.8 %collective-permute-start = (f32[2,32,8,1]{3,2,1,0:T(8,128)S(1)}, f32[2,32,8,1]{3,2,1,0:T(8,128)S(1)}, u32[]{:S(2)}, u32[]{:S(2)}) collective-permute-start(f32[2,32,8,1]{3,2,1,0:T(8,128)S(1)} %copy.305), channel_id=1, source_target_pairs={{1,0},{2,1},{3,2},{4,3},{5,4},{6,5},{7,6},{8,7},{9,8},{10,9},{11,1... | collective-permute-start | bytes 6152 | tf_op jit(solution)/shard_map/ppermute | solution.py:208
  11.1 1.9 %collective-permute-start.1 = (f32[32,8,1]{2,1,0:T(8,128)S(1)}, f32[32,8,1]{2,1,0:T(8,128)S(1)}, u32[]{:S(2)}, u32[]{:S(2)}) collective-permute-start(f32[32,8,1]{2,1,0:T(8,128)S(1)} %get-tuple-element.247), channel_id=1, source_target_pairs={{0,1},{1,2},{2,3},{3,4},{4,5},{5,6},{6,7},{7,8},{8,9},{9,10},{10,1... | collective-permute-start | bytes 3080 | tf_op jit(solution)/shard_map/ppermute | solution.py:209
  13.0 1.9 %collective-permute-done.1.tl_ref = f32[32,8,1]{2,1,0:T(8,128)S(1)} collective-permute-done((f32[32,8,1]{2,1,0:T(8,128)S(1)}, f32[32,8,1]{2,1,0:T(8,128)S(1)}, u32[]{:S(2)}, u32[]{:S(2)}) %collective-permute-start.1) | collective-permute-done | bytes 1056 | tf_op jit(solution)/shard_map/ppermute | solution.py:209
  15.0 0.6 copy-done.6
  15.6 0.7 copy-done.2
  16.3 2.5 %shard_map.37 = (f32[32,8,128]{2,1,0:T(8,128)}, f32[32,8,128]{2,1,0:T(8,128)}, f32[32,8,128]{2,1,0:T(8,128)}, f32[32,6,8,128]{3,2,1,0:T(8,128)}) custom-call(f32[32,8,128]{2,1,0:T(8,128)} %t_ref.1, f32[32,8,128]{2,1,0:T(8,128)} %s_ref.1, f32[32,8,128]{2,1,0:T(8,128)} %d_ref.1, f32[2,32,8,1]{3,2,1,0:T(8,128)} %copy-done.2, f32[32,8,1]{2,1,0:T(8,128)} %copy-done.6), custom_call_target="tpu_custom_call" | custom-call | tf_op jit(solution)/shard_map/pallas_call | solution.py:139
  18.9 6.4 %all-to-all-start = ((f32[32,6,8,128]{3,2,1,0:T(8,128)}), f32[32,6,8,128]{3,2,1,0:T(8,128)S(1)}, u32[]{:S(2)}, u32[]{:S(2)}) async-start(f32[32,6,8,128]{3,2,1,0:T(8,128)} %get-tuple-element.11), calls=%async_computation | async-start | bytes 1572864 | tf_op jit(solution)/shard_map/all_to_all | solution.py:146
  25.5 0.2 copy.337
  25.8 0.2 copy.336
  26.2 20.6 %all-to-all-done = f32[32,6,8,128]{3,2,1,0:T(8,128)S(1)} async-done(((f32[32,6,8,128]{3,2,1,0:T(8,128)}), f32[32,6,8,128]{3,2,1,0:T(8,128)S(1)}, u32[]{:S(2)}, u32[]{:S(2)}) %all-to-all-start) | async-done | bytes 786464 | tf_op jit(solution)/shard_map/all_to_all | solution.py:146
  47.1 0.1 multiply_add_fusion.31
  48.1 0.8 copy-done.4
  49.1 0.2 fusion.3
  50.1 0.3 multiply_add_fusion.6
  51.2 0.2 multiply_add_fusion.5
  52.1 0.2 multiply_add_fusion.4
  53.1 0.2 multiply_add_fusion.3
  54.1 0.2 multiply_add_fusion.2
  54.8 0.2 multiply_add_fusion.1
  55.5 0.2 add_divide_fusion
  55.7 0.2 add_divide_fusion.2
  55.9 0.2 slice_multiply_fusion
  57.0 0.8 %reshape.23 = f32[16,1,1536]{2,1,0:T(1,128)} reshape(f32[16,6,1,8,32]{4,3,2,1,0:T(8,128)S(1)} %broadcast_bitcast_fusion) | data formatting | bytes 196608
  57.9 12.1 %all-to-all-start.1 = ((f32[16,1,1536]{2,1,0:T(1,128)}), f32[16,1,1536]{2,1,0:T(1,128)S(1)}, u32[]{:S(2)}, u32[]{:S(2)}) async-start(f32[16,1,1536]{2,1,0:T(1,128)} %reshape.23), calls=%async_computation.1 | async-start | bytes 196608 | tf_op jit(solution)/shard_map/all_to_all | solution.py:146
  69.9 8.5 %all-to-all-done.1 = f32[16,1,1536]{2,1,0:T(1,128)S(1)} async-done(((f32[16,1,1536]{2,1,0:T(1,128)}), f32[16,1,1536]{2,1,0:T(1,128)S(1)}, u32[]{:S(2)}, u32[]{:S(2)}) %all-to-all-start.1) | async-done | bytes 98336 | tf_op jit(solution)/shard_map/all_to_all | solution.py:146
  78.4 0.5 broadcast.370
  78.9 0.9 %reduce = f32[16,1536]{1,0:T(8,128)S(1)} reduce(f32[16,1,1536]{2,1,0:T(1,128)S(1)} %all-to-all-done.1, f32[]{:T(128)} %broadcast.370), dimensions={1}, to_apply=%all_to_all.7.reduce_sub_computation | reduce | bytes 196612 | tf_op jit(solution)/shard_map/all_to_all | solution.py:146
  79.8 0.1 reshape.24
  81.1 0.8 pad_maximum_fusion
  (135 shorter events, 7.8 us)
Async XLA Ops:
  1.1 0.9 %copy-start = (f32[32,8,128]{2,1,0:T(8,128)S(1)}, f32[32,8,128]{2,1,0:T(8,128)}, u32[]{:S(2)}) copy-start(f32[32,8,128]{2,1,0:T(8,128)} %s_ref.1) | copy-start | bytes 393220
  2.3 12.7 %collective-permute-start = (f32[2,32,8,1]{3,2,1,0:T(8,128)S(1)}, f32[2,32,8,1]{3,2,1,0:T(8,128)S(1)}, u32[]{:S(2)}, u32[]{:S(2)}) collective-permute-start(f32[2,32,8,1]{3,2,1,0:T(8,128)S(1)} %copy.305), channel_id=1, source_target_pairs={{1,0},{2,1},{3,2},{4,3},{5,4},{6,5},{7,6},{8,7},{9,8},{10,9},{11,1... | collective-permute-start | bytes 6152 | tf_op jit(solution)/shard_map/ppermute | solution.py:208
  11.1 3.9 %collective-permute-start.1 = (f32[32,8,1]{2,1,0:T(8,128)S(1)}, f32[32,8,1]{2,1,0:T(8,128)S(1)}, u32[]{:S(2)}, u32[]{:S(2)}) collective-permute-start(f32[32,8,1]{2,1,0:T(8,128)S(1)} %get-tuple-element.247), channel_id=1, source_target_pairs={{0,1},{1,2},{2,3},{3,4},{4,5},{5,6},{6,7},{7,8},{8,9},{9,10},{10,1... | collective-permute-start | bytes 3080 | tf_op jit(solution)/shard_map/ppermute | solution.py:209
  15.0 0.7 copy-start.6
  15.6 0.7 copy-start.2
  18.9 6.4 %copy-start.1 = (f32[32,8,128]{2,1,0:T(8,128)S(1)}, f32[32,8,128]{2,1,0:T(8,128)}, u32[]{:S(2)}) copy-start(f32[32,8,128]{2,1,0:T(8,128)} %s_ref.1) | copy-start | bytes 393220
  18.9 27.9 %all-to-all-start = ((f32[32,6,8,128]{3,2,1,0:T(8,128)}), f32[32,6,8,128]{3,2,1,0:T(8,128)S(1)}, u32[]{:S(2)}, u32[]{:S(2)}) async-start(f32[32,6,8,128]{3,2,1,0:T(8,128)} %get-tuple-element.11), calls=%async_computation | async-start | bytes 1572864 | tf_op jit(solution)/shard_map/all_to_all | solution.py:146
  48.0 0.9 %copy-start.4 = (f32[32,8,128]{2,1,0:T(8,128)S(1)}, f32[32,8,128]{2,1,0:T(8,128)}, u32[]{:S(2)}) copy-start(f32[32,8,128]{2,1,0:T(8,128)} %get-tuple-element.10) | copy-start | bytes 393220
  48.0 1.0 %copy-start.5 = (f32[32,8,128]{2,1,0:T(8,128)S(1)}, f32[32,8,128]{2,1,0:T(8,128)}, u32[]{:S(2)}) copy-start(f32[32,8,128]{2,1,0:T(8,128)} %get-tuple-element.12) | copy-start | bytes 393220
  48.1 0.9 %copy-start.3 = (f32[32,8,128]{2,1,0:T(8,128)S(1)}, f32[32,8,128]{2,1,0:T(8,128)}, u32[]{:S(2)}) copy-start(f32[32,8,128]{2,1,0:T(8,128)} %get-tuple-element.9) | copy-start | bytes 393220
  57.9 20.6 %all-to-all-start.1 = ((f32[16,1,1536]{2,1,0:T(1,128)}), f32[16,1,1536]{2,1,0:T(1,128)S(1)}, u32[]{:S(2)}, u32[]{:S(2)}) async-start(f32[16,1,1536]{2,1,0:T(1,128)} %reshape.23), calls=%async_computation.1 | async-start | bytes 196608 | tf_op jit(solution)/shard_map/all_to_all | solution.py:146

commit v5 on v4

--- a/solution.py
+++ b/solution.py
@@ -141,6 +141,70 @@
     )
 
 
+def lateral_kernel(base_ref, p_ref, n_ref, xp_ref, x_ref, s_ref, local_ref, prev_ref, next_ref, pieces_ref):
+    rows, lines, width = s_ref.shape
+    ratio = sideways_coupling_quotient
+    rights = base_ref[...] + p_ref[...] * xp_ref[...][None] + n_ref[...] * x_ref[...][None]
+    conduct = s_ref[...]
+    lane = lax.broadcasted_iota(jnp.int32, conduct.shape, 2)
+    inner = lane < width - 1
+    conduct_next = pltpu.roll(conduct, width - 1, 2)
+    lower_full = -ratio * conduct
+    upper_full = -ratio * conduct_next
+    diagonal = jnp.where(inner, 1.0 - lower_full - upper_full, 1.0)
+    lower = jnp.where((lane >= 1) & inner, lower_full, 0.0)
+    upper = jnp.where(lane < width - 2, upper_full, 0.0)
+    columns = (
+        jnp.where(inner, rights, 0.0),
+        jnp.where(lane == 0, -lower_full, 0.0),
+        jnp.where(lane == width - 2, -upper_full, 0.0),
+    )
+    stride = 1
+    while stride < width:
+        has_below = lane >= stride
+        has_above = lane < width - stride
+
+        def below(v, filler):
+            return jnp.where(has_below, pltpu.roll(v, stride, 2), filler)
+
+        def above(v, filler):
+            return jnp.where(has_above, pltpu.roll(v, width - stride, 2), filler)
+
+        alpha_term = -lower / below(diagonal, 1.0)
+        gamma_term = -upper / above(diagonal, 1.0)
+        new_diagonal = diagonal + alpha_term * below(upper, 0.0) + gamma_term * above(lower, 0.0)
+        columns = tuple(
+            column + alpha_term * below(column, 0.0) + gamma_term * above(column, 0.0)
+            for column in columns
+        )
+        lower, upper = alpha_term * below(lower, 0.0), gamma_term * above(upper, 0.0)
+        diagonal = new_diagonal
+        stride = stride * 2
+    local, prev, nxt = (column / diagonal for column in columns)
+    local_ref[...] = local
+    prev_ref[...] = prev
+    next_ref[...] = nxt
+    tail = [pltpu.roll(v, 1, 2) for v in (local, prev, nxt)]
+    own_lower = lower_full * tail[1]
+    own_diag = 1.0 - lower_full + lower_full * tail[2]
+    own_right = rights - lower_full * tail[0]
+    own = [v[:, :, width - 1 :] for v in (own_lower, own_diag, own_right)]
+    heads = (lower_full * (prev - 1.0), lower_full * nxt, lower_full * local)
+    own = own + [v[:, :, :1] for v in heads]
+    for block in range(pieces_ref.shape[0]):
+        for i in range(6):
+            pieces_ref[block, i] = own[i]
+
+
+def lateral_local(base, prev_weight, own_weight, previous, interface_value, conduct, blocks):
+    rows, lines, width = conduct.shape
+    full = jax.ShapeDtypeStruct(conduct.shape, conduct.dtype)
+    copies = jax.ShapeDtypeStruct((blocks, 6, rows, lines, 1), conduct.dtype)
+    return pl.pallas_call(lateral_kernel, out_shape=(full, full, full, copies))(
+        base, prev_weight, own_weight, previous, interface_value, conduct
+    )
+
+
 def reduced_solve(copies, ratio, axis):
     line_shape = copies.shape[2:]
     every = lax.all_to_all(copies, axis, 0, 0, tiled=False)
@@ -216,9 +280,19 @@
         lax.axis_size("depth"),
     )
     previous, interface_value = reduced_solve(pieces, ratio_z, "depth")
-    reflected = base + prev_weight * previous + own_weight * interface_value
-    return partition_solve(
-        sideways_face_flux_factor, None, reflected, sideways_coupling_quotient, 2, "lat"
+    local, prev, nxt, copies = lateral_local(
+        base,
+        prev_weight,
+        own_weight,
+        previous,
+        interface_value,
+        sideways_face_flux_factor,
+        lax.axis_size("lat"),
+    )
+    previous, interface_value = reduced_solve(copies, sideways_coupling_quotient, "lat")
+    lane = lax.broadcasted_iota(jnp.int32, local.shape, 2)
+    return jnp.where(
+        lane == width - 1, interface_value, local + prev * previous + nxt * interface_value
     )
 
 

time: 82.2 us -> 91.8 us (1.12)
  Pallas kernels: 2.54 us -> 12.3 us
  other arithmetic: 6.05 us -> 2.7 us
  local copies, waits for them, and re-layouts: 12 us -> 14.9 us
    pallas_call x0 -> x1, Pallas kernels: none -> 9.76 us  [lateral_local(): pl.pallas_call(lateral_kernel, out_shape=(full, full, full, copies))]
    pallas_call x0 -> x1, local copies, waits for them, and re-layouts: none -> 8.42 us  [lateral_local(): pl.pallas_call(lateral_kernel, out_shape=(full, full, full, copies))]
    slice x76 -> x35, local copies, waits for them, and re-layouts: 4.35 us -> 0.48 us  [take_rows(): return lax.slice_in_dim(values, start, stop, axis=axis_index)]
    add x12 -> x5, other arithmetic: 2.24 us -> 0.5 us  [level_update(): column + alpha_term * low_col + gamma_term * high_col]
    unnamed x24 -> x14, local copies, waits for them, and re-layouts: 4.33 us -> 3.5 us
  transfers between devices with their start and end apart: 4 -> 4, of which waited for: 3 -> 3; matrix products, arithmetic and copies ran while one was open for 1% -> 0% of each run, Pallas kernels for 0% -> 0%
where the time goes in v5:
time: 91.8 us; the launch traced here: 91.4 us
  waiting for transfers between devices  31.9 us (35%)
  starting transfers between devices  29.1 us (32%)
  local copies, waits for them, and re-layouts  14.9 us (16%)
  Pallas kernels  12.3 us (13%)
  other arithmetic  2.7 us (3%)
    all_to_all x2, waiting for transfers between devices, reduced_solve(): every = lax.all_to_all(copies, axis, 0, 0, tiled=False)  30 us
    all_to_all x2, starting transfers between devices, reduced_solve(): every = lax.all_to_all(copies, axis, 0, 0, tiled=False)  18.4 us
    pallas_call x1, Pallas kernels, lateral_local(): pl.pallas_call(lateral_kernel, out_shape=(full, full, full, copies))  9.76 us
    ppermute x1, starting transfers between devices, on_device(): from_right = lax.ppermute(first_cols, 'lat', left_pairs)  8.79 us
    pallas_call x1, local copies, waits for them, and re-layouts, lateral_local(): pl.pallas_call(lateral_kernel, out_shape=(full, full, full, copies))  8.42 us
    unnamed x14, local copies, waits for them, and re-layouts  3.5 us
    pallas_call x1, Pallas kernels, depth_local(): pl.pallas_call(depth_kernel, out_shape=(full, full, full, copies))  2.55 us
    ppermute x1, waiting for transfers between devices, on_device(): lax.ppermute(thermal_state[:, :, width - 1:], 'lat', right_pairs)  1.93 us
  transfers between devices with their start and end apart: 4, of which 3 were waited for; matrix products, arithmetic and copies ran while one was open for 0% of the time, Pallas kernels for 0%

profile of v5, /device:TPU:1, one launch (start us, length us, event | category | flops | bytes accessed | tf_op | source)
XLA Modules:
  0.0 91.4 jit_solution(7268008878972875079)
XLA Ops:
  0.0 1.1 %fusion.29 = (f32[32,8,1]{2,1,0:T(8,128)S(1)}, f32[32,8,1]{2,1,0:T(8,128)S(1)}) fusion(f32[32,8,128]{2,1,0:T(8,128)} %t_ref.1), kind=kLoop, calls=%fused_computation.96 | loop fusion | bytes 4096 | tf_op jit(solution)/shard_map/slice | solution.py:273
  1.1 0.1 copy.232
  1.2 1.0 %copy.233 = f32[32,8,1]{0,1,2:T(8,128)S(1)} copy(f32[32,8,1]{2,1,0:T(8,128)} %bitcast.103) | data formatting | bytes 2048
  2.2 0.2 copy.221
  2.4 8.8 %collective-permute-start = (f32[2,32,8,1]{3,2,1,0:T(8,128)S(1)}, f32[2,32,8,1]{3,2,1,0:T(8,128)S(1)}, u32[]{:S(2)}, u32[]{:S(2)}) collective-permute-start(f32[2,32,8,1]{3,2,1,0:T(8,128)S(1)} %copy.221), channel_id=1, source_target_pairs={{1,0},{2,1},{3,2},{4,3},{5,4},{6,5},{7,6},{8,7},{9,8},{10,9},{11,1... | collective-permute-start | bytes 6152 | tf_op jit(solution)/shard_map/ppermute | solution.py:272
  11.2 1.9 %collective-permute-start.1 = (f32[32,8,1]{2,1,0:T(8,128)S(1)}, f32[32,8,1]{2,1,0:T(8,128)S(1)}, u32[]{:S(2)}, u32[]{:S(2)}) collective-permute-start(f32[32,8,1]{2,1,0:T(8,128)S(1)} %get-tuple-element.91), channel_id=1, source_target_pairs={{0,1},{1,2},{2,3},{3,4},{4,5},{5,6},{6,7},{7,8},{8,9},{9,10},{10,1... | collective-permute-start | bytes 3080 | tf_op jit(solution)/shard_map/ppermute | solution.py:273
  13.2 1.9 %collective-permute-done.1.tl_ref = f32[32,8,1]{2,1,0:T(8,128)S(1)} collective-permute-done((f32[32,8,1]{2,1,0:T(8,128)S(1)}, f32[32,8,1]{2,1,0:T(8,128)S(1)}, u32[]{:S(2)}, u32[]{:S(2)}) %collective-permute-start.1) | collective-permute-done | bytes 1056 | tf_op jit(solution)/shard_map/ppermute | solution.py:273
  15.1 0.6 copy-done.4
  15.7 0.7 copy-done
  16.4 2.5 %shard_map.37 = (f32[32,8,128]{2,1,0:T(8,128)}, f32[32,8,128]{2,1,0:T(8,128)}, f32[32,8,128]{2,1,0:T(8,128)}, f32[32,6,8,128]{3,2,1,0:T(8,128)}) custom-call(f32[32,8,128]{2,1,0:T(8,128)} %t_ref.1, f32[32,8,128]{2,1,0:T(8,128)} %s_ref.3, f32[32,8,128]{2,1,0:T(8,128)} %d_ref.1, f32[2,32,8,1]{3,2,1,0:T(8,128)} %copy-done, f32[32,8,1]{2,1,0:T(8,128)} %copy-done.4), custom_call_target="tpu_custom_call" | custom-call | tf_op jit(solution)/shard_map/pallas_call | solution.py:139
  19.0 6.3 %all-to-all-start = ((f32[32,6,8,128]{3,2,1,0:T(8,128)}), f32[32,6,8,128]{3,2,1,0:T(8,128)S(1)}, u32[]{:S(2)}, u32[]{:S(2)}) async-start(f32[32,6,8,128]{3,2,1,0:T(8,128)} %get-tuple-element.16), calls=%async_computation | async-start | bytes 1572864 | tf_op jit(solution)/shard_map/all_to_all | solution.py:210
  25.3 21.5 %all-to-all-done = f32[32,6,8,128]{3,2,1,0:T(8,128)S(1)} async-done(((f32[32,6,8,128]{3,2,1,0:T(8,128)}), f32[32,6,8,128]{3,2,1,0:T(8,128)S(1)}, u32[]{:S(2)}, u32[]{:S(2)}) %all-to-all-start) | async-done | bytes 786464 | tf_op jit(solution)/shard_map/all_to_all | solution.py:210
  47.0 0.1 multiply_add_fusion.6
  47.1 0.1 multiply_add_fusion.5
  47.4 0.1 multiply_add_fusion.3
  47.7 0.1 multiply_add_fusion.1
  47.8 0.1 pad_multiply_fusion
  48.0 0.1 add_divide_fusion
  48.0 0.6 fusion.12
  48.7 9.8 %shard_map.38 = (f32[32,8,128]{2,1,0:T(8,128)}, f32[32,8,128]{2,1,0:T(8,128)}, f32[32,8,128]{2,1,0:T(8,128)}, f32[16,6,32,8,1]{4,3,2,1,0:T(8,128)}) custom-call(f32[32,8,128]{2,1,0:T(8,128)} %get-tuple-element.13.base_ref, f32[32,8,128]{2,1,0:T(8,128)} %get-tuple-element.14.p_ref, f32[32,8,128]{2,1,0:T(8,128)} %get-tuple-element.15.n_ref, ...), custom_call_target="tpu_custom_call" | custom-call | tf_op jit(solution)/shard_map/pallas_call | solution.py:203
  58.4 8.4 %copy.229 = f32[16,6,32,8,1]{2,3,4,1,0:T(8,128)S(1)} copy(f32[16,6,32,8,1]{4,3,2,1,0:T(8,128)} %get-tuple-element.17) | data formatting | bytes 196608 | tf_op jit(solution)/shard_map/pallas_call | solution.py:203
  66.8 0.8 reshape.20
  67.7 12.1 %all-to-all-start.1 = ((f32[16,1,1536]{2,1,0:T(1,128)}), f32[16,1,1536]{2,1,0:T(1,128)S(1)}, u32[]{:S(2)}, u32[]{:S(2)}) async-start(f32[16,1,1536]{2,1,0:T(1,128)} %reshape.20), calls=%async_computation.1 | async-start | bytes 196608 | tf_op jit(solution)/shard_map/all_to_all | solution.py:210
  79.8 8.5 %all-to-all-done.1 = f32[16,1,1536]{2,1,0:T(1,128)S(1)} async-done(((f32[16,1,1536]{2,1,0:T(1,128)}), f32[16,1,1536]{2,1,0:T(1,128)S(1)}, u32[]{:S(2)}, u32[]{:S(2)}) %all-to-all-start.1) | async-done | bytes 98336 | tf_op jit(solution)/shard_map/all_to_all | solution.py:210
  88.3 0.5 broadcast.172
  88.8 0.8 reduce
  89.6 0.1 reshape.21
  89.9 0.1 multiply_add_fusion.11
  90.1 0.1 multiply_add_fusion.9
  90.4 0.1 copy.230
  90.5 0.1 copy.231
  90.6 0.8 add_select_fusion
  (55 shorter events, 0.9 us)
Async XLA Ops:
  2.4 12.7 %collective-permute-start = (f32[2,32,8,1]{3,2,1,0:T(8,128)S(1)}, f32[2,32,8,1]{3,2,1,0:T(8,128)S(1)}, u32[]{:S(2)}, u32[]{:S(2)}) collective-permute-start(f32[2,32,8,1]{3,2,1,0:T(8,128)S(1)} %copy.221), channel_id=1, source_target_pairs={{1,0},{2,1},{3,2},{4,3},{5,4},{6,5},{7,6},{8,7},{9,8},{10,9},{11,1... | collective-permute-start | bytes 6152 | tf_op jit(solution)/shard_map/ppermute | solution.py:272
  11.2 3.9 %collective-permute-start.1 = (f32[32,8,1]{2,1,0:T(8,128)S(1)}, f32[32,8,1]{2,1,0:T(8,128)S(1)}, u32[]{:S(2)}, u32[]{:S(2)}) collective-permute-start(f32[32,8,1]{2,1,0:T(8,128)S(1)} %get-tuple-element.91), channel_id=1, source_target_pairs={{0,1},{1,2},{2,3},{3,4},{4,5},{5,6},{6,7},{7,8},{8,9},{9,10},{10,1... | collective-permute-start | bytes 3080 | tf_op jit(solution)/shard_map/ppermute | solution.py:273
  15.1 0.7 copy-start.4
  15.7 0.7 copy-start
  19.0 27.8 %all-to-all-start = ((f32[32,6,8,128]{3,2,1,0:T(8,128)}), f32[32,6,8,128]{3,2,1,0:T(8,128)S(1)}, u32[]{:S(2)}, u32[]{:S(2)}) async-start(f32[32,6,8,128]{3,2,1,0:T(8,128)} %get-tuple-element.16), calls=%async_computation | async-start | bytes 1572864 | tf_op jit(solution)/shard_map/all_to_all | solution.py:210
  58.4 32.1 %copy-start.1 = (f32[32,8,128]{2,1,0:T(8,128)S(1)}, f32[32,8,128]{2,1,0:T(8,128)}, u32[]{:S(2)}) copy-start(f32[32,8,128]{2,1,0:T(8,128)} %get-tuple-element.18) | copy-start | bytes 393220
  58.4 32.1 %copy-start.2 = (f32[32,8,128]{2,1,0:T(8,128)S(1)}, f32[32,8,128]{2,1,0:T(8,128)}, u32[]{:S(2)}) copy-start(f32[32,8,128]{2,1,0:T(8,128)} %get-tuple-element.19) | copy-start | bytes 393220
  58.4 32.1 %copy-start.3 = (f32[32,8,128]{2,1,0:T(8,128)S(1)}, f32[32,8,128]{2,1,0:T(8,128)}, u32[]{:S(2)}) copy-start(f32[32,8,128]{2,1,0:T(8,128)} %get-tuple-element.20) | copy-start | bytes 393220
  67.7 20.6 %all-to-all-start.1 = ((f32[16,1,1536]{2,1,0:T(1,128)}), f32[16,1,1536]{2,1,0:T(1,128)S(1)}, u32[]{:S(2)}, u32[]{:S(2)}) async-start(f32[16,1,1536]{2,1,0:T(1,128)} %reshape.20), calls=%async_computation.1 | async-start | bytes 196608 | tf_op jit(solution)/shard_map/all_to_all | solution.py:210

commit v6 on v4

--- a/solution.py
+++ b/solution.py
@@ -40,27 +40,40 @@
     return (alpha_term * below[0], new_diagonal, gamma_term * above[2], new_rights)
 
 
-def cyclic(lower_band, diagonal, upper_band, rights, axis_index):
+def cyclic_factors(lower_band, diagonal, upper_band, axis_index):
     count = lower_band.shape[axis_index]
     stride = 1
+    levels = []
     while stride < count:
-        below = (
-            moved(lower_band, stride, axis_index, 0.0, False),
-            moved(diagonal, stride, axis_index, 1.0, False),
-            moved(upper_band, stride, axis_index, 0.0, False),
-            tuple((moved(column, stride, axis_index, 0.0, False) for column in rights)),
-        )
-        above = (
-            moved(lower_band, stride, axis_index, 0.0, True),
-            moved(diagonal, stride, axis_index, 1.0, True),
-            moved(upper_band, stride, axis_index, 0.0, True),
-            tuple((moved(column, stride, axis_index, 0.0, True) for column in rights)),
-        )
-        lower_band, diagonal, upper_band, rights = level_update(
-            lower_band, diagonal, upper_band, rights, below, above
-        )
+        alpha_term = -lower_band / moved(diagonal, stride, axis_index, 1.0, False)
+        gamma_term = -upper_band / moved(diagonal, stride, axis_index, 1.0, True)
+        new_diagonal = (
+            diagonal
+            + alpha_term * moved(upper_band, stride, axis_index, 0.0, False)
+            + gamma_term * moved(lower_band, stride, axis_index, 0.0, True)
+        )
+        lower_band = alpha_term * moved(lower_band, stride, axis_index, 0.0, False)
+        upper_band = gamma_term * moved(upper_band, stride, axis_index, 0.0, True)
+        diagonal = new_diagonal
+        levels.append((stride, alpha_term, gamma_term))
         stride = stride * 2
-    return tuple((column / diagonal for column in rights))
+    return levels, diagonal
+
+
+def cyclic_apply(factors, column, axis_index):
+    levels, diagonal = factors
+    for stride, alpha_term, gamma_term in levels:
+        column = (
+            column
+            + alpha_term * moved(column, stride, axis_index, 0.0, False)
+            + gamma_term * moved(column, stride, axis_index, 0.0, True)
+        )
+    return column / diagonal
+
+
+def cyclic(lower_band, diagonal, upper_band, rights, axis_index):
+    factors = cyclic_factors(lower_band, diagonal, upper_band, axis_index)
+    return tuple(cyclic_apply(factors, column, axis_index) for column in rights)
 
 
 def depth_kernel(t_ref, s_ref, d_ref, right_ref, tl_ref, base_ref, p_ref, n_ref, pieces_ref):
@@ -171,9 +184,17 @@
     from_prev = jnp.where(positions == 0, -first_lower, 0.0)
     from_next = jnp.where(positions == count - 2, -last_upper, 0.0)
     inner_rights = take_rows(rights, 0, count - 1, axis_index)
-    local_part, prev_part, next_part = cyclic(
-        solve_lower, diagonal, solve_upper, (inner_rights, from_prev, from_next), axis_index
-    )
+    factors = cyclic_factors(solve_lower, diagonal, solve_upper, axis_index)
+    prev_part = cyclic_apply(factors, from_prev, axis_index)
+    next_part = cyclic_apply(factors, from_next, axis_index)
+    levels, last_diagonal = factors
+    strides = [level[0] for level in levels]
+    terms = [level[1:] for level in levels]
+    terms, last_diagonal, prev_part, next_part = lax.optimization_barrier(
+        (terms, last_diagonal, prev_part, next_part)
+    )
+    factors = ([(s,) + tuple(t) for s, t in zip(strides, terms)], last_diagonal)
+    local_part = cyclic_apply(factors, inner_rights, axis_index)
     tail_local = take_rows(local_part, count - 2, count - 1, axis_index)
     tail_prev = take_rows(prev_part, count - 2, count - 1, axis_index)
     tail_next = take_rows(next_part, count - 2, count - 1, axis_index)

time: 82.2 us -> 79.1 us (0.962)
  starting transfers between devices: 29.2 us -> 26.6 us
  waiting for transfers between devices: 31.1 us -> 29.1 us
  other arithmetic: 6.05 us -> 7.55 us
    all_to_all x2, starting transfers between devices: 18.5 us -> 15.9 us  [reduced_solve(): every = lax.all_to_all(copies, axis, 0, 0, tiled=False)]
    ppermute x1, waiting for transfers between devices: 1.93 us -> 0.01 us  [on_device(): lax.ppermute(thermal_state[:, :, width - 1:], 'lat', right_pairs)]
    add x22 -> x28, other arithmetic: 3.08 us -> 4.47 us  [the longest x18 3.63 us: cyclic_apply(): column + alpha_term * moved(column, stride, axis_index, 0.0, False)]
    unnamed x24 -> x20, local copies, waits for them, and re-layouts: 4.33 us -> 3.68 us
    slice x76 -> x75, local copies, waits for them, and re-layouts: 4.35 us -> 4.91 us  [take_rows(): return lax.slice_in_dim(values, start, stop, axis=axis_index)]
  transfers between devices with their start and end apart: 4 -> 4, of which waited for: 3 -> 2; matrix products, arithmetic and copies ran while one was open for 1% -> 10% of each run, Pallas kernels for 0% -> 0%
where the time goes in v6:
time: 79.1 us; the launch traced here: 78.7 us
  waiting for transfers between devices  29.1 us (37%)
  starting transfers between devices  26.6 us (34%)
  local copies, waits for them, and re-layouts  12 us (15%)
  other arithmetic  7.55 us (10%)
  Pallas kernels  2.56 us (3%)
  between operations  0.99 us (1%)
    all_to_all x2, waiting for transfers between devices, reduced_solve(): every = lax.all_to_all(copies, axis, 0, 0, tiled=False)  29 us
    all_to_all x2, starting transfers between devices, reduced_solve(): every = lax.all_to_all(copies, axis, 0, 0, tiled=False)  15.9 us
    ppermute x1, starting transfers between devices, on_device(): from_right = lax.ppermute(first_cols, 'lat', left_pairs)  8.79 us
    slice x75, local copies, waits for them, and re-layouts, take_rows(): return lax.slice_in_dim(values, start, stop, axis=axis_index)  4.91 us
    unnamed x20, local copies, waits for them, and re-layouts  3.68 us
    add x18, other arithmetic, cyclic_apply(): column + alpha_term * moved(column, stride, axis_index, 0.0, False)  3.63 us
    pallas_call x1, Pallas kernels, depth_local(): pl.pallas_call(depth_kernel, out_shape=(full, full, full, copies))  2.56 us
    ppermute x1, starting transfers between devices, on_device(): lax.ppermute(thermal_state[:, :, width - 1:], 'lat', right_pairs)  1.92 us
  transfers between devices with their start and end apart: 4, of which 2 were waited for; matrix products, arithmetic and copies ran while one was open for 10% of the time, Pallas kernels for 0%

profile of v6, /device:TPU:1, one launch (start us, length us, event | category | flops | bytes accessed | tf_op | source)
XLA Modules:
  0.0 78.7 jit_solution(3758340978738096288)
XLA Ops:
  0.0 1.1 %fusion.40 = (f32[32,8,1]{2,1,0:T(8,128)S(1)}, f32[32,8,1]{2,1,0:T(8,128)S(1)}) fusion(f32[32,8,128]{2,1,0:T(8,128)} %t_ref.1), kind=kLoop, calls=%fused_computation.185 | loop fusion | bytes 4096 | tf_op jit(solution)/shard_map/slice | solution.py:230
  1.2 0.8 copy-done
  2.1 0.2 copy.302
  2.3 8.8 %collective-permute-start = (f32[2,32,8,1]{3,2,1,0:T(8,128)S(1)}, f32[2,32,8,1]{3,2,1,0:T(8,128)S(1)}, u32[]{:S(2)}, u32[]{:S(2)}) collective-permute-start(f32[2,32,8,1]{3,2,1,0:T(8,128)S(1)} %copy.302), channel_id=1, source_target_pairs={{1,0},{2,1},{3,2},{4,3},{5,4},{6,5},{7,6},{8,7},{9,8},{10,9},{11,1... | collective-permute-start | bytes 6152 | tf_op jit(solution)/shard_map/ppermute | solution.py:229
  11.1 1.9 %collective-permute-start.1 = (f32[32,8,1]{2,1,0:T(8,128)S(1)}, f32[32,8,1]{2,1,0:T(8,128)}, u32[]{:S(2)}, u32[]{:S(2)}) collective-permute-start(f32[32,8,1]{2,1,0:T(8,128)S(1)} %get-tuple-element.182), channel_id=1, source_target_pairs={{0,1},{1,2},{2,3},{3,4},{4,5},{5,6},{6,7},{7,8},{8,9},{9,10},{10,1... | collective-permute-start | bytes 3080 | tf_op jit(solution)/shard_map/ppermute | solution.py:230
  13.3 0.2 copy.334
  13.9 0.2 copy.333
  14.1 0.3 multiply_add_fusion.12
  15.0 0.2 multiply_add_fusion.11
  15.8 0.2 multiply_add_fusion.10
  16.7 0.2 multiply_add_fusion.9
  17.5 0.2 multiply_add_fusion.8
  18.3 0.2 multiply_add_fusion.7
  18.8 0.7 copy-done.1
  19.5 2.6 %shard_map.37 = (f32[32,8,128]{2,1,0:T(8,128)}, f32[32,8,128]{2,1,0:T(8,128)}, f32[32,8,128]{2,1,0:T(8,128)}, f32[32,6,8,128]{3,2,1,0:T(8,128)}) custom-call(f32[32,8,128]{2,1,0:T(8,128)} %t_ref.1, f32[32,8,128]{2,1,0:T(8,128)} %s_ref.1, f32[32,8,128]{2,1,0:T(8,128)} %d_ref.1, f32[2,32,8,1]{3,2,1,0:T(8,128)} %copy-done.1, ...), custom_call_target="tpu_custom_call" | custom-call | tf_op jit(solution)/shard_map/pallas_call | solution.py:152
  22.0 6.3 %all-to-all-start = ((f32[32,6,8,128]{3,2,1,0:T(8,128)}), f32[32,6,8,128]{3,2,1,0:T(8,128)S(1)}, u32[]{:S(2)}, u32[]{:S(2)}) async-start(f32[32,6,8,128]{3,2,1,0:T(8,128)} %get-tuple-element.28), calls=%async_computation | async-start | bytes 1572864 | tf_op jit(solution)/shard_map/all_to_all | solution.py:159
  28.3 0.8 fusion.50
  29.1 1.1 %multiply_add_fusion.13 = (f32[32,8,127]{2,1,0:T(8,128)S(1)}, f32[32,8,127]{2,1,0:T(8,128)S(1)}, f32[32,8,127]{2,1,0:T(8,128)S(1)}, f32[32,8,127]{2,1,0:T(8,128)S(1)}) fusion(f32[32,8,127]{2,1,0:T(8,128)S(1)} %get-tuple-element.41, f32[32,8,95]{2,1,0:T(8,128)S(1)} %get-tuple-element.189, f32[32,8,127]{2,1,0:T(8,128)S(1)} %get-tuple-element.122, ...), kind=kLoop, calls=%fused_computation.34 | loop fusion | flops 325120 | bytes 1624064 | tf_op jit(solution)/shard_map/add | solution.py:67
  30.6 0.2 add_divide_fusion.1
  30.9 20.6 %all-to-all-done = f32[32,6,8,128]{3,2,1,0:T(8,128)S(1)} async-done(((f32[32,6,8,128]{3,2,1,0:T(8,128)}), f32[32,6,8,128]{3,2,1,0:T(8,128)S(1)}, u32[]{:S(2)}, u32[]{:S(2)}) %all-to-all-start) | async-done | bytes 786464 | tf_op jit(solution)/shard_map/all_to_all | solution.py:159
  51.8 0.1 multiply_add_fusion.32
  52.8 0.8 copy-done.3
  55.2 0.2 slice_multiply_fusion
  56.3 0.8 %reshape.23 = f32[16,1,1536]{2,1,0:T(1,128)} reshape(f32[16,6,1,8,32]{4,3,2,1,0:T(8,128)S(1)} %broadcast_bitcast_fusion) | data formatting | bytes 196608
  57.2 9.6 %all-to-all-start.1 = ((f32[16,1,1536]{2,1,0:T(1,128)}), f32[16,1,1536]{2,1,0:T(1,128)S(1)}, u32[]{:S(2)}, u32[]{:S(2)}) async-start(f32[16,1,1536]{2,1,0:T(1,128)} %reshape.23), calls=%async_computation.1 | async-start | bytes 196608 | tf_op jit(solution)/shard_map/all_to_all | solution.py:159
  66.8 8.5 %all-to-all-done.1 = f32[16,1,1536]{2,1,0:T(1,128)S(1)} async-done(((f32[16,1,1536]{2,1,0:T(1,128)}), f32[16,1,1536]{2,1,0:T(1,128)S(1)}, u32[]{:S(2)}, u32[]{:S(2)}) %all-to-all-start.1) | async-done | bytes 98336 | tf_op jit(solution)/shard_map/all_to_all | solution.py:159
  75.3 0.5 broadcast.370
  75.8 0.9 %reduce = f32[16,1536]{1,0:T(8,128)S(1)} reduce(f32[16,1,1536]{2,1,0:T(1,128)S(1)} %all-to-all-done.1, f32[]{:T(128)} %broadcast.370), dimensions={1}, to_apply=%all_to_all.7.reduce_sub_computation | reduce | bytes 196612 | tf_op jit(solution)/shard_map/all_to_all | solution.py:159
  76.7 0.1 reshape.24
  77.6 0.1 copy.332
  77.8 0.1 multiply_add_fusion
  77.9 0.8 pad_maximum_fusion
  (139 shorter events, 8.3 us)
Async XLA Ops:
  1.1 0.9 %copy-start = (f32[32,8,128]{2,1,0:T(8,128)S(1)}, f32[32,8,128]{2,1,0:T(8,128)}, u32[]{:S(2)}) copy-start(f32[32,8,128]{2,1,0:T(8,128)} %s_ref.1) | copy-start | bytes 393220
  2.3 16.4 %collective-permute-start = (f32[2,32,8,1]{3,2,1,0:T(8,128)S(1)}, f32[2,32,8,1]{3,2,1,0:T(8,128)S(1)}, u32[]{:S(2)}, u32[]{:S(2)}) collective-permute-start(f32[2,32,8,1]{3,2,1,0:T(8,128)S(1)} %copy.302), channel_id=1, source_target_pairs={{1,0},{2,1},{3,2},{4,3},{5,4},{6,5},{7,6},{8,7},{9,8},{10,9},{11,1... | collective-permute-start | bytes 6152 | tf_op jit(solution)/shard_map/ppermute | solution.py:229
  11.1 7.6 %collective-permute-start.1 = (f32[32,8,1]{2,1,0:T(8,128)S(1)}, f32[32,8,1]{2,1,0:T(8,128)}, u32[]{:S(2)}, u32[]{:S(2)}) collective-permute-start(f32[32,8,1]{2,1,0:T(8,128)S(1)} %get-tuple-element.182), channel_id=1, source_target_pairs={{0,1},{1,2},{2,3},{3,4},{4,5},{5,6},{6,7},{7,8},{8,9},{9,10},{10,1... | collective-permute-start | bytes 3080 | tf_op jit(solution)/shard_map/ppermute | solution.py:230
  18.8 0.7 copy-start.1
  22.0 29.5 %all-to-all-start = ((f32[32,6,8,128]{3,2,1,0:T(8,128)}), f32[32,6,8,128]{3,2,1,0:T(8,128)S(1)}, u32[]{:S(2)}, u32[]{:S(2)}) async-start(f32[32,6,8,128]{3,2,1,0:T(8,128)} %get-tuple-element.28), calls=%async_computation | async-start | bytes 1572864 | tf_op jit(solution)/shard_map/all_to_all | solution.py:159
  52.6 0.9 %copy-start.3 = (f32[32,8,128]{2,1,0:T(8,128)S(1)}, f32[32,8,128]{2,1,0:T(8,128)}, u32[]{:S(2)}) copy-start(f32[32,8,128]{2,1,0:T(8,128)} %get-tuple-element.27) | copy-start | bytes 393220
  52.7 1.0 %copy-start.4 = (f32[32,8,128]{2,1,0:T(8,128)S(1)}, f32[32,8,128]{2,1,0:T(8,128)}, u32[]{:S(2)}) copy-start(f32[32,8,128]{2,1,0:T(8,128)} %get-tuple-element.29) | copy-start | bytes 393220
  52.7 1.0 %copy-start.2 = (f32[32,8,128]{2,1,0:T(8,128)S(1)}, f32[32,8,128]{2,1,0:T(8,128)}, u32[]{:S(2)}) copy-start(f32[32,8,128]{2,1,0:T(8,128)} %get-tuple-element.26) | copy-start | bytes 393220
  57.2 18.1 %all-to-all-start.1 = ((f32[16,1,1536]{2,1,0:T(1,128)}), f32[16,1,1536]{2,1,0:T(1,128)S(1)}, u32[]{:S(2)}, u32[]{:S(2)}) async-start(f32[16,1,1536]{2,1,0:T(1,128)} %reshape.23), calls=%async_computation.1 | async-start | bytes 196608 | tf_op jit(solution)/shard_map/all_to_all | solution.py:159

commit v7 on v6

--- a/solution.py
+++ b/solution.py
@@ -237,9 +237,10 @@
         lax.axis_size("depth"),
     )
     previous, interface_value = reduced_solve(pieces, ratio_z, "depth")
+    lateral_conduct = lax.optimization_barrier((sideways_face_flux_factor, pieces))[0]
     reflected = base + prev_weight * previous + own_weight * interface_value
     return partition_solve(
-        sideways_face_flux_factor, None, reflected, sideways_coupling_quotient, 2, "lat"
+        lateral_conduct, None, reflected, sideways_coupling_quotient, 2, "lat"
     )
 
 

time: 79.1 us -> 77 us (0.973)
  waiting for transfers between devices: 29.1 us -> 25.2 us
  starting transfers between devices: 26.6 us -> 29.2 us
  other arithmetic: 7.55 us -> 6.65 us
    all_to_all x2, waiting for transfers between devices: 29 us -> 23.3 us  [reduced_solve(): every = lax.all_to_all(copies, axis, 0, 0, tiled=False)]
    all_to_all x2, starting transfers between devices: 15.9 us -> 18.5 us  [reduced_solve(): every = lax.all_to_all(copies, axis, 0, 0, tiled=False)]
    ppermute x1, waiting for transfers between devices: 0.01 us -> 1.9 us  [on_device(): lax.ppermute(thermal_state[:, :, width - 1:], 'lat', right_pairs)]
    add x18, other arithmetic: 3.63 us -> 2.67 us  [cyclic_apply(): column + alpha_term * moved(column, stride, axis_index, 0.0, False)]
    unnamed x20 -> x24, local copies, waits for them, and re-layouts: 3.68 us -> 4.34 us
  transfers between devices with their start and end apart: 4 -> 4, of which waited for: 2 -> 3; matrix products, arithmetic and copies ran while one was open for 10% -> 8% of each run, Pallas kernels for 0% -> 0%
where the time goes in v7:
time: 77 us; the launch traced here: 76.6 us
  starting transfers between devices  29.2 us (38%)
  waiting for transfers between devices  25.2 us (33%)
  local copies, waits for them, and re-layouts  12 us (16%)
  other arithmetic  6.65 us (9%)
  Pallas kernels  2.53 us (3%)
  between operations  0.98 us (1%)
    all_to_all x2, waiting for transfers between devices, reduced_solve(): every = lax.all_to_all(copies, axis, 0, 0, tiled=False)  23.3 us
    all_to_all x2, starting transfers between devices, reduced_solve(): every = lax.all_to_all(copies, axis, 0, 0, tiled=False)  18.5 us
    ppermute x1, starting transfers between devices, on_device(): from_right = lax.ppermute(first_cols, 'lat', left_pairs)  8.79 us
    unnamed x24, local copies, waits for them, and re-layouts  4.34 us
    slice x75, local copies, waits for them, and re-layouts, take_rows(): return lax.slice_in_dim(values, start, stop, axis=axis_index)  4.26 us
    add x18, other arithmetic, cyclic_apply(): column + alpha_term * moved(column, stride, axis_index, 0.0, False)  2.67 us
    pallas_call x1, Pallas kernels, depth_local(): pl.pallas_call(depth_kernel, out_shape=(full, full, full, copies))  2.53 us
    ppermute x1, starting transfers between devices, on_device(): lax.ppermute(thermal_state[:, :, width - 1:], 'lat', right_pairs)  1.92 us
  transfers between devices with their start and end apart: 4, of which 3 were waited for; matrix products, arithmetic and copies ran while one was open for 8% of the time, Pallas kernels for 0%

profile of v7, /device:TPU:1, one launch (start us, length us, event | category | flops | bytes accessed | tf_op | source)
XLA Modules:
  0.0 76.6 jit_solution(13647573490066700188)
XLA Ops:
  0.0 1.1 %fusion.73 = (f32[32,8,1]{2,1,0:T(8,128)S(1)}, f32[32,8,1]{2,1,0:T(8,128)S(1)}) fusion(f32[32,8,128]{2,1,0:T(8,128)} %t_ref.1), kind=kLoop, calls=%fused_computation.218 | loop fusion | bytes 4096 | tf_op jit(solution)/shard_map/slice | solution.py:230
  1.2 0.8 %copy-done = f32[32,8,128]{2,1,0:T(8,128)S(1)} copy-done((f32[32,8,128]{2,1,0:T(8,128)S(1)}, f32[32,8,128]{2,1,0:T(8,128)}, u32[]{:S(2)}) %copy-start) | copy-done | bytes 131096
  2.1 0.2 copy.302
  2.3 8.8 %collective-permute-start = (f32[2,32,8,1]{3,2,1,0:T(8,128)S(1)}, f32[2,32,8,1]{3,2,1,0:T(8,128)S(1)}, u32[]{:S(2)}, u32[]{:S(2)}) collective-permute-start(f32[2,32,8,1]{3,2,1,0:T(8,128)S(1)} %copy.302), channel_id=1, source_target_pairs={{1,0},{2,1},{3,2},{4,3},{5,4},{6,5},{7,6},{8,7},{9,8},{10,9},{11,1... | collective-permute-start | bytes 6152 | tf_op jit(solution)/shard_map/ppermute | solution.py:229
  11.1 1.9 %collective-permute-start.1 = (f32[32,8,1]{2,1,0:T(8,128)S(1)}, f32[32,8,1]{2,1,0:T(8,128)S(1)}, u32[]{:S(2)}, u32[]{:S(2)}) collective-permute-start(f32[32,8,1]{2,1,0:T(8,128)S(1)} %get-tuple-element.254), channel_id=1, source_target_pairs={{0,1},{1,2},{2,3},{3,4},{4,5},{5,6},{6,7},{7,8},{8,9},{9,10},{10,1... | collective-permute-start | bytes 3080 | tf_op jit(solution)/shard_map/ppermute | solution.py:230
  13.1 1.9 %collective-permute-done.1.tl_ref = f32[32,8,1]{2,1,0:T(8,128)S(1)} collective-permute-done((f32[32,8,1]{2,1,0:T(8,128)S(1)}, f32[32,8,1]{2,1,0:T(8,128)S(1)}, u32[]{:S(2)}, u32[]{:S(2)}) %collective-permute-start.1) | collective-permute-done | bytes 1056 | tf_op jit(solution)/shard_map/ppermute | solution.py:230
  15.0 0.6 copy-done.6
  15.6 0.7 copy-done.2
  16.3 2.5 %shard_map.37 = (f32[32,8,128]{2,1,0:T(8,128)}, f32[32,8,128]{2,1,0:T(8,128)}, f32[32,8,128]{2,1,0:T(8,128)}, f32[32,6,8,128]{3,2,1,0:T(8,128)}) custom-call(f32[32,8,128]{2,1,0:T(8,128)} %t_ref.1, f32[32,8,128]{2,1,0:T(8,128)} %s_ref.1, f32[32,8,128]{2,1,0:T(8,128)} %d_ref.1, f32[2,32,8,1]{3,2,1,0:T(8,128)} %copy-done.2, f32[32,8,1]{2,1,0:T(8,128)} %copy-done.6), custom_call_target="tpu_custom_call" | custom-call | tf_op jit(solution)/shard_map/pallas_call | solution.py:152
  18.9 6.4 %all-to-all-start = ((f32[32,6,8,128]{3,2,1,0:T(8,128)}), f32[32,6,8,128]{3,2,1,0:T(8,128)S(1)}, u32[]{:S(2)}, u32[]{:S(2)}) async-start(f32[32,6,8,128]{3,2,1,0:T(8,128)} %get-tuple-element.29), calls=%async_computation | async-start | bytes 1572864 | tf_op jit(solution)/shard_map/all_to_all | solution.py:159
  25.5 0.2 copy.334
  26.1 0.2 copy.333
  26.4 0.3 multiply_add_fusion.12
  27.2 0.2 multiply_add_fusion.11
  28.0 0.2 multiply_add_fusion.10
  28.9 0.2 multiply_add_fusion.9
  29.7 0.2 multiply_add_fusion.8
  30.6 0.2 multiply_add_fusion.7
  31.1 0.2 multiply_add_fusion.13
  31.7 0.2 add_divide_fusion.1
  32.0 14.8 %all-to-all-done = f32[32,6,8,128]{3,2,1,0:T(8,128)S(1)} async-done(((f32[32,6,8,128]{3,2,1,0:T(8,128)}), f32[32,6,8,128]{3,2,1,0:T(8,128)S(1)}, u32[]{:S(2)}, u32[]{:S(2)}) %all-to-all-start) | async-done | bytes 786464 | tf_op jit(solution)/shard_map/all_to_all | solution.py:159
  47.1 0.1 multiply_add_fusion.32
  48.2 0.8 %copy-done.4 = f32[32,8,128]{2,1,0:T(8,128)S(1)} copy-done((f32[32,8,128]{2,1,0:T(8,128)S(1)}, f32[32,8,128]{2,1,0:T(8,128)}, u32[]{:S(2)}) %copy-start.4) | copy-done | bytes 131096
  50.6 0.2 slice_multiply_fusion
  51.7 0.8 %reshape.23 = f32[16,1,1536]{2,1,0:T(1,128)} reshape(f32[16,6,1,8,32]{4,3,2,1,0:T(8,128)S(1)} %broadcast_bitcast_fusion) | data formatting | bytes 196608
  52.6 12.1 %all-to-all-start.1 = ((f32[16,1,1536]{2,1,0:T(1,128)}), f32[16,1,1536]{2,1,0:T(1,128)S(1)}, u32[]{:S(2)}, u32[]{:S(2)}) async-start(f32[16,1,1536]{2,1,0:T(1,128)} %reshape.23), calls=%async_computation.1 | async-start | bytes 196608 | tf_op jit(solution)/shard_map/all_to_all | solution.py:159
  64.6 8.5 %all-to-all-done.1 = f32[16,1,1536]{2,1,0:T(1,128)S(1)} async-done(((f32[16,1,1536]{2,1,0:T(1,128)}), f32[16,1,1536]{2,1,0:T(1,128)S(1)}, u32[]{:S(2)}, u32[]{:S(2)}) %all-to-all-start.1) | async-done | bytes 98336 | tf_op jit(solution)/shard_map/all_to_all | solution.py:159
  73.1 0.5 broadcast.370
  73.6 0.9 %reduce = f32[16,1536]{1,0:T(8,128)S(1)} reduce(f32[16,1,1536]{2,1,0:T(1,128)S(1)} %all-to-all-done.1, f32[]{:T(128)} %broadcast.370), dimensions={1}, to_apply=%all_to_all.7.reduce_sub_computation | reduce | bytes 196612 | tf_op jit(solution)/shard_map/all_to_all | solution.py:159
  74.5 0.1 reshape.24
  75.5 0.1 copy.332
  75.8 0.8 pad_maximum_fusion
  (143 shorter events, 8.6 us)
Async XLA Ops:
  1.1 0.9 %copy-start = (f32[32,8,128]{2,1,0:T(8,128)S(1)}, f32[32,8,128]{2,1,0:T(8,128)}, u32[]{:S(2)}) copy-start(f32[32,8,128]{2,1,0:T(8,128)} %s_ref.1) | copy-start | bytes 393220
  2.3 12.7 %collective-permute-start = (f32[2,32,8,1]{3,2,1,0:T(8,128)S(1)}, f32[2,32,8,1]{3,2,1,0:T(8,128)S(1)}, u32[]{:S(2)}, u32[]{:S(2)}) collective-permute-start(f32[2,32,8,1]{3,2,1,0:T(8,128)S(1)} %copy.302), channel_id=1, source_target_pairs={{1,0},{2,1},{3,2},{4,3},{5,4},{6,5},{7,6},{8,7},{9,8},{10,9},{11,1... | collective-permute-start | bytes 6152 | tf_op jit(solution)/shard_map/ppermute | solution.py:229
  11.1 3.9 %collective-permute-start.1 = (f32[32,8,1]{2,1,0:T(8,128)S(1)}, f32[32,8,1]{2,1,0:T(8,128)S(1)}, u32[]{:S(2)}, u32[]{:S(2)}) collective-permute-start(f32[32,8,1]{2,1,0:T(8,128)S(1)} %get-tuple-element.254), channel_id=1, source_target_pairs={{0,1},{1,2},{2,3},{3,4},{4,5},{5,6},{6,7},{7,8},{8,9},{9,10},{10,1... | collective-permute-start | bytes 3080 | tf_op jit(solution)/shard_map/ppermute | solution.py:230
  15.0 0.7 copy-start.6
  15.6 0.7 copy-start.2
  18.9 6.4 %copy-start.1 = (f32[32,8,128]{2,1,0:T(8,128)S(1)}, f32[32,8,128]{2,1,0:T(8,128)}, u32[]{:S(2)}) copy-start(f32[32,8,128]{2,1,0:T(8,128)} %s_ref.1) | copy-start | bytes 393220
  18.9 28.0 %all-to-all-start = ((f32[32,6,8,128]{3,2,1,0:T(8,128)}), f32[32,6,8,128]{3,2,1,0:T(8,128)S(1)}, u32[]{:S(2)}, u32[]{:S(2)}) async-start(f32[32,6,8,128]{3,2,1,0:T(8,128)} %get-tuple-element.29), calls=%async_computation | async-start | bytes 1572864 | tf_op jit(solution)/shard_map/all_to_all | solution.py:159
  48.0 0.9 %copy-start.4 = (f32[32,8,128]{2,1,0:T(8,128)S(1)}, f32[32,8,128]{2,1,0:T(8,128)}, u32[]{:S(2)}) copy-start(f32[32,8,128]{2,1,0:T(8,128)} %get-tuple-element.28) | copy-start | bytes 393220
  48.0 1.0 %copy-start.5 = (f32[32,8,128]{2,1,0:T(8,128)S(1)}, f32[32,8,128]{2,1,0:T(8,128)}, u32[]{:S(2)}) copy-start(f32[32,8,128]{2,1,0:T(8,128)} %get-tuple-element.30) | copy-start | bytes 393220
  48.1 0.9 %copy-start.3 = (f32[32,8,128]{2,1,0:T(8,128)S(1)}, f32[32,8,128]{2,1,0:T(8,128)}, u32[]{:S(2)}) copy-start(f32[32,8,128]{2,1,0:T(8,128)} %get-tuple-element.27) | copy-start | bytes 393220
  52.6 20.6 %all-to-all-start.1 = ((f32[16,1,1536]{2,1,0:T(1,128)}), f32[16,1,1536]{2,1,0:T(1,128)S(1)}, u32[]{:S(2)}, u32[]{:S(2)}) async-start(f32[16,1,1536]{2,1,0:T(1,128)} %reshape.23), calls=%async_computation.1 | async-start | bytes 196608 | tf_op jit(solution)/shard_map/all_to_all | solution.py:159

commit v8 on v7

--- a/solution.py
+++ b/solution.py
@@ -212,8 +212,11 @@
         ]
     )
     blocks = lax.axis_size(axis)
-    copies = jnp.broadcast_to(pieces[None], (blocks,) + pieces.shape)
+    flat = pieces.reshape(pieces.shape[0], -1)
+    copies = jnp.broadcast_to(flat[None], (blocks,) + flat.shape)
     previous, interface_value = reduced_solve(copies, ratio, axis)
+    previous = previous.reshape(pieces.shape[1:])
+    interface_value = interface_value.reshape(pieces.shape[1:])
     inner_values = local_part + prev_part * previous + next_part * interface_value
     return jnp.concatenate([inner_values, interface_value], axis=axis_index)
 

time: 77 us -> 77.1 us (level)
  other arithmetic: 6.65 us -> 5.78 us
    dynamic_slice x0 -> x2, local copies, waits for them, and re-layouts: none -> 1.19 us  [reduced_solve(): interface_value = lax.dynamic_slice_in_dim(padded, index + 1, 1, 0)[0]]
    unnamed x24 -> x21, local copies, waits for them, and re-layouts: 4.34 us -> 3.34 us
    all_to_all x1 -> x0, other arithmetic: 0.87 us -> none  [reduced_solve(): every = lax.all_to_all(copies, axis, 0, 0, tiled=False)]
where the time goes in v8:
time: 77.1 us; the launch traced here: 76.7 us
  starting transfers between devices  29.2 us (38%)
  waiting for transfers between devices  25.9 us (34%)
  local copies, waits for them, and re-layouts  12.2 us (16%)
  other arithmetic  5.78 us (7%)
  Pallas kernels  2.59 us (3%)
  between operations  1.03 us (1%)
    all_to_all x2, waiting for transfers between devices, reduced_solve(): every = lax.all_to_all(copies, axis, 0, 0, tiled=False)  24 us
    all_to_all x2, starting transfers between devices, reduced_solve(): every = lax.all_to_all(copies, axis, 0, 0, tiled=False)  18.5 us
    ppermute x1, starting transfers between devices, on_device(): from_right = lax.ppermute(first_cols, 'lat', left_pairs)  8.79 us
    slice x75, local copies, waits for them, and re-layouts, take_rows(): return lax.slice_in_dim(values, start, stop, axis=axis_index)  4.23 us
    unnamed x21, local copies, waits for them, and re-layouts  3.34 us
    pallas_call x1, Pallas kernels, depth_local(): pl.pallas_call(depth_kernel, out_shape=(full, full, full, copies))  2.59 us
    add x18, other arithmetic, cyclic_apply(): column + alpha_term * moved(column, stride, axis_index, 0.0, False)  2.58 us
    ppermute x1, starting transfers between devices, on_device(): lax.ppermute(thermal_state[:, :, width - 1:], 'lat', right_pairs)  1.92 us
  transfers between devices with their start and end apart: 4, of which 3 were waited for; matrix products, arithmetic and copies ran while one was open for 8% of the time, Pallas kernels for 0%

profile of v8, /device:TPU:1, one launch (start us, length us, event | category | flops | bytes accessed | tf_op | source)
XLA Modules:
  0.0 76.7 jit_solution(16704850146535976390)
XLA Ops:
  0.0 1.1 %fusion.75 = (f32[32,8,1]{2,1,0:T(8,128)S(1)}, f32[32,8,1]{2,1,0:T(8,128)S(1)}) fusion(f32[32,8,128]{2,1,0:T(8,128)} %t_ref.1), kind=kLoop, calls=%fused_computation.214 | loop fusion | bytes 4096 | tf_op jit(solution)/shard_map/slice | solution.py:233
  1.2 0.8 %copy-done = f32[32,8,128]{2,1,0:T(8,128)S(1)} copy-done((f32[32,8,128]{2,1,0:T(8,128)S(1)}, f32[32,8,128]{2,1,0:T(8,128)}, u32[]{:S(2)}) %copy-start) | copy-done | bytes 131096
  2.1 0.2 copy.53
  2.3 8.8 %collective-permute-start = (f32[2,32,8,1]{3,2,1,0:T(8,128)S(1)}, f32[2,32,8,1]{3,2,1,0:T(8,128)S(1)}, u32[]{:S(2)}, u32[]{:S(2)}) collective-permute-start(f32[2,32,8,1]{3,2,1,0:T(8,128)S(1)} %copy.53), channel_id=1, source_target_pairs={{1,0},{2,1},{3,2},{4,3},{5,4},{6,5},{7,6},{8,7},{9,8},{10,9},{11,1... | collective-permute-start | bytes 6152 | tf_op jit(solution)/shard_map/ppermute | solution.py:232
  11.1 1.9 %collective-permute-start.1 = (f32[32,8,1]{2,1,0:T(8,128)S(1)}, f32[32,8,1]{2,1,0:T(8,128)S(1)}, u32[]{:S(2)}, u32[]{:S(2)}) collective-permute-start(f32[32,8,1]{2,1,0:T(8,128)S(1)} %get-tuple-element.255), channel_id=1, source_target_pairs={{0,1},{1,2},{2,3},{3,4},{4,5},{5,6},{6,7},{7,8},{8,9},{9,10},{10,1... | collective-permute-start | bytes 3080 | tf_op jit(solution)/shard_map/ppermute | solution.py:233
  13.1 1.9 %collective-permute-done.1.tl_ref = f32[32,8,1]{2,1,0:T(8,128)S(1)} collective-permute-done((f32[32,8,1]{2,1,0:T(8,128)S(1)}, f32[32,8,1]{2,1,0:T(8,128)S(1)}, u32[]{:S(2)}, u32[]{:S(2)}) %collective-permute-start.1) | collective-permute-done | bytes 1056 | tf_op jit(solution)/shard_map/ppermute | solution.py:233
  15.0 0.6 copy-done.6
  15.6 0.7 copy-done.2
  16.3 2.6 %shard_map.37 = (f32[32,8,128]{2,1,0:T(8,128)}, f32[32,8,128]{2,1,0:T(8,128)}, f32[32,8,128]{2,1,0:T(8,128)}, f32[32,6,8,128]{3,2,1,0:T(8,128)}) custom-call(f32[32,8,128]{2,1,0:T(8,128)} %t_ref.1, f32[32,8,128]{2,1,0:T(8,128)} %s_ref.1, f32[32,8,128]{2,1,0:T(8,128)} %d_ref.1, f32[2,32,8,1]{3,2,1,0:T(8,128)} %copy-done.2, f32[32,8,1]{2,1,0:T(8,128)} %copy-done.6), custom_call_target="tpu_custom_call" | custom-call | tf_op jit(solution)/shard_map/pallas_call | solution.py:152
  18.9 6.4 %all-to-all-start = ((f32[32,6,8,128]{3,2,1,0:T(8,128)}), f32[32,6,8,128]{3,2,1,0:T(8,128)S(1)}, u32[]{:S(2)}, u32[]{:S(2)}) async-start(f32[32,6,8,128]{3,2,1,0:T(8,128)} %get-tuple-element.29), calls=%async_computation | async-start | bytes 1572864 | tf_op jit(solution)/shard_map/all_to_all | solution.py:159
  25.6 0.2 copy.74
  26.2 0.2 copy.73
  26.4 0.3 multiply_add_fusion.11
  27.2 0.2 multiply_add_fusion.10
  28.1 0.2 multiply_add_fusion.9
  29.0 0.2 multiply_add_fusion.8
  29.8 0.2 multiply_add_fusion.7
  30.6 0.2 multiply_add_fusion.6
  31.1 0.2 multiply_add_fusion.12
  31.7 0.2 add_divide_fusion.1
  32.0 14.9 %all-to-all-done = f32[32,6,8,128]{3,2,1,0:T(8,128)S(1)} async-done(((f32[32,6,8,128]{3,2,1,0:T(8,128)}), f32[32,6,8,128]{3,2,1,0:T(8,128)S(1)}, u32[]{:S(2)}, u32[]{:S(2)}) %all-to-all-start) | async-done | bytes 786464 | tf_op jit(solution)/shard_map/all_to_all | solution.py:159
  47.2 0.1 multiply_add_fusion.31
  48.2 0.8 copy-done.4
  50.7 0.5 fusion
  51.7 0.7 broadcast_in_dim.38
  52.4 12.1 %all-to-all-start.1 = ((f32[16,6,256]{2,1,0:T(8,128)}), f32[16,6,256]{2,1,0:T(8,128)S(1)}, u32[]{:S(2)}, u32[]{:S(2)}) async-start(f32[16,6,256]{2,1,0:T(8,128)} %broadcast_in_dim.38), calls=%async_computation.1 | async-start | bytes 262144 | tf_op jit(solution)/shard_map/all_to_all | solution.py:159
  64.5 9.2 %all-to-all-done.1 = f32[16,6,256]{2,1,0:T(8,128)S(1)} async-done(((f32[16,6,256]{2,1,0:T(8,128)}), f32[16,6,256]{2,1,0:T(8,128)S(1)}, u32[]{:S(2)}, u32[]{:S(2)}) %all-to-all-start.1) | async-done | bytes 98336 | tf_op jit(solution)/shard_map/all_to_all | solution.py:159
  74.2 0.5 broadcast.385
  74.7 0.7 fusion.16
  75.5 0.2 reshape_squeeze.5
  75.8 0.1 multiply_add_fusion
  75.9 0.8 pad_maximum_fusion
  (142 shorter events, 8.0 us)
Async XLA Ops:
  1.1 0.9 %copy-start = (f32[32,8,128]{2,1,0:T(8,128)S(1)}, f32[32,8,128]{2,1,0:T(8,128)}, u32[]{:S(2)}) copy-start(f32[32,8,128]{2,1,0:T(8,128)} %s_ref.1) | copy-start | bytes 393220
  2.3 12.7 %collective-permute-start = (f32[2,32,8,1]{3,2,1,0:T(8,128)S(1)}, f32[2,32,8,1]{3,2,1,0:T(8,128)S(1)}, u32[]{:S(2)}, u32[]{:S(2)}) collective-permute-start(f32[2,32,8,1]{3,2,1,0:T(8,128)S(1)} %copy.53), channel_id=1, source_target_pairs={{1,0},{2,1},{3,2},{4,3},{5,4},{6,5},{7,6},{8,7},{9,8},{10,9},{11,1... | collective-permute-start | bytes 6152 | tf_op jit(solution)/shard_map/ppermute | solution.py:232
  11.1 3.9 %collective-permute-start.1 = (f32[32,8,1]{2,1,0:T(8,128)S(1)}, f32[32,8,1]{2,1,0:T(8,128)S(1)}, u32[]{:S(2)}, u32[]{:S(2)}) collective-permute-start(f32[32,8,1]{2,1,0:T(8,128)S(1)} %get-tuple-element.255), channel_id=1, source_target_pairs={{0,1},{1,2},{2,3},{3,4},{4,5},{5,6},{6,7},{7,8},{8,9},{9,10},{10,1... | collective-permute-start | bytes 3080 | tf_op jit(solution)/shard_map/ppermute | solution.py:233
  15.0 0.7 copy-start.6
  15.6 0.7 copy-start.2
  18.9 6.4 %copy-start.1 = (f32[32,8,128]{2,1,0:T(8,128)S(1)}, f32[32,8,128]{2,1,0:T(8,128)}, u32[]{:S(2)}) copy-start(f32[32,8,128]{2,1,0:T(8,128)} %s_ref.1) | copy-start | bytes 393220
  18.9 28.0 %all-to-all-start = ((f32[32,6,8,128]{3,2,1,0:T(8,128)}), f32[32,6,8,128]{3,2,1,0:T(8,128)S(1)}, u32[]{:S(2)}, u32[]{:S(2)}) async-start(f32[32,6,8,128]{3,2,1,0:T(8,128)} %get-tuple-element.29), calls=%async_computation | async-start | bytes 1572864 | tf_op jit(solution)/shard_map/all_to_all | solution.py:159
  48.1 0.9 %copy-start.4 = (f32[32,8,128]{2,1,0:T(8,128)S(1)}, f32[32,8,128]{2,1,0:T(8,128)}, u32[]{:S(2)}) copy-start(f32[32,8,128]{2,1,0:T(8,128)} %get-tuple-element.28) | copy-start | bytes 393220
  48.1 1.0 %copy-start.5 = (f32[32,8,128]{2,1,0:T(8,128)S(1)}, f32[32,8,128]{2,1,0:T(8,128)}, u32[]{:S(2)}) copy-start(f32[32,8,128]{2,1,0:T(8,128)} %get-tuple-element.30) | copy-start | bytes 393220
  48.2 0.9 %copy-start.3 = (f32[32,8,128]{2,1,0:T(8,128)S(1)}, f32[32,8,128]{2,1,0:T(8,128)}, u32[]{:S(2)}) copy-start(f32[32,8,128]{2,1,0:T(8,128)} %get-tuple-element.27) | copy-start | bytes 393220
  52.4 21.3 %all-to-all-start.1 = ((f32[16,6,256]{2,1,0:T(8,128)}), f32[16,6,256]{2,1,0:T(8,128)S(1)}, u32[]{:S(2)}, u32[]{:S(2)}) async-start(f32[16,6,256]{2,1,0:T(8,128)} %broadcast_in_dim.38), calls=%async_computation.1 | async-start | bytes 262144 | tf_op jit(solution)/shard_map/all_to_all | solution.py:159

commit v9 on v8

--- a/solution.py
+++ b/solution.py
@@ -76,7 +76,47 @@
     return tuple(cyclic_apply(factors, column, axis_index) for column in rights)
 
 
-def depth_kernel(t_ref, s_ref, d_ref, right_ref, tl_ref, base_ref, p_ref, n_ref, pieces_ref):
+def depth_factor_kernel(d_ref, den_ref, c_ref, p_ref, n_ref, fixed_ref):
+    rows = d_ref.shape[0]
+    inner = rows - 1
+    lower = [-ratio_z * d_ref[i] for i in range(rows)]
+    upper = [lower[i + 1] for i in range(inner)]
+    c_term, r_prev = [], []
+    r_next = None
+    for i in range(inner):
+        diagonal = 1.0 - lower[i] - upper[i]
+        if i == 0:
+            den = diagonal
+            prev = -lower[i] / den
+        else:
+            den = diagonal - lower[i] * c_term[i - 1]
+            prev = (-lower[i] * r_prev[i - 1]) / den
+        den_ref[i] = den
+        if i < inner - 1:
+            c_term.append(upper[i] / den)
+            c_ref[i] = c_term[i]
+        else:
+            c_term.append(None)
+            r_next = -upper[i] / den
+        r_prev.append(prev)
+    prev = r_prev[inner - 1]
+    nxt = r_next
+    lower_last = lower[rows - 1]
+    fixed_ref[0] = lower_last * prev
+    fixed_ref[1] = 1.0 - lower_last + lower_last * nxt
+    p_ref[rows - 1] = jnp.zeros_like(prev)
+    n_ref[rows - 1] = jnp.full_like(prev, 2.0)
+    for i in range(inner - 1, -1, -1):
+        if i < inner - 1:
+            prev = r_prev[i] - c_term[i] * prev
+            nxt = -c_term[i] * nxt
+        p_ref[i] = 2.0 * prev
+        n_ref[i] = 2.0 * nxt
+    fixed_ref[2] = lower[0] * (prev - 1.0)
+    fixed_ref[3] = lower[0] * nxt
+
+
+def depth_kernel(t_ref, s_ref, d_ref, right_ref, tl_ref, den_ref, c_ref, fixed_ref, base_ref, pieces_ref):
     rows, _, width = t_ref.shape
     temp = t_ref[...]
     conduct = s_ref[...]
@@ -90,55 +130,30 @@
         conduct_right * (temp_right - temp) - conduct * (temp - temp_left)
     )
     inner = rows - 1
-    lower = [-ratio_z * d_ref[i] for i in range(rows)]
-    upper = [lower[i + 1] for i in range(inner)]
-    c_term, r_local, r_prev = [], [], []
-    r_next = None
+    r_local = []
     for i in range(inner):
-        diagonal = 1.0 - lower[i] - upper[i]
         rhs = base_ref[i]
         if i == 0:
-            den = diagonal
-            local = rhs / den
-            prev = -lower[i] / den
+            local = rhs / den_ref[i]
         else:
-            den = diagonal - lower[i] * c_term[i - 1]
-            local = (rhs - lower[i] * r_local[i - 1]) / den
-            prev = (-lower[i] * r_prev[i - 1]) / den
-        if i < inner - 1:
-            c_term.append(upper[i] / den)
-        else:
-            c_term.append(None)
-            r_next = -upper[i] / den
+            local = (rhs - (-ratio_z * d_ref[i]) * r_local[i - 1]) / den_ref[i]
         r_local.append(local)
-        r_prev.append(prev)
     local = r_local[inner - 1]
-    prev = r_prev[inner - 1]
-    nxt = r_next
-    lower_last = lower[rows - 1]
+    lower_last = -ratio_z * d_ref[rows - 1]
     right_last = base_ref[rows - 1]
-    own_lower = lower_last * prev
-    own_diag = 1.0 - lower_last + lower_last * nxt
     own_right = right_last - lower_last * local
     base_ref[rows - 1] = -right_last
-    p_ref[rows - 1] = jnp.zeros_like(local)
-    n_ref[rows - 1] = jnp.full_like(local, 2.0)
     for i in range(inner - 1, -1, -1):
         if i < inner - 1:
-            local = r_local[i] - c_term[i] * local
-            prev = r_prev[i] - c_term[i] * prev
-            nxt = -c_term[i] * nxt
+            local = r_local[i] - c_ref[i] * local
         base_ref[i] = 2.0 * local - base_ref[i]
-        p_ref[i] = 2.0 * prev
-        n_ref[i] = 2.0 * nxt
-    head_coupling = lower[0]
     own = (
-        own_lower,
-        own_diag,
+        fixed_ref[0],
+        fixed_ref[1],
         own_right,
-        head_coupling * (prev - 1.0),
-        head_coupling * nxt,
-        head_coupling * local,
+        fixed_ref[2],
+        fixed_ref[3],
+        (-ratio_z * d_ref[0]) * local,
     )
     for block in range(pieces_ref.shape[0]):
         for i in range(6):
@@ -148,10 +163,16 @@
 def depth_local(temp, conduct, downward, from_right, temp_prev, blocks):
     rows, lines, width = temp.shape
     full = jax.ShapeDtypeStruct(temp.shape, temp.dtype)
+    inner = jax.ShapeDtypeStruct((rows - 1, lines, width), temp.dtype)
+    den, c_term, prev_weight, own_weight, fixed = pl.pallas_call(
+        depth_factor_kernel,
+        out_shape=(inner, inner, full, full, jax.ShapeDtypeStruct((4, lines, width), temp.dtype)),
+    )(downward)
     copies = jax.ShapeDtypeStruct((blocks, 6, lines, width), temp.dtype)
-    return pl.pallas_call(depth_kernel, out_shape=(full, full, full, copies))(
-        temp, conduct, downward, from_right, temp_prev
-    )
+    base, pieces = pl.pallas_call(depth_kernel, out_shape=(full, copies))(
+        temp, conduct, downward, from_right, temp_prev, den, c_term, fixed
+    )
+    return base, prev_weight, own_weight, pieces
 
 
 def reduced_solve(copies, ratio, axis):

time: 77.1 us -> 76.6 us (level)
  Pallas kernels: 2.59 us -> 4.53 us
  waiting for transfers between devices: 25.9 us -> 24.3 us
    pallas_call x1 -> x2, Pallas kernels: 2.59 us -> 4.53 us  [the longest x1 2.57 us: depth_local(): pl.pallas_call(depth_kernel, out_shape=(full, copies))]
    ppermute x1, waiting for transfers between devices: 1.9 us -> 0.01 us  [on_device(): lax.ppermute(thermal_state[:, :, width - 1:], 'lat', right_pairs)]
  transfers between devices with their start and end apart: 4 -> 4, of which waited for: 3 -> 2; matrix products, arithmetic and copies ran while one was open for 8% -> 8% of each run, Pallas kernels for 0% -> 3%
where the time goes in v9:
time: 76.6 us; the launch traced here: 76.2 us
  starting transfers between devices  29 us (38%)
  waiting for transfers between devices  24.3 us (32%)
  local copies, waits for them, and re-layouts  11.5 us (15%)
  other arithmetic  5.8 us (8%)
  Pallas kernels  4.53 us (6%)
  between operations  1.02 us (1%)
    all_to_all x2, waiting for transfers between devices, reduced_solve(): every = lax.all_to_all(copies, axis, 0, 0, tiled=False)  24.3 us
    all_to_all x2, starting transfers between devices, reduced_solve(): every = lax.all_to_all(copies, axis, 0, 0, tiled=False)  18.3 us
    ppermute x1, starting transfers between devices, on_device(): from_right = lax.ppermute(first_cols, 'lat', left_pairs)  8.79 us
    slice x75, local copies, waits for them, and re-layouts, take_rows(): return lax.slice_in_dim(values, start, stop, axis=axis_index)  4.23 us
    unnamed x21, local copies, waits for them, and re-layouts  2.71 us
    add x18, other arithmetic, cyclic_apply(): column + alpha_term * moved(column, stride, axis_index, 0.0, False)  2.58 us
    pallas_call x1, Pallas kernels, depth_local(): pl.pallas_call(depth_kernel, out_shape=(full, copies))  2.57 us
    pallas_call x1, Pallas kernels, depth_local(): pl.pallas_call(depth_factor_kernel, out_shape=(inner, inner, full, full,...  1.96 us
  transfers between devices with their start and end apart: 4, of which 2 were waited for; matrix products, arithmetic and copies ran while one was open for 8% of the time, Pallas kernels for 3%

profile of v9, /device:TPU:1, one launch (start us, length us, event | category | flops | bytes accessed | tf_op | source)
XLA Modules:
  0.0 76.2 jit_solution(16554203685849598750)
XLA Ops:
  0.0 1.1 %fusion.75 = (f32[32,8,1]{2,1,0:T(8,128)S(1)}, f32[32,8,1]{2,1,0:T(8,128)S(1)}) fusion(f32[32,8,128]{2,1,0:T(8,128)} %t_ref.1), kind=kLoop, calls=%fused_computation.214 | loop fusion | bytes 4096 | tf_op jit(solution)/shard_map/slice | solution.py:254
  1.2 0.8 %copy-done = f32[32,8,128]{2,1,0:T(8,128)S(1)} copy-done((f32[32,8,128]{2,1,0:T(8,128)S(1)}, f32[32,8,128]{2,1,0:T(8,128)}, u32[]{:S(2)}) %copy-start) | copy-done | bytes 131096
  2.1 0.2 copy.53
  2.3 8.8 %collective-permute-start = (f32[2,32,8,1]{3,2,1,0:T(8,128)S(1)}, f32[2,32,8,1]{3,2,1,0:T(8,128)S(1)}, u32[]{:S(2)}, u32[]{:S(2)}) collective-permute-start(f32[2,32,8,1]{3,2,1,0:T(8,128)S(1)} %copy.53), channel_id=1, source_target_pairs={{1,0},{2,1},{3,2},{4,3},{5,4},{6,5},{7,6},{8,7},{9,8},{10,9},{11,1... | collective-permute-start | bytes 6152 | tf_op jit(solution)/shard_map/ppermute | solution.py:253
  11.1 1.9 %collective-permute-start.1 = (f32[32,8,1]{2,1,0:T(8,128)S(1)}, f32[32,8,1]{2,1,0:T(8,128)S(1)}, u32[]{:S(2)}, u32[]{:S(2)}) collective-permute-start(f32[32,8,1]{2,1,0:T(8,128)S(1)} %get-tuple-element.261), channel_id=1, source_target_pairs={{0,1},{1,2},{2,3},{3,4},{4,5},{5,6},{6,7},{7,8},{8,9},{9,10},{10,1... | collective-permute-start | bytes 3080 | tf_op jit(solution)/shard_map/ppermute | solution.py:254
  13.1 2.0 %shard_map.37 = (f32[31,8,128]{2,1,0:T(8,128)}, f32[31,8,128]{2,1,0:T(8,128)}, f32[32,8,128]{2,1,0:T(8,128)}, f32[32,8,128]{2,1,0:T(8,128)}, f32[4,8,128]{2,1,0:T(8,128)}) custom-call(f32[32,8,128]{2,1,0:T(8,128)} %d_ref.3), custom_call_target="tpu_custom_call" | custom-call | tf_op jit(solution)/shard_map/pallas_call | solution.py:167
  15.1 0.6 copy-done.6
  15.8 2.6 %shard_map.38 = (f32[32,8,128]{2,1,0:T(8,128)}, f32[32,6,8,128]{3,2,1,0:T(8,128)}) custom-call(f32[32,8,128]{2,1,0:T(8,128)} %t_ref.1, f32[32,8,128]{2,1,0:T(8,128)} %s_ref.1, f32[32,8,128]{2,1,0:T(8,128)} %d_ref.3, f32[2,32,8,1]{3,2,1,0:T(8,128)} %copy-done.2, f32[32,8,1]{2,1,0:T(8,128)} %copy-done.6, f32[31,8,128]{2,1,0:T(8,128)} %get-tuple-element.30.den_ref, ...), custom_call_target="tpu_custom_call" | custom-call | tf_op jit(solution)/shard_map/pallas_call | solution.py:172
  18.4 6.5 %all-to-all-start = ((f32[32,6,8,128]{3,2,1,0:T(8,128)}), f32[32,6,8,128]{3,2,1,0:T(8,128)S(1)}, u32[]{:S(2)}, u32[]{:S(2)}) async-start(f32[32,6,8,128]{3,2,1,0:T(8,128)} %get-tuple-element.35), calls=%async_computation | async-start | bytes 1572864 | tf_op jit(solution)/shard_map/all_to_all | solution.py:180
  25.1 0.2 copy.74
  25.7 0.2 copy.73
  25.9 0.3 multiply_add_fusion.11
  26.3 0.1 fusion.48
  26.8 0.2 multiply_add_fusion.10
  27.6 0.2 multiply_add_fusion.9
  28.5 0.2 multiply_add_fusion.8
  29.3 0.2 multiply_add_fusion.7
  30.1 0.2 multiply_add_fusion.6
  30.7 0.2 multiply_add_fusion.12
  31.3 0.2 add_divide_fusion.1
  31.6 15.1 %all-to-all-done = f32[32,6,8,128]{3,2,1,0:T(8,128)S(1)} async-done(((f32[32,6,8,128]{3,2,1,0:T(8,128)}), f32[32,6,8,128]{3,2,1,0:T(8,128)S(1)}, u32[]{:S(2)}, u32[]{:S(2)}) %all-to-all-start) | async-done | bytes 786464 | tf_op jit(solution)/shard_map/all_to_all | solution.py:180
  47.0 0.1 multiply_add_fusion.31
  48.0 0.8 %copy-done.4 = f32[32,8,128]{2,1,0:T(8,128)S(1)} copy-done((f32[32,8,128]{2,1,0:T(8,128)S(1)}, f32[32,8,128]{2,1,0:T(8,128)}, u32[]{:S(2)}) %copy-start.4) | copy-done | bytes 131096
  50.5 0.5 fusion
  51.5 0.7 broadcast_in_dim.38
  52.2 11.8 %all-to-all-start.1 = ((f32[16,6,256]{2,1,0:T(8,128)}), f32[16,6,256]{2,1,0:T(8,128)S(1)}, u32[]{:S(2)}, u32[]{:S(2)}) async-start(f32[16,6,256]{2,1,0:T(8,128)} %broadcast_in_dim.38), calls=%async_computation.1 | async-start | bytes 262144 | tf_op jit(solution)/shard_map/all_to_all | solution.py:180
  64.0 9.2 %all-to-all-done.1 = f32[16,6,256]{2,1,0:T(8,128)S(1)} async-done(((f32[16,6,256]{2,1,0:T(8,128)}), f32[16,6,256]{2,1,0:T(8,128)S(1)}, u32[]{:S(2)}, u32[]{:S(2)}) %all-to-all-start.1) | async-done | bytes 98336 | tf_op jit(solution)/shard_map/all_to_all | solution.py:180
  73.7 0.5 broadcast.385
  74.2 0.7 fusion.16
  75.1 0.2 reshape_squeeze.5
  75.3 0.1 multiply_add_fusion
  75.4 0.8 pad_maximum_fusion
  (143 shorter events, 8.0 us)
Async XLA Ops:
  1.1 0.9 %copy-start = (f32[32,8,128]{2,1,0:T(8,128)S(1)}, f32[32,8,128]{2,1,0:T(8,128)}, u32[]{:S(2)}) copy-start(f32[32,8,128]{2,1,0:T(8,128)} %s_ref.1) | copy-start | bytes 393220
  2.3 12.7 %collective-permute-start = (f32[2,32,8,1]{3,2,1,0:T(8,128)S(1)}, f32[2,32,8,1]{3,2,1,0:T(8,128)S(1)}, u32[]{:S(2)}, u32[]{:S(2)}) collective-permute-start(f32[2,32,8,1]{3,2,1,0:T(8,128)S(1)} %copy.53), channel_id=1, source_target_pairs={{1,0},{2,1},{3,2},{4,3},{5,4},{6,5},{7,6},{8,7},{9,8},{10,9},{11,1... | collective-permute-start | bytes 6152 | tf_op jit(solution)/shard_map/ppermute | solution.py:253
  11.1 3.9 %collective-permute-start.1 = (f32[32,8,1]{2,1,0:T(8,128)S(1)}, f32[32,8,1]{2,1,0:T(8,128)S(1)}, u32[]{:S(2)}, u32[]{:S(2)}) collective-permute-start(f32[32,8,1]{2,1,0:T(8,128)S(1)} %get-tuple-element.261), channel_id=1, source_target_pairs={{0,1},{1,2},{2,3},{3,4},{4,5},{5,6},{6,7},{7,8},{8,9},{9,10},{10,1... | collective-permute-start | bytes 3080 | tf_op jit(solution)/shard_map/ppermute | solution.py:254
  15.0 0.6 copy-start.6
  15.0 0.8 copy-start.2
  18.4 6.5 %copy-start.1 = (f32[32,8,128]{2,1,0:T(8,128)S(1)}, f32[32,8,128]{2,1,0:T(8,128)}, u32[]{:S(2)}) copy-start(f32[32,8,128]{2,1,0:T(8,128)} %s_ref.1) | copy-start | bytes 393220
  18.4 28.3 %all-to-all-start = ((f32[32,6,8,128]{3,2,1,0:T(8,128)}), f32[32,6,8,128]{3,2,1,0:T(8,128)S(1)}, u32[]{:S(2)}, u32[]{:S(2)}) async-start(f32[32,6,8,128]{3,2,1,0:T(8,128)} %get-tuple-element.35), calls=%async_computation | async-start | bytes 1572864 | tf_op jit(solution)/shard_map/all_to_all | solution.py:180
  47.9 0.9 %copy-start.4 = (f32[32,8,128]{2,1,0:T(8,128)S(1)}, f32[32,8,128]{2,1,0:T(8,128)}, u32[]{:S(2)}) copy-start(f32[32,8,128]{2,1,0:T(8,128)} %get-tuple-element.36) | copy-start | bytes 393220
  47.9 1.0 %copy-start.5 = (f32[32,8,128]{2,1,0:T(8,128)S(1)}, f32[32,8,128]{2,1,0:T(8,128)}, u32[]{:S(2)}) copy-start(f32[32,8,128]{2,1,0:T(8,128)} %get-tuple-element.33) | copy-start | bytes 393220
  48.0 1.0 %copy-start.3 = (f32[32,8,128]{2,1,0:T(8,128)S(1)}, f32[32,8,128]{2,1,0:T(8,128)}, u32[]{:S(2)}) copy-start(f32[32,8,128]{2,1,0:T(8,128)} %get-tuple-element.34) | copy-start | bytes 393220
  52.2 21.0 %all-to-all-start.1 = ((f32[16,6,256]{2,1,0:T(8,128)}), f32[16,6,256]{2,1,0:T(8,128)S(1)}, u32[]{:S(2)}, u32[]{:S(2)}) async-start(f32[16,6,256]{2,1,0:T(8,128)} %broadcast_in_dim.38), calls=%async_computation.1 | async-start | bytes 262144 | tf_op jit(solution)/shard_map/all_to_all | solution.py:180

commit v10 on v9

--- a/solution.py
+++ b/solution.py
@@ -247,11 +247,13 @@
     count = lax.axis_size("lat")
     right_pairs = [(i, i + 1) for i in range(count - 1)]
     left_pairs = [(i + 1, i) for i in range(count - 1)]
+    edge_shape = thermal_state.shape[:2] + (1,)
     first_cols = jnp.stack(
-        [thermal_state[:, :, :1], sideways_face_flux_factor[:, :, :1]]
-    )
-    from_right = lax.ppermute(first_cols, "lat", left_pairs)
-    from_left = lax.ppermute(thermal_state[:, :, width - 1 :], "lat", right_pairs)
+        [thermal_state[:, :, 0].reshape(-1), sideways_face_flux_factor[:, :, 0].reshape(-1)]
+    )
+    from_right = lax.ppermute(first_cols, "lat", left_pairs).reshape((2,) + edge_shape)
+    last_col = thermal_state[:, :, width - 1].reshape(-1)
+    from_left = lax.ppermute(last_col, "lat", right_pairs).reshape(edge_shape)
     base, prev_weight, own_weight, pieces = depth_local(
         thermal_state,
         sideways_face_flux_factor,

time: 76.6 us -> 76.5 us (level)
    reshape x0 -> x2, local copies, waits for them, and re-layouts: none -> 1.79 us  [the longest x1 0.92 us: on_device(): lax.ppermute(first_cols, 'lat', left_pairs).reshape((2,) + edge_shape)]
    unnamed x21 -> x15, local copies, waits for them, and re-layouts: 2.71 us -> 0.95 us
  transfers between devices with their start and end apart: 4 -> 4, of which waited for: 2 -> 2; matrix products, arithmetic and copies ran while one was open for 8% -> 10% of each run, Pallas kernels for 3% -> 3%
where the time goes in v10:
time: 76.5 us; the launch traced here: 76.1 us
  starting transfers between devices  28.6 us (37%)
  waiting for transfers between devices  24.3 us (32%)
  local copies, waits for them, and re-layouts  11.9 us (16%)
  other arithmetic  5.8 us (8%)
  Pallas kernels  4.55 us (6%)
  between operations  1.02 us (1%)
    all_to_all x2, waiting for transfers between devices, reduced_solve(): every = lax.all_to_all(copies, axis, 0, 0, tiled=False)  24.3 us
    all_to_all x2, starting transfers between devices, reduced_solve(): every = lax.all_to_all(copies, axis, 0, 0, tiled=False)  17.9 us
    ppermute x1, starting transfers between devices, on_device(): lax.ppermute(first_cols, 'lat', left_pairs).reshape((2,) + edge_shape)  8.79 us
    slice x75, local copies, waits for them, and re-layouts, take_rows(): return lax.slice_in_dim(values, start, stop, axis=axis_index)  4.23 us
    pallas_call x1, Pallas kernels, depth_local(): pl.pallas_call(depth_kernel, out_shape=(full, copies))  2.59 us
    add x18, other arithmetic, cyclic_apply(): column + alpha_term * moved(column, stride, axis_index, 0.0, False)  2.58 us
    pallas_call x1, Pallas kernels, depth_local(): pl.pallas_call(depth_factor_kernel, out_shape=(inner, inner, full, full,...  1.96 us
    ppermute x1, starting transfers between devices, on_device(): from_left = lax.ppermute(last_col, 'lat', right_pairs).reshape(edge_shape)  1.92 us
  transfers between devices with their start and end apart: 4, of which 2 were waited for; matrix products, arithmetic and copies ran while one was open for 10% of the time, Pallas kernels for 3%

profile of v10, /device:TPU:1, one launch (start us, length us, event | category | flops | bytes accessed | tf_op | source)
XLA Modules:
  0.0 76.1 jit_solution(11980698847140019204)
XLA Ops:
  0.0 1.2 %slice_reduce_fusion = (f32[32,8]{1,0:T(8,128)S(1)}, f32[32,8]{1,0:T(8,128)S(1)}) fusion(f32[32,8,128]{2,1,0:T(8,128)} %t_ref.1), kind=kLoop, calls=%fused_computation.102 | loop fusion | bytes 4096 | tf_op jit(solution)/shard_map/slice | solution.py:255
  1.5 8.8 %collective-permute-start = (f32[2,256]{1,0:T(2,128)S(1)}, f32[2,256]{1,0:T(2,128)S(1)}, u32[]{:S(2)}, u32[]{:S(2)}) collective-permute-start(f32[2,256]{1,0:T(2,128)S(1)} %pad_maximum_fusion.1), channel_id=1, source_target_pairs={{1,0},{2,1},{3,2},{4,3},{5,4},{6,5},{7,6},{8,7},{9,8},{10,9},{11,1... | collective-permute-start | bytes 6152 | tf_op jit(solution)/shard_map/ppermute | solution.py:254
  10.4 1.9 %collective-permute-start.1 = (f32[256]{0:T(256)S(1)}, f32[256]{0:T(256)S(1)}, u32[]{:S(2)}, u32[]{:S(2)}) collective-permute-start(f32[256]{0:T(256)S(1)} %reshape_squeeze.7), channel_id=1, source_target_pairs={{0,1},{1,2},{2,3},{3,4},{4,5},{5,6},{6,7},{7,8},{8,9},{9,10},{10,1... | collective-permute-start | bytes 3080 | tf_op jit(solution)/shard_map/ppermute | solution.py:256
  12.4 2.0 %shard_map.37 = (f32[31,8,128]{2,1,0:T(8,128)}, f32[31,8,128]{2,1,0:T(8,128)}, f32[32,8,128]{2,1,0:T(8,128)}, f32[32,8,128]{2,1,0:T(8,128)}, f32[4,8,128]{2,1,0:T(8,128)}) custom-call(f32[32,8,128]{2,1,0:T(8,128)} %d_ref.3), custom_call_target="tpu_custom_call" | custom-call | tf_op jit(solution)/shard_map/pallas_call | solution.py:167
  14.3 0.9 %reshape.29.tl_ref = f32[32,8,1]{2,1,0:T(8,128)} reshape(f32[256]{0:T(256)S(1)} %collective-permute-done.1) | data formatting | bytes 2048 | tf_op jit(solution)/shard_map/reshape | solution.py:256
  15.2 0.9 %reshape.28.right_ref = f32[2,32,8,1]{3,2,1,0:T(8,128)} reshape(f32[2,256]{1,0:T(2,128)S(1)} %collective-permute-done) | data formatting | bytes 4096 | tf_op jit(solution)/shard_map/reshape | solution.py:254
  16.1 2.6 %shard_map.38 = (f32[32,8,128]{2,1,0:T(8,128)}, f32[32,6,8,128]{3,2,1,0:T(8,128)}) custom-call(f32[32,8,128]{2,1,0:T(8,128)} %t_ref.1, f32[32,8,128]{2,1,0:T(8,128)} %s_ref.1, f32[32,8,128]{2,1,0:T(8,128)} %d_ref.3, f32[2,32,8,1]{3,2,1,0:T(8,128)} %reshape.28.right_ref, f32[32,8,1]{2,1,0:T(8,128)} %reshape.29.tl_ref, ...), custom_call_target="tpu_custom_call" | custom-call | tf_op jit(solution)/shard_map/pallas_call | solution.py:172
  18.7 6.4 %all-to-all-start = ((f32[32,6,8,128]{3,2,1,0:T(8,128)}), f32[32,6,8,128]{3,2,1,0:T(8,128)S(1)}, u32[]{:S(2)}, u32[]{:S(2)}) async-start(f32[32,6,8,128]{3,2,1,0:T(8,128)} %get-tuple-element.35), calls=%async_computation | async-start | bytes 1572864 | tf_op jit(solution)/shard_map/all_to_all | solution.py:180
  25.4 0.2 copy.68
  25.7 0.1 broadcast_select_fusion
  26.0 0.2 copy.67
  26.2 0.3 multiply_add_fusion.11
  26.6 0.1 fusion.48
  27.0 0.2 multiply_add_fusion.10
  27.9 0.2 multiply_add_fusion.9
  28.8 0.2 multiply_add_fusion.8
  29.6 0.2 multiply_add_fusion.7
  30.4 0.2 multiply_add_fusion.6
  31.0 0.2 multiply_add_fusion.12
  31.5 0.2 add_divide_fusion.1
  31.8 15.1 %all-to-all-done = f32[32,6,8,128]{3,2,1,0:T(8,128)S(1)} async-done(((f32[32,6,8,128]{3,2,1,0:T(8,128)}), f32[32,6,8,128]{3,2,1,0:T(8,128)S(1)}, u32[]{:S(2)}, u32[]{:S(2)}) %all-to-all-start) | async-done | bytes 786464 | tf_op jit(solution)/shard_map/all_to_all | solution.py:180
  47.3 0.1 multiply_add_fusion.31
  48.3 0.8 %copy-done.3 = f32[32,8,128]{2,1,0:T(8,128)S(1)} copy-done((f32[32,8,128]{2,1,0:T(8,128)S(1)}, f32[32,8,128]{2,1,0:T(8,128)}, u32[]{:S(2)}) %copy-start.3) | copy-done | bytes 131096
  50.8 0.5 fusion
  51.8 0.7 broadcast_in_dim.38
  52.5 11.5 %all-to-all-start.1 = ((f32[16,6,256]{2,1,0:T(8,128)}), f32[16,6,256]{2,1,0:T(8,128)S(1)}, u32[]{:S(2)}, u32[]{:S(2)}) async-start(f32[16,6,256]{2,1,0:T(8,128)} %broadcast_in_dim.38), calls=%async_computation.1 | async-start | bytes 262144 | tf_op jit(solution)/shard_map/all_to_all | solution.py:180
  63.9 9.2 %all-to-all-done.1 = f32[16,6,256]{2,1,0:T(8,128)S(1)} async-done(((f32[16,6,256]{2,1,0:T(8,128)}), f32[16,6,256]{2,1,0:T(8,128)S(1)}, u32[]{:S(2)}, u32[]{:S(2)}) %all-to-all-start.1) | async-done | bytes 98336 | tf_op jit(solution)/shard_map/all_to_all | solution.py:180
  73.7 0.5 broadcast.388
  74.2 0.7 fusion.16
  75.0 0.2 reshape_squeeze.9
  75.2 0.1 multiply_add_fusion
  75.4 0.8 pad_maximum_fusion
  (142 shorter events, 7.9 us)
Async XLA Ops:
  0.0 1.3 %copy-start = (f32[32,8,128]{2,1,0:T(8,128)S(1)}, f32[32,8,128]{2,1,0:T(8,128)}, u32[]{:S(2)}) copy-start(f32[32,8,128]{2,1,0:T(8,128)} %s_ref.1) | copy-start | bytes 393220
  1.5 13.7 %collective-permute-start = (f32[2,256]{1,0:T(2,128)S(1)}, f32[2,256]{1,0:T(2,128)S(1)}, u32[]{:S(2)}, u32[]{:S(2)}) collective-permute-start(f32[2,256]{1,0:T(2,128)S(1)} %pad_maximum_fusion.1), channel_id=1, source_target_pairs={{1,0},{2,1},{3,2},{4,3},{5,4},{6,5},{7,6},{8,7},{9,8},{10,9},{11,1... | collective-permute-start | bytes 6152 | tf_op jit(solution)/shard_map/ppermute | solution.py:254
  10.4 3.9 %collective-permute-start.1 = (f32[256]{0:T(256)S(1)}, f32[256]{0:T(256)S(1)}, u32[]{:S(2)}, u32[]{:S(2)}) collective-permute-start(f32[256]{0:T(256)S(1)} %reshape_squeeze.7), channel_id=1, source_target_pairs={{0,1},{1,2},{2,3},{3,4},{4,5},{5,6},{6,7},{7,8},{8,9},{9,10},{10,1... | collective-permute-start | bytes 3080 | tf_op jit(solution)/shard_map/ppermute | solution.py:256
  18.7 6.4 %copy-start.1 = (f32[32,8,128]{2,1,0:T(8,128)S(1)}, f32[32,8,128]{2,1,0:T(8,128)}, u32[]{:S(2)}) copy-start(f32[32,8,128]{2,1,0:T(8,128)} %s_ref.1) | copy-start | bytes 393220
  18.7 28.3 %all-to-all-start = ((f32[32,6,8,128]{3,2,1,0:T(8,128)}), f32[32,6,8,128]{3,2,1,0:T(8,128)S(1)}, u32[]{:S(2)}, u32[]{:S(2)}) async-start(f32[32,6,8,128]{3,2,1,0:T(8,128)} %get-tuple-element.35), calls=%async_computation | async-start | bytes 1572864 | tf_op jit(solution)/shard_map/all_to_all | solution.py:180
  48.2 0.9 %copy-start.3 = (f32[32,8,128]{2,1,0:T(8,128)S(1)}, f32[32,8,128]{2,1,0:T(8,128)}, u32[]{:S(2)}) copy-start(f32[32,8,128]{2,1,0:T(8,128)} %get-tuple-element.36) | copy-start | bytes 393220
  48.2 1.0 %copy-start.4 = (f32[32,8,128]{2,1,0:T(8,128)S(1)}, f32[32,8,128]{2,1,0:T(8,128)}, u32[]{:S(2)}) copy-start(f32[32,8,128]{2,1,0:T(8,128)} %get-tuple-element.33) | copy-start | bytes 393220
  48.3 1.0 %copy-start.2 = (f32[32,8,128]{2,1,0:T(8,128)S(1)}, f32[32,8,128]{2,1,0:T(8,128)}, u32[]{:S(2)}) copy-start(f32[32,8,128]{2,1,0:T(8,128)} %get-tuple-element.34) | copy-start | bytes 393220
  52.5 20.6 %all-to-all-start.1 = ((f32[16,6,256]{2,1,0:T(8,128)}), f32[16,6,256]{2,1,0:T(8,128)S(1)}, u32[]{:S(2)}, u32[]{:S(2)}) async-start(f32[16,6,256]{2,1,0:T(8,128)} %broadcast_in_dim.38), calls=%async_computation.1 | async-start | bytes 262144 | tf_op jit(solution)/shard_map/all_to_all | solution.py:180

commit v11 on v8

--- a/solution.py
+++ b/solution.py
@@ -226,11 +226,13 @@
     count = lax.axis_size("lat")
     right_pairs = [(i, i + 1) for i in range(count - 1)]
     left_pairs = [(i + 1, i) for i in range(count - 1)]
+    edge_shape = thermal_state.shape[:2] + (1,)
     first_cols = jnp.stack(
-        [thermal_state[:, :, :1], sideways_face_flux_factor[:, :, :1]]
-    )
-    from_right = lax.ppermute(first_cols, "lat", left_pairs)
-    from_left = lax.ppermute(thermal_state[:, :, width - 1 :], "lat", right_pairs)
+        [thermal_state[:, :, 0].reshape(-1), sideways_face_flux_factor[:, :, 0].reshape(-1)]
+    )
+    from_right = lax.ppermute(first_cols, "lat", left_pairs).reshape((2,) + edge_shape)
+    last_col = thermal_state[:, :, width - 1].reshape(-1)
+    from_left = lax.ppermute(last_col, "lat", right_pairs).reshape(edge_shape)
     base, prev_weight, own_weight, pieces = depth_local(
         thermal_state,
         sideways_face_flux_factor,

time: 77.1 us -> 75.5 us (0.979)
  starting transfers between devices: 29.2 us -> 28.4 us
    unnamed x21 -> x15, local copies, waits for them, and re-layouts: 3.34 us -> 0.95 us
    reshape x0 -> x2, local copies, waits for them, and re-layouts: none -> 1.77 us  [the longest x1 0.91 us: on_device(): lax.ppermute(first_cols, 'lat', left_pairs).reshape((2,) + edge_shape)]
    all_to_all x2, starting transfers between devices: 18.5 us -> 17.7 us  [reduced_solve(): every = lax.all_to_all(copies, axis, 0, 0, tiled=False)]
    ppermute x2, waiting for transfers between devices: 1.9 us -> 1.08 us  [the longest x1 1.07 us: on_device(): from_left = lax.ppermute(last_col, 'lat', right_pairs).reshape(edge_shape)]
  transfers between devices with their start and end apart: 4 -> 4, of which waited for: 3 -> 3; matrix products, arithmetic and copies ran while one was open for 8% -> 10% of each run, Pallas kernels for 0% -> 0%
where the time goes in v11:
time: 75.5 us; the launch traced here: 75.1 us
  starting transfers between devices  28.4 us (38%)
  waiting for transfers between devices  25.5 us (34%)
  local copies, waits for them, and re-layouts  11.9 us (16%)
  other arithmetic  5.78 us (8%)
  Pallas kernels  2.58 us (3%)
  between operations  1.04 us (1%)
    all_to_all x2, waiting for transfers between devices, reduced_solve(): every = lax.all_to_all(copies, axis, 0, 0, tiled=False)  24.4 us
    all_to_all x2, starting transfers between devices, reduced_solve(): every = lax.all_to_all(copies, axis, 0, 0, tiled=False)  17.7 us
    ppermute x1, starting transfers between devices, on_device(): lax.ppermute(first_cols, 'lat', left_pairs).reshape((2,) + edge_shape)  8.79 us
    slice x75, local copies, waits for them, and re-layouts, take_rows(): return lax.slice_in_dim(values, start, stop, axis=axis_index)  4.23 us
    pallas_call x1, Pallas kernels, depth_local(): pl.pallas_call(depth_kernel, out_shape=(full, full, full, copies))  2.58 us
    add x18, other arithmetic, cyclic_apply(): column + alpha_term * moved(column, stride, axis_index, 0.0, False)  2.58 us
    ppermute x1, starting transfers between devices, on_device(): from_left = lax.ppermute(last_col, 'lat', right_pairs).reshape(edge_shape)  1.92 us
  transfers between devices with their start and end apart: 4, of which 3 were waited for; matrix products, arithmetic and copies ran while one was open for 10% of the time, Pallas kernels for 0%

profile of v11, /device:TPU:1, one launch (start us, length us, event | category | flops | bytes accessed | tf_op | source)
XLA Modules:
  0.0 75.1 jit_solution(8980127307538945102)
XLA Ops:
  0.0 1.2 %slice_reduce_fusion = (f32[32,8]{1,0:T(8,128)S(1)}, f32[32,8]{1,0:T(8,128)S(1)}) fusion(f32[32,8,128]{2,1,0:T(8,128)} %t_ref.1), kind=kLoop, calls=%fused_computation.102 | loop fusion | bytes 4096 | tf_op jit(solution)/shard_map/slice | solution.py:234
  1.5 8.8 %collective-permute-start = (f32[2,256]{1,0:T(2,128)S(1)}, f32[2,256]{1,0:T(2,128)S(1)}, u32[]{:S(2)}, u32[]{:S(2)}) collective-permute-start(f32[2,256]{1,0:T(2,128)S(1)} %pad_maximum_fusion.1), channel_id=1, source_target_pairs={{1,0},{2,1},{3,2},{4,3},{5,4},{6,5},{7,6},{8,7},{9,8},{10,9},{11,1... | collective-permute-start | bytes 6152 | tf_op jit(solution)/shard_map/ppermute | solution.py:233
  10.4 1.9 %collective-permute-start.1 = (f32[256]{0:T(256)S(1)}, f32[256]{0:T(256)S(1)}, u32[]{:S(2)}, u32[]{:S(2)}) collective-permute-start(f32[256]{0:T(256)S(1)} %reshape_squeeze.7), channel_id=1, source_target_pairs={{0,1},{1,2},{2,3},{3,4},{4,5},{5,6},{6,7},{7,8},{8,9},{9,10},{10,1... | collective-permute-start | bytes 3080 | tf_op jit(solution)/shard_map/ppermute | solution.py:235
  12.4 1.1 %collective-permute-done.1 = f32[256]{0:T(256)S(1)} collective-permute-done((f32[256]{0:T(256)S(1)}, f32[256]{0:T(256)S(1)}, u32[]{:S(2)}, u32[]{:S(2)}) %collective-permute-start.1) | collective-permute-done | bytes 1056 | tf_op jit(solution)/shard_map/ppermute | solution.py:235
  13.5 0.9 %reshape.29.tl_ref = f32[32,8,1]{2,1,0:T(8,128)} reshape(f32[256]{0:T(256)S(1)} %collective-permute-done.1) | data formatting | bytes 2048 | tf_op jit(solution)/shard_map/reshape | solution.py:235
  14.3 0.9 %reshape.28.right_ref = f32[2,32,8,1]{3,2,1,0:T(8,128)} reshape(f32[2,256]{1,0:T(2,128)S(1)} %collective-permute-done) | data formatting | bytes 4096 | tf_op jit(solution)/shard_map/reshape | solution.py:233
  15.2 2.6 %shard_map.37 = (f32[32,8,128]{2,1,0:T(8,128)}, f32[32,8,128]{2,1,0:T(8,128)}, f32[32,8,128]{2,1,0:T(8,128)}, f32[32,6,8,128]{3,2,1,0:T(8,128)}) custom-call(f32[32,8,128]{2,1,0:T(8,128)} %t_ref.1, f32[32,8,128]{2,1,0:T(8,128)} %s_ref.1, f32[32,8,128]{2,1,0:T(8,128)} %d_ref.1, f32[2,32,8,1]{3,2,1,0:T(8,128)} %reshape.28.right_ref, f32[32,8,1]{2,1,0:T(8,128)} %reshape.29.tl_ref), custom_call_target="tpu_custom_call" | custom-call | tf_op jit(solution)/shard_map/pallas_call | solution.py:152
  17.8 6.0 %all-to-all-start = ((f32[32,6,8,128]{3,2,1,0:T(8,128)}), f32[32,6,8,128]{3,2,1,0:T(8,128)S(1)}, u32[]{:S(2)}, u32[]{:S(2)}) async-start(f32[32,6,8,128]{3,2,1,0:T(8,128)} %get-tuple-element.29), calls=%async_computation | async-start | bytes 1572864 | tf_op jit(solution)/shard_map/all_to_all | solution.py:159
  24.1 0.2 copy.68
  24.3 0.1 broadcast_select_fusion
  24.7 0.2 copy.67
  24.9 0.3 multiply_add_fusion.11
  25.3 0.1 fusion.48
  25.7 0.2 multiply_add_fusion.10
  26.6 0.2 multiply_add_fusion.9
  27.4 0.2 multiply_add_fusion.8
  28.3 0.2 multiply_add_fusion.7
  29.1 0.2 multiply_add_fusion.6
  29.6 0.2 multiply_add_fusion.12
  30.2 0.2 add_divide_fusion.1
  30.5 15.2 %all-to-all-done = f32[32,6,8,128]{3,2,1,0:T(8,128)S(1)} async-done(((f32[32,6,8,128]{3,2,1,0:T(8,128)}), f32[32,6,8,128]{3,2,1,0:T(8,128)S(1)}, u32[]{:S(2)}, u32[]{:S(2)}) %all-to-all-start) | async-done | bytes 786464 | tf_op jit(solution)/shard_map/all_to_all | solution.py:159
  46.1 0.1 multiply_add_fusion.31
  47.1 0.8 %copy-done.3 = f32[32,8,128]{2,1,0:T(8,128)S(1)} copy-done((f32[32,8,128]{2,1,0:T(8,128)S(1)}, f32[32,8,128]{2,1,0:T(8,128)}, u32[]{:S(2)}) %copy-start.3) | copy-done | bytes 131096
  49.5 0.5 fusion
  50.6 0.7 broadcast_in_dim.38
  51.2 11.7 %all-to-all-start.1 = ((f32[16,6,256]{2,1,0:T(8,128)}), f32[16,6,256]{2,1,0:T(8,128)S(1)}, u32[]{:S(2)}, u32[]{:S(2)}) async-start(f32[16,6,256]{2,1,0:T(8,128)} %broadcast_in_dim.38), calls=%async_computation.1 | async-start | bytes 262144 | tf_op jit(solution)/shard_map/all_to_all | solution.py:159
  62.9 9.2 %all-to-all-done.1 = f32[16,6,256]{2,1,0:T(8,128)S(1)} async-done(((f32[16,6,256]{2,1,0:T(8,128)}), f32[16,6,256]{2,1,0:T(8,128)S(1)}, u32[]{:S(2)}, u32[]{:S(2)}) %all-to-all-start.1) | async-done | bytes 98336 | tf_op jit(solution)/shard_map/all_to_all | solution.py:159
  72.6 0.5 broadcast.388
  73.1 0.7 fusion.16
  74.0 0.2 reshape_squeeze.9
  74.2 0.1 multiply_add_fusion
  74.3 0.8 %pad_maximum_fusion = f32[32,8,128]{2,1,0:T(8,128)} fusion(f32[32,8,1]{2,1,0:T(8,128)S(1)} %reshape_squeeze.9, f32[32,8,127]{2,1,0:T(8,128)S(1)} %multiply_add_fusion), kind=kLoop, calls=%fused_computation.16 | loop fusion | flops 32768 | bytes 262144 | tf_op jit(solution)/shard_map/concatenate | solution.py:221
  (141 shorter events, 7.9 us)
Async XLA Ops:
  0.0 1.3 %copy-start = (f32[32,8,128]{2,1,0:T(8,128)S(1)}, f32[32,8,128]{2,1,0:T(8,128)}, u32[]{:S(2)}) copy-start(f32[32,8,128]{2,1,0:T(8,128)} %s_ref.1) | copy-start | bytes 393220
  1.5 12.8 %collective-permute-start = (f32[2,256]{1,0:T(2,128)S(1)}, f32[2,256]{1,0:T(2,128)S(1)}, u32[]{:S(2)}, u32[]{:S(2)}) collective-permute-start(f32[2,256]{1,0:T(2,128)S(1)} %pad_maximum_fusion.1), channel_id=1, source_target_pairs={{1,0},{2,1},{3,2},{4,3},{5,4},{6,5},{7,6},{8,7},{9,8},{10,9},{11,1... | collective-permute-start | bytes 6152 | tf_op jit(solution)/shard_map/ppermute | solution.py:233
  10.4 3.0 %collective-permute-start.1 = (f32[256]{0:T(256)S(1)}, f32[256]{0:T(256)S(1)}, u32[]{:S(2)}, u32[]{:S(2)}) collective-permute-start(f32[256]{0:T(256)S(1)} %reshape_squeeze.7), channel_id=1, source_target_pairs={{0,1},{1,2},{2,3},{3,4},{4,5},{5,6},{6,7},{7,8},{8,9},{9,10},{10,1... | collective-permute-start | bytes 3080 | tf_op jit(solution)/shard_map/ppermute | solution.py:235
  17.8 6.0 %copy-start.1 = (f32[32,8,128]{2,1,0:T(8,128)S(1)}, f32[32,8,128]{2,1,0:T(8,128)}, u32[]{:S(2)}) copy-start(f32[32,8,128]{2,1,0:T(8,128)} %s_ref.1) | copy-start | bytes 393220
  17.8 27.9 %all-to-all-start = ((f32[32,6,8,128]{3,2,1,0:T(8,128)}), f32[32,6,8,128]{3,2,1,0:T(8,128)S(1)}, u32[]{:S(2)}, u32[]{:S(2)}) async-start(f32[32,6,8,128]{3,2,1,0:T(8,128)} %get-tuple-element.29), calls=%async_computation | async-start | bytes 1572864 | tf_op jit(solution)/shard_map/all_to_all | solution.py:159
  47.0 0.9 %copy-start.3 = (f32[32,8,128]{2,1,0:T(8,128)S(1)}, f32[32,8,128]{2,1,0:T(8,128)}, u32[]{:S(2)}) copy-start(f32[32,8,128]{2,1,0:T(8,128)} %get-tuple-element.28) | copy-start | bytes 393220
  47.0 1.0 %copy-start.4 = (f32[32,8,128]{2,1,0:T(8,128)S(1)}, f32[32,8,128]{2,1,0:T(8,128)}, u32[]{:S(2)}) copy-start(f32[32,8,128]{2,1,0:T(8,128)} %get-tuple-element.30) | copy-start | bytes 393220
  47.1 0.9 %copy-start.2 = (f32[32,8,128]{2,1,0:T(8,128)S(1)}, f32[32,8,128]{2,1,0:T(8,128)}, u32[]{:S(2)}) copy-start(f32[32,8,128]{2,1,0:T(8,128)} %get-tuple-element.27) | copy-start | bytes 393220
  51.2 20.8 %all-to-all-start.1 = ((f32[16,6,256]{2,1,0:T(8,128)}), f32[16,6,256]{2,1,0:T(8,128)S(1)}, u32[]{:S(2)}, u32[]{:S(2)}) async-start(f32[16,6,256]{2,1,0:T(8,128)} %broadcast_in_dim.38), calls=%async_computation.1 | async-start | bytes 262144 | tf_op jit(solution)/shard_map/all_to_all | solution.py:159

commit v12 on v11

--- a/solution.py
+++ b/solution.py
@@ -83,9 +83,9 @@
     lane = lax.broadcasted_iota(jnp.int32, temp.shape, 2)
     last = lane == width - 1
     first = lane == 0
-    temp_right = jnp.where(last, right_ref[0], pltpu.roll(temp, width - 1, 2))
-    conduct_right = jnp.where(last, right_ref[1], pltpu.roll(conduct, width - 1, 2))
-    temp_left = jnp.where(first, tl_ref[...], pltpu.roll(temp, 1, 2))
+    temp_right = jnp.where(last, right_ref[0][:, :, None], pltpu.roll(temp, width - 1, 2))
+    conduct_right = jnp.where(last, right_ref[1][:, :, None], pltpu.roll(conduct, width - 1, 2))
+    temp_left = jnp.where(first, tl_ref[...][:, :, None], pltpu.roll(temp, 1, 2))
     base_ref[...] = temp + sideways_coupling_quotient * (
         conduct_right * (temp_right - temp) - conduct * (temp - temp_left)
     )
@@ -226,7 +226,7 @@
     count = lax.axis_size("lat")
     right_pairs = [(i, i + 1) for i in range(count - 1)]
     left_pairs = [(i + 1, i) for i in range(count - 1)]
-    edge_shape = thermal_state.shape[:2] + (1,)
+    edge_shape = thermal_state.shape[:2]
     first_cols = jnp.stack(
         [thermal_state[:, :, 0].reshape(-1), sideways_face_flux_factor[:, :, 0].reshape(-1)]
     )

time: 75.5 us -> 75 us (level)
  transfers between devices with their start and end apart: 4 -> 4, of which waited for: 3 -> 3; matrix products, arithmetic and copies ran while one was open for 10% -> 9% of each run, Pallas kernels for 0% -> 0%
where the time goes in v12:
time: 75 us; the launch traced here: 74.6 us
  starting transfers between devices  28.4 us (38%)
  waiting for transfers between devices  25.5 us (34%)
  local copies, waits for them, and re-layouts  11.5 us (15%)
  other arithmetic  5.78 us (8%)
  Pallas kernels  2.45 us (3%)
  between operations  1.04 us (1%)
    all_to_all x2, waiting for transfers between devices, reduced_solve(): every = lax.all_to_all(copies, axis, 0, 0, tiled=False)  24.4 us
    all_to_all x2, starting transfers between devices, reduced_solve(): every = lax.all_to_all(copies, axis, 0, 0, tiled=False)  17.7 us
    ppermute x1, starting transfers between devices, on_device(): lax.ppermute(first_cols, 'lat', left_pairs).reshape((2,) + edge_shape)  8.79 us
    slice x75, local copies, waits for them, and re-layouts, take_rows(): return lax.slice_in_dim(values, start, stop, axis=axis_index)  4.23 us
    add x18, other arithmetic, cyclic_apply(): column + alpha_term * moved(column, stride, axis_index, 0.0, False)  2.58 us
    pallas_call x1, Pallas kernels, depth_local(): pl.pallas_call(depth_kernel, out_shape=(full, full, full, copies))  2.45 us
    ppermute x1, starting transfers between devices, on_device(): from_left = lax.ppermute(last_col, 'lat', right_pairs).reshape(edge_shape)  1.92 us
  transfers between devices with their start and end apart: 4, of which 3 were waited for; matrix products, arithmetic and copies ran while one was open for 9% of the time, Pallas kernels for 0%

profile of v12, /device:TPU:1, one launch (start us, length us, event | category | flops | bytes accessed | tf_op | source)
XLA Modules:
  0.0 74.6 jit_solution(6317464227063035161)
XLA Ops:
  0.0 1.2 %slice_reduce_fusion = (f32[32,8]{1,0:T(8,128)S(1)}, f32[32,8]{1,0:T(8,128)S(1)}) fusion(f32[32,8,128]{2,1,0:T(8,128)} %t_ref.1), kind=kLoop, calls=%fused_computation.102 | loop fusion | bytes 4096 | tf_op jit(solution)/shard_map/slice | solution.py:234
  1.5 8.8 %collective-permute-start = (f32[2,256]{1,0:T(2,128)S(1)}, f32[2,256]{1,0:T(2,128)S(1)}, u32[]{:S(2)}, u32[]{:S(2)}) collective-permute-start(f32[2,256]{1,0:T(2,128)S(1)} %pad_maximum_fusion.1), channel_id=1, source_target_pairs={{1,0},{2,1},{3,2},{4,3},{5,4},{6,5},{7,6},{8,7},{9,8},{10,9},{11,1... | collective-permute-start | bytes 6152 | tf_op jit(solution)/shard_map/ppermute | solution.py:233
  10.4 1.9 %collective-permute-start.1 = (f32[256]{0:T(256)S(1)}, f32[256]{0:T(256)S(1)}, u32[]{:S(2)}, u32[]{:S(2)}) collective-permute-start(f32[256]{0:T(256)S(1)} %reshape_squeeze.7), channel_id=1, source_target_pairs={{0,1},{1,2},{2,3},{3,4},{4,5},{5,6},{6,7},{7,8},{8,9},{9,10},{10,1... | collective-permute-start | bytes 3080 | tf_op jit(solution)/shard_map/ppermute | solution.py:235
  12.4 1.1 %collective-permute-done.1 = f32[256]{0:T(256)S(1)} collective-permute-done((f32[256]{0:T(256)S(1)}, f32[256]{0:T(256)S(1)}, u32[]{:S(2)}, u32[]{:S(2)}) %collective-permute-start.1) | collective-permute-done | bytes 1056 | tf_op jit(solution)/shard_map/ppermute | solution.py:235
  13.5 0.7 reshape.27.tl_ref
  14.1 0.7 reshape.26.right_ref
  14.8 2.5 %shard_map.37 = (f32[32,8,128]{2,1,0:T(8,128)}, f32[32,8,128]{2,1,0:T(8,128)}, f32[32,8,128]{2,1,0:T(8,128)}, f32[32,6,8,128]{3,2,1,0:T(8,128)}) custom-call(f32[32,8,128]{2,1,0:T(8,128)} %t_ref.1, f32[32,8,128]{2,1,0:T(8,128)} %s_ref.1, f32[32,8,128]{2,1,0:T(8,128)} %d_ref.1, f32[2,32,8]{2,1,0:T(8,128)} %reshape.26.right_ref, f32[32,8]{1,0:T(8,128)} %reshape.27.tl_ref), custom_call_target="tpu_custom_call" | custom-call | tf_op jit(solution)/shard_map/pallas_call | solution.py:152
  17.3 6.0 %all-to-all-start = ((f32[32,6,8,128]{3,2,1,0:T(8,128)}), f32[32,6,8,128]{3,2,1,0:T(8,128)S(1)}, u32[]{:S(2)}, u32[]{:S(2)}) async-start(f32[32,6,8,128]{3,2,1,0:T(8,128)} %get-tuple-element.29), calls=%async_computation | async-start | bytes 1572864 | tf_op jit(solution)/shard_map/all_to_all | solution.py:159
  23.6 0.2 copy.62
  23.8 0.1 broadcast_select_fusion
  24.1 0.2 copy.61
  24.4 0.3 multiply_add_fusion.11
  24.7 0.1 fusion.48
  25.2 0.2 multiply_add_fusion.10
  26.1 0.2 multiply_add_fusion.9
  26.9 0.2 multiply_add_fusion.8
  27.7 0.2 multiply_add_fusion.7
  28.6 0.2 multiply_add_fusion.6
  29.1 0.2 multiply_add_fusion.12
  29.7 0.2 add_divide_fusion.1
  30.0 15.2 %all-to-all-done = f32[32,6,8,128]{3,2,1,0:T(8,128)S(1)} async-done(((f32[32,6,8,128]{3,2,1,0:T(8,128)}), f32[32,6,8,128]{3,2,1,0:T(8,128)S(1)}, u32[]{:S(2)}, u32[]{:S(2)}) %all-to-all-start) | async-done | bytes 786464 | tf_op jit(solution)/shard_map/all_to_all | solution.py:159
  45.5 0.1 multiply_add_fusion.31
  46.6 0.8 %copy-done.3 = f32[32,8,128]{2,1,0:T(8,128)S(1)} copy-done((f32[32,8,128]{2,1,0:T(8,128)S(1)}, f32[32,8,128]{2,1,0:T(8,128)}, u32[]{:S(2)}) %copy-start.3) | copy-done | bytes 131096
  49.0 0.5 fusion
  50.0 0.7 broadcast_in_dim.38
  50.7 11.7 %all-to-all-start.1 = ((f32[16,6,256]{2,1,0:T(8,128)}), f32[16,6,256]{2,1,0:T(8,128)S(1)}, u32[]{:S(2)}, u32[]{:S(2)}) async-start(f32[16,6,256]{2,1,0:T(8,128)} %broadcast_in_dim.38), calls=%async_computation.1 | async-start | bytes 262144 | tf_op jit(solution)/shard_map/all_to_all | solution.py:159
  62.4 9.2 %all-to-all-done.1 = f32[16,6,256]{2,1,0:T(8,128)S(1)} async-done(((f32[16,6,256]{2,1,0:T(8,128)}), f32[16,6,256]{2,1,0:T(8,128)S(1)}, u32[]{:S(2)}, u32[]{:S(2)}) %all-to-all-start.1) | async-done | bytes 98336 | tf_op jit(solution)/shard_map/all_to_all | solution.py:159
  72.1 0.5 broadcast.388
  72.6 0.7 fusion.16
  73.4 0.2 reshape_squeeze.9
  73.7 0.1 multiply_add_fusion
  73.8 0.8 %pad_maximum_fusion = f32[32,8,128]{2,1,0:T(8,128)} fusion(f32[32,8,1]{2,1,0:T(8,128)S(1)} %reshape_squeeze.9, f32[32,8,127]{2,1,0:T(8,128)S(1)} %multiply_add_fusion), kind=kLoop, calls=%fused_computation.16 | loop fusion | flops 32768 | bytes 262144 | tf_op jit(solution)/shard_map/concatenate | solution.py:221
  (141 shorter events, 7.9 us)
Async XLA Ops:
  0.0 1.3 %copy-start = (f32[32,8,128]{2,1,0:T(8,128)S(1)}, f32[32,8,128]{2,1,0:T(8,128)}, u32[]{:S(2)}) copy-start(f32[32,8,128]{2,1,0:T(8,128)} %s_ref.1) | copy-start | bytes 393220
  1.5 12.6 %collective-permute-start = (f32[2,256]{1,0:T(2,128)S(1)}, f32[2,256]{1,0:T(2,128)S(1)}, u32[]{:S(2)}, u32[]{:S(2)}) collective-permute-start(f32[2,256]{1,0:T(2,128)S(1)} %pad_maximum_fusion.1), channel_id=1, source_target_pairs={{1,0},{2,1},{3,2},{4,3},{5,4},{6,5},{7,6},{8,7},{9,8},{10,9},{11,1... | collective-permute-start | bytes 6152 | tf_op jit(solution)/shard_map/ppermute | solution.py:233
  10.4 3.0 %collective-permute-start.1 = (f32[256]{0:T(256)S(1)}, f32[256]{0:T(256)S(1)}, u32[]{:S(2)}, u32[]{:S(2)}) collective-permute-start(f32[256]{0:T(256)S(1)} %reshape_squeeze.7), channel_id=1, source_target_pairs={{0,1},{1,2},{2,3},{3,4},{4,5},{5,6},{6,7},{7,8},{8,9},{9,10},{10,1... | collective-permute-start | bytes 3080 | tf_op jit(solution)/shard_map/ppermute | solution.py:235
  17.3 6.0 %copy-start.1 = (f32[32,8,128]{2,1,0:T(8,128)S(1)}, f32[32,8,128]{2,1,0:T(8,128)}, u32[]{:S(2)}) copy-start(f32[32,8,128]{2,1,0:T(8,128)} %s_ref.1) | copy-start | bytes 393220
  17.3 27.9 %all-to-all-start = ((f32[32,6,8,128]{3,2,1,0:T(8,128)}), f32[32,6,8,128]{3,2,1,0:T(8,128)S(1)}, u32[]{:S(2)}, u32[]{:S(2)}) async-start(f32[32,6,8,128]{3,2,1,0:T(8,128)} %get-tuple-element.29), calls=%async_computation | async-start | bytes 1572864 | tf_op jit(solution)/shard_map/all_to_all | solution.py:159
  46.4 0.9 %copy-start.3 = (f32[32,8,128]{2,1,0:T(8,128)S(1)}, f32[32,8,128]{2,1,0:T(8,128)}, u32[]{:S(2)}) copy-start(f32[32,8,128]{2,1,0:T(8,128)} %get-tuple-element.28) | copy-start | bytes 393220
  46.4 1.0 %copy-start.4 = (f32[32,8,128]{2,1,0:T(8,128)S(1)}, f32[32,8,128]{2,1,0:T(8,128)}, u32[]{:S(2)}) copy-start(f32[32,8,128]{2,1,0:T(8,128)} %get-tuple-element.30) | copy-start | bytes 393220
  46.5 1.0 %copy-start.2 = (f32[32,8,128]{2,1,0:T(8,128)S(1)}, f32[32,8,128]{2,1,0:T(8,128)}, u32[]{:S(2)}) copy-start(f32[32,8,128]{2,1,0:T(8,128)} %get-tuple-element.27) | copy-start | bytes 393220
  50.7 20.8 %all-to-all-start.1 = ((f32[16,6,256]{2,1,0:T(8,128)}), f32[16,6,256]{2,1,0:T(8,128)S(1)}, u32[]{:S(2)}, u32[]{:S(2)}) async-start(f32[16,6,256]{2,1,0:T(8,128)} %broadcast_in_dim.38), calls=%async_computation.1 | async-start | bytes 262144 | tf_op jit(solution)/shard_map/all_to_all | solution.py:159
